TPU v7x, 128 devices: a whole 4x4x4 slice. The times are simulated.
128 devices in a mesh: node: 8 (over x, core), dev: 16 (over z, y).
Axes of the slice: x: 4, y: 4, z: 4, core: 2. Of those that a mesh axis runs over, the one named last changes fastest.
Arguments:
- tokens: bfloat16 [32768, 7168], P(('node', 'dev')), may hold values from -6 to 6
- grad_out: bfloat16 [32768, 7168], P(('node', 'dev')), may hold values from -1.796875 to 1.796875
- router_gates: bfloat16 [32768, 8], P(('node', 'dev')), may hold values from 0.049804688 to 1
- expert_ids: int32 [32768, 8], P(('node', 'dev')), may hold values from 0 to 255, as said below
- slot_plan: int32 [256, 2], replicated, may hold values from 0 to 16, as said below
- w_gate: bfloat16 [8, 7168, 2048], P(None, 'dev', 'node'), may hold values from -0.0625 to 0.0625
- w_up: bfloat16 [8, 7168, 2048], P(None, 'dev', 'node'), may hold values from -0.0625 to 0.0625
- w_down: bfloat16 [8, 2048, 7168], P(None, 'node', 'dev'), may hold values from -0.125 to 0.125
Outputs:
- grad_tokens: bfloat16 [32768, 7168], P(('node', 'dev'))
- grad_gates: float32 [32768, 8], P(('node', 'dev'))
- grad_w_gate: bfloat16 [8, 7168, 2048], P(None, 'dev', 'node')
- grad_w_up: bfloat16 [8, 7168, 2048], P(None, 'dev', 'node')
- grad_w_down: bfloat16 [8, 2048, 7168], P(None, 'node', 'dev')
Inputs may be any that keep to these rules, and one draw needn't show every extreme that they name: `expert_ids`: each token names 8 different experts. Within one block of 256 tokens (the tokens of one device), at most 4 pairs name any one expert that has slots, and in every draw one expert that has slots is named exactly 2 * 2 times in every block. `slot_plan`: exactly 8 rows hold slots: each such row holds two different slots, and every slot 0 .. 15 stands in exactly one row. Every entry of the other rows equals 16.
All inputs are finite; a program needn't handle non-finite values.
Results may differ from a plain program's by a relative error of at most 0.0059.
Values may be sent and summed in bfloat16 or wider, within the bound.
No kernel may reach another device: no remote copies, remote signals or barrier semaphores. Data moves between devices by JAX's collectives and lax.ppermute only.
A program may use at most 128 MiB of HBM per device.

v0:
```python
import jax
import jax.numpy as jnp
from jax import lax
from jax.sharding import PartitionSpec as P

EXPERTS = 256
TOP = 8
CAP = 2


def expert_pass(pieces, slot_gate, slot_up, slot_down):
    x_piece, dy_piece, gate_piece = pieces
    lead_count = x_piece.shape[0]
    slot_count = slot_down.shape[0]
    model_width = x_piece.shape[-1]
    x_rows = x_piece.reshape(-1, model_width)
    dy_split = dy_piece.reshape(-1, slot_count, model_width // slot_count)
    gate_rows = gate_piece.reshape(-1, 1).astype(jnp.float32)
    gate_pre = jnp.dot(x_rows, slot_gate, preferred_element_type=jnp.float32)
    up_pre = jnp.dot(x_rows, slot_up, preferred_element_type=jnp.float32)
    back_proj = jnp.einsum("rsk,shk->rh", dy_split, slot_down, preferred_element_type=jnp.float32)
    sigmoid_gate = jax.nn.sigmoid(gate_pre)
    active = gate_pre * sigmoid_gate
    hidden = active * up_pre
    scaled_back = gate_rows * back_proj
    d_gate = (scaled_back * up_pre * sigmoid_gate * (1.0 + gate_pre * (1.0 - sigmoid_gate))).astype(
        jnp.bfloat16
    )
    d_up = (scaled_back * active).astype(jnp.bfloat16)
    scaled_hidden = (gate_rows * hidden).astype(jnp.bfloat16)
    gate_terms = jnp.sum(back_proj * hidden, axis=-1)
    row_terms = jnp.einsum("rh,dh->rd", d_gate, slot_gate, preferred_element_type=jnp.float32)
    row_terms = row_terms + jnp.einsum(
        "rh,dh->rd", d_up, slot_up, preferred_element_type=jnp.float32
    )
    acc_gate = jnp.einsum("rd,rh->dh", x_rows, d_gate, preferred_element_type=jnp.float32)
    acc_up = jnp.einsum("rd,rh->dh", x_rows, d_up, preferred_element_type=jnp.float32)
    acc_down = jnp.einsum(
        "rsk,rh->shk", dy_split, scaled_hidden, preferred_element_type=jnp.float32
    )
    row_acc = row_terms.reshape(lead_count, slot_count, -1, model_width)
    gate_acc = gate_terms.reshape(lead_count, slot_count, -1)
    return (acc_gate, acc_up, acc_down, row_acc, gate_acc)


def local(tokens, grad_out, router_gates, expert_ids, slot_plan, w_gate, w_up, w_down):
    slot_count = lax.axis_size("dev")
    tok_rows, model_width = tokens.shape
    hidden_width = w_gate.shape[2]
    round_total = w_gate.shape[0]
    pair_total = tok_rows * TOP
    expert_match = expert_ids[:, :, None] == jnp.arange(EXPERTS, dtype=jnp.int32)
    first_slot = jnp.sum(jnp.where(expert_match, slot_plan[:, 0], 0), axis=-1).reshape(pair_total)
    second_slot = jnp.sum(jnp.where(expert_match, slot_plan[:, 1], 0), axis=-1).reshape(pair_total)
    is_live = first_slot < slot_count
    first_hot = (first_slot[:, None] == jnp.arange(slot_count, dtype=jnp.int32)[None, :]).astype(
        jnp.int32
    )
    pair_order = jnp.sum(first_hot * (jnp.cumsum(first_hot, axis=0) - 1), axis=-1)
    pair_slot = jnp.where(pair_order % 2 == 0, first_slot, second_slot)
    target_row = pair_slot * CAP + pair_order // 2
    position_ids = jnp.arange(slot_count * CAP, dtype=jnp.int32)
    chooser = (is_live[None, :] & (target_row[None, :] == position_ids[:, None])).astype(
        jnp.float32
    )
    pick_rows = jnp.sum(chooser.reshape(slot_count * CAP, tok_rows, TOP), axis=-1)
    pick_half = pick_rows.astype(jnp.bfloat16)
    x_send = (
        jnp.dot(pick_half, tokens, preferred_element_type=jnp.float32)
        .astype(jnp.bfloat16)
        .reshape(slot_count, CAP, model_width)
    )
    dy_send = (
        jnp.dot(pick_half, grad_out, preferred_element_type=jnp.float32)
        .astype(jnp.bfloat16)
        .reshape(slot_count, CAP, model_width)
    )
    flat_gates = router_gates.reshape(pair_total).astype(jnp.float32)
    gate_send = (
        jnp.dot(chooser, flat_gates, precision=lax.Precision.HIGHEST)
        .astype(jnp.bfloat16)
        .reshape(slot_count, CAP)
    )
    in_round = (slot_plan[:, 0] < slot_count).astype(jnp.int32)
    expert_rank = jnp.cumsum(in_round) - 1
    holder = jnp.any(slot_plan[:, :, None] == jnp.arange(slot_count, dtype=jnp.int32), axis=1)
    slot_rank = jnp.sum(jnp.where(holder, expert_rank[:, None], 0), axis=0)
    grouping = (slot_rank[None, :] == jnp.arange(round_total, dtype=jnp.int32)[:, None]).astype(
        jnp.bfloat16
    )
    copy_gate = jnp.take(w_gate, slot_rank, axis=0)
    copy_up = jnp.take(w_up, slot_rank, axis=0)
    copy_down = jnp.take(w_down, slot_rank, axis=0)
    slot_gate, slot_up, slot_down = (
        lax.all_to_all(copy_gate, "dev", split_axis=0, concat_axis=0, tiled=True),
        lax.all_to_all(copy_up, "dev", split_axis=0, concat_axis=0, tiled=True),
        lax.all_to_all(copy_down, "dev", split_axis=0, concat_axis=0, tiled=True),
    )
    slot_gate = slot_gate.reshape(model_width, hidden_width)
    slot_up = slot_up.reshape(model_width, hidden_width)
    got_x, got_dy, got_gate = (
        lax.all_to_all(x_send, "dev", split_axis=0, concat_axis=0, tiled=True),
        lax.all_to_all(dy_send, "dev", split_axis=0, concat_axis=0, tiled=True),
        lax.all_to_all(gate_send, "dev", split_axis=0, concat_axis=0, tiled=True),
    )
    totals = expert_pass(
        (
            lax.all_gather(got_x[None], "node", axis=0, tiled=True),
            lax.all_gather(got_dy[None], "node", axis=0, tiled=True),
            lax.all_gather(got_gate[None], "node", axis=0, tiled=True),
        ),
        slot_gate,
        slot_up,
        slot_down,
    )
    acc_gate, acc_up, acc_down, row_acc, gate_acc = totals
    summed_rows, summed_gates = (
        lax.psum_scatter(row_acc, "node", scatter_dimension=0, tiled=True),
        lax.psum_scatter(gate_acc, "node", scatter_dimension=0, tiled=True),
    )
    back_rows, back_gates = (
        lax.all_to_all(summed_rows, "dev", split_axis=1, concat_axis=1, tiled=True),
        lax.all_to_all(summed_gates, "dev", split_axis=1, concat_axis=1, tiled=True),
    )
    grad_tokens = jnp.einsum(
        "qt,qd->td",
        pick_rows,
        back_rows.reshape(slot_count * CAP, model_width),
        precision=lax.Precision.HIGHEST,
    ).astype(jnp.bfloat16)
    grad_gates = jnp.dot(
        back_gates.reshape(slot_count * CAP), chooser, precision=lax.Precision.HIGHEST
    ).reshape(tok_rows, TOP)
    send_gate = acc_gate.astype(jnp.bfloat16).reshape(
        slot_count, model_width // slot_count, hidden_width
    )
    send_up = acc_up.astype(jnp.bfloat16).reshape(
        slot_count, model_width // slot_count, hidden_width
    )
    send_down = acc_down.astype(jnp.bfloat16)
    got_wgate, got_wup, got_wdown = (
        lax.all_to_all(send_gate, "dev", split_axis=0, concat_axis=0, tiled=True),
        lax.all_to_all(send_up, "dev", split_axis=0, concat_axis=0, tiled=True),
        lax.all_to_all(send_down, "dev", split_axis=0, concat_axis=0, tiled=True),
    )
    grad_w_gate = jnp.einsum(
        "js,sdh->jdh", grouping, got_wgate, preferred_element_type=jnp.float32
    ).astype(jnp.bfloat16)
    grad_w_up = jnp.einsum(
        "js,sdh->jdh", grouping, got_wup, preferred_element_type=jnp.float32
    ).astype(jnp.bfloat16)
    grad_w_down = jnp.einsum(
        "js,shk->jhk", grouping, got_wdown, preferred_element_type=jnp.float32
    ).astype(jnp.bfloat16)
    return (grad_tokens, grad_gates, grad_w_gate, grad_w_up, grad_w_down)


def solution(mesh):
    return jax.shard_map(
        local,
        mesh=mesh,
        in_specs=(
            P(("node", "dev"), None),
            P(("node", "dev"), None),
            P(("node", "dev"), None),
            P(("node", "dev"), None),
            P(),
            P(None, "dev", "node"),
            P(None, "dev", "node"),
            P(None, "node", "dev"),
        ),
        out_specs=(
            P(("node", "dev"), None),
            P(("node", "dev"), None),
            P(None, "dev", "node"),
            P(None, "dev", "node"),
            P(None, "node", "dev"),
        ),
        check_vma=False,
    )
```

profile of v0, /device:TPU:0, one launch (start us, length us, event | category | flops | bytes accessed | tf_op | source)
XLA Modules:
  0.0 506.4 jit_solution(3346200505427443808)
XLA Ops:
  8.9 9.2 %select_reduce_fusion = (s32[256,8]{1,0:T(8,128)S(1)}, s32[256,8]{1,0:T(8,128)S(1)}) fusion(s32[256]{0:T(256)S(1)} %bitcast.78, s32[256,8]{1,0:T(8,128)S(1)} %copy.90, s32[256]{0:T(256)S(1)} %bitcast.77), kind=kLoop, calls=%fused_computation.21 | loop fusion | flops 2617344 | bytes 26624 | tf_op jit(solution)/shard_map/reduce_sum | solution.py:54
  18.4 4.5 reduce-window.15
  27.2 18.9 %all_to_all.60 = bf16[16,2,7168]{2,1,0:T(2,128)(2,1)} all-to-all(bf16[16,2,7168]{2,1,0:T(2,128)(2,1)S(1)} %reshape.235), channel_id=1, replica_groups=mesh['node'=8,'dev'=16] {'dev'}, dimensions={0} | all-to-all | bytes 917504 | tf_op jit(solution)/shard_map/all_to_all | solution.py:102
  62.2 7.2 %all-to-all-start.1 = ((bf16[16,2,7168]{2,1,0:T(2,128)(2,1)}), bf16[16,2,7168]{2,1,0:T(2,128)(2,1)S(1)}, u32[]{:S(2)}, u32[]{:S(2)}) async-start(bf16[16,2,7168]{2,1,0:T(2,128)(2,1)} %reshape.232), calls=%async_computation.1 | async-start | bytes 917504 | tf_op jit(solution)/shard_map/all_to_all | solution.py:103
  69.4 7.1 %broadcast_select_fusion.1 = (bf16[16,448,256]{2,1,0:T(8,128)(2,1)}, bf16[16,448,256]{2,1,0:T(8,128)(2,1)}) fusion(bf16[16,448,256]{2,1,0:T(8,128)(2,1)} %gather_fusion.1, pred[16]{0:T(512)(128)(4,1)S(1)} %compare_and_fusion, bf16[16,448,256]{2,1,0:T(8,128)(2,1)} %gather_fusion.2), kind=kLoop, calls=%fused_computation.19 | loop fusion | flops 3670016 | bytes 14680080 | tf_op jit(solution)/shard_map/jit(_take)/select_n | solution.py:92
  79.9 4.6 all-to-all-start.5
  85.2 48.9 %all-to-all-done.5 = bf16[16,448,256]{2,1,0:T(8,128)(2,1)} async-done(((bf16[16,448,256]{2,1,0:T(8,128)(2,1)}), bf16[16,448,256]{2,1,0:T(8,128)(2,1)}, u32[]{:S(2)}, u32[]{:S(2)}) %all-to-all-start.5) | async-done | bytes 3670048 | tf_op jit(solution)/shard_map/all_to_all | solution.py:95
  134.2 4.6 all-to-all-start.4
  141.5 4.3 broadcast_select_fusion.2
  145.8 43.1 %all-to-all-done.4 = bf16[16,448,256]{2,1,0:T(8,128)(2,1)} async-done(((bf16[16,448,256]{2,1,0:T(8,128)(2,1)}), bf16[16,448,256]{2,1,0:T(8,128)(2,1)}, u32[]{:S(2)}, u32[]{:S(2)}) %all-to-all-start.4) | async-done | bytes 3670048 | tf_op jit(solution)/shard_map/all_to_all | solution.py:96
  188.9 4.5 all-to-all-start.2
  193.4 13.3 %all-gather = bf16[128,1,2]{2,1,0:T(2,128)(2,1)S(1)} all-gather(bf16[16,1,2]{2,1,0:T(2,128)(2,1)S(1)} %all-to-all-done), channel_id=2, replica_groups=mesh['node'=8,'dev'=16] {'node'}, dimensions={0}, use_global_device_ids=true | all-gather | bytes 576 | tf_op jit(solution)/shard_map/all_gather | solution.py:110
  207.1 8.4 %reshape.236 = bf16[256,7168]{1,0:T(8,128)(2,1)} reshape(bf16[128,2,7168]{2,1,0:T(2,128)(2,1)} %all-gather.8.cloned.1.call-done) | data formatting | bytes 7340032 | tf_op jit(solution)/shard_map/reshape | solution.py:16
  215.5 9.6 %reshape.233 = bf16[256,16,448]{2,1,0:T(8,128)(2,1)} reshape(bf16[128,2,7168]{2,1,0:T(2,128)(2,1)} %all-gather.6.cloned.1.call-done) | data formatting | bytes 7340032 | tf_op jit(solution)/shard_map/reshape | solution.py:17
  225.1 4.8 fusion.62
  233.6 9.5 %all-to-all-done.2 = bf16[16,256,448]{1,2,0:T(8,128)(2,1)} async-done(((bf16[16,256,448]{1,2,0:T(8,128)(2,1)}), bf16[16,256,448]{1,2,0:T(8,128)(2,1)}, u32[]{:S(2)}, u32[]{:S(2)}) %all-to-all-start.2) | async-done | bytes 3670048 | tf_op jit(solution)/shard_map/all_to_all | solution.py:97
  243.1 8.3 %multiply_reduce_fusion = (f32[256]{0:T(256)S(1)}, bf16[256,256]{0,1:T(8,128)(2,1)S(1)}, bf16[256,256]{0,1:T(8,128)(2,1)S(1)}) fusion(f32[256,256]{0,1:T(8,128)S(1)} %fusion.61, f32[256,256]{0,1:T(8,128)S(1)} %fusion.62, f32[256]{0:T(256)S(1)} %reshape.245, bf16[16,256,448]{1,2,0:T(8,128)(2,1)} %all-to-all-done.2, bf16[256,16,448]{2,1,0:T(8,128)(2,1)} %reshape.233), kind=kOutput, calls=%fused_computation.32 | convolution fusion | flops 940637952 | bytes 8128512 | tf_op jit(solution)/shard_map/rsk,shk->rh/dot_general | solution.py:21
  251.5 6.2 %fusion.63 = f32[256,7168]{1,0:T(8,128)} fusion(bf16[256,256]{0,1:T(8,128)(2,1)S(1)} %get-tuple-element.39, bf16[7168,256]{1,0:T(8,128)(2,1)} %bitcast.10), kind=kOutput, calls=%fused_computation.105 | convolution fusion | flops 939524096 | bytes 11141120 | tf_op jit(solution)/shard_map/rh,dh->rd/dot_general | solution.py:32
  258.5 8.4 %convolution_add_fusion = f32[256,7168]{1,0:T(8,128)} fusion(f32[256,7168]{1,0:T(8,128)} %fusion.63, bf16[256,256]{0,1:T(8,128)(2,1)S(1)} %get-tuple-element.40, bf16[7168,256]{1,0:T(8,128)(2,1)} %bitcast.9), kind=kOutput, calls=%fused_computation.3 | convolution fusion | flops 941359104 | bytes 18481152 | tf_op jit(solution)/shard_map/rh,dh->rd/dot_general | solution.py:33
  266.8 9.7 %reshape.239 = f32[8,16,2,7168]{3,2,1,0:T(2,128)} reshape(f32[256,7168]{1,0:T(8,128)} %convolution_add_fusion) | data formatting | bytes 14680064 | tf_op jit(solution)/shard_map/reshape | solution.py:41
  276.6 8.3 %copy.96 = f32[8,16,2,7168]{3,1,2,0:T(8,128)} copy(f32[8,16,2,7168]{3,2,1,0:T(2,128)} %reshape.239) | data formatting | bytes 14680064 | tf_op jit(solution)/shard_map/reshape | solution.py:41
  284.8 8.5 %copy.103 = bf16[256,16,448]{0,1,2:T(8,128)(2,1)} copy(bf16[256,16,448]{2,1,0:T(8,128)(2,1)} %reshape.233) | data formatting | bytes 7340032 | tf_op jit(solution)/shard_map/reshape | solution.py:17
  293.4 4.4 all-to-all-start.7
  305.2 6.5 %all-to-all-start.10 = ((bf16[16,256,448]{1,2,0:T(8,128)(2,1)}), bf16[16,256,448]{1,2,0:T(8,128)(2,1)}, u32[]{:S(2)}, u32[]{:S(2)}) async-start(bf16[16,256,448]{1,2,0:T(8,128)(2,1)} %copy.104), calls=%async_computation.12 | async-start | bytes 7340032 | tf_op jit(solution)/shard_map/all_to_all | solution.py:144
  311.7 5.1 %convolution_convert_fusion.1 = bf16[7168,256]{1,0:T(8,128)(2,1)} fusion(bf16[256,7168]{1,0:T(8,128)(2,1)} %reshape.236, bf16[256,256]{0,1:T(8,128)(2,1)S(1)} %get-tuple-element.39), kind=kOutput, calls=%fused_computation.5 | convolution fusion | flops 941359104 | bytes 7471104 | tf_op jit(solution)/shard_map/rd,rh->dh/dot_general | solution.py:36
  316.8 42.8 %all-to-all-done.10 = bf16[16,256,448]{1,2,0:T(8,128)(2,1)} async-done(((bf16[16,256,448]{1,2,0:T(8,128)(2,1)}), bf16[16,256,448]{1,2,0:T(8,128)(2,1)}, u32[]{:S(2)}, u32[]{:S(2)}) %all-to-all-start.10) | async-done | bytes 3670048 | tf_op jit(solution)/shard_map/all_to_all | solution.py:144
  359.6 4.5 all-to-all-start.8
  364.1 5.1 convolution_convert_fusion
  369.2 46.3 %all-to-all-done.8 = bf16[16,448,256]{2,1,0:T(8,128)(2,1)} async-done(((bf16[16,448,256]{2,1,0:T(8,128)(2,1)}), bf16[16,448,256]{2,1,0:T(8,128)(2,1)}, u32[]{:S(2)}, u32[]{:S(2)}) %all-to-all-start.8) | async-done | bytes 3670048 | tf_op jit(solution)/shard_map/all_to_all | solution.py:142
  415.5 4.5 all-to-all-start.9
  426.1 41.8 %all-to-all-done.9 = bf16[16,448,256]{2,1,0:T(8,128)(2,1)} async-done(((bf16[16,448,256]{2,1,0:T(8,128)(2,1)}), bf16[16,448,256]{2,1,0:T(8,128)(2,1)}, u32[]{:S(2)}, u32[]{:S(2)}) %all-to-all-start.9) | async-done | bytes 3670048 | tf_op jit(solution)/shard_map/all_to_all | solution.py:143
  491.2 8.5 %convolution_convert_fusion.2 = bf16[256,7168]{1,0:T(8,128)(2,1)} fusion(f32[32,256]{1,0:T(8,128)S(1)} %convert_reduce_fusion, f32[32,7168]{1,0:T(8,128)} %reshape.240), kind=kOutput, calls=%fused_computation.6 | convolution fusion | flops 706478080 | bytes 4620288 | tf_op jit(solution)/shard_map/qt,qd->td/dot_general | solution.py:125
  (93 shorter events, 70.7 us)
Async XLA Ops:
  7.2 44.4 %copy-start = (bf16[8,448,256]{2,1,0:T(8,128)(2,1)S(1)}, bf16[8,448,256]{2,1,0:T(8,128)(2,1)}, u32[]{:S(2)}) copy-start(bf16[8,448,256]{2,1,0:T(8,128)(2,1)} %param.16) | copy-start | bytes 5505028
  7.2 199.9 %all-gather.8.cloned.1.call-start = ((), (), s32[]{:S(2)}) async-start(), calls=%async_computation.16 | async-start | bytes 4128768 | tf_op jit(solution)/shard_map/all_gather | solution.py:108
  23.9 22.3 %copy-start.6 = (bf16[256,8]{0,1:T(8,128)(2,1)S(1)}, bf16[256,8]{0,1:T(8,128)(2,1)}, u32[]{:S(2)}) copy-start(bf16[256,8]{0,1:T(8,128)(2,1)} %param.12) | copy-start | bytes 12292
  24.0 26.8 %copy-start.5 = (s32[256,2]{0,1:T(2,128)S(1)}, s32[256,2]{0,1:T(2,128)}, u32[]{:S(2)}) copy-start(s32[256,2]{0,1:T(2,128)} %param.14) | copy-start | bytes 6148
  47.3 14.9 %all-to-all-start = ((bf16[16,1,2]{2,1,0:T(2,128)(2,1)}), bf16[16,1,2]{2,1,0:T(2,128)(2,1)S(1)}, u32[]{:S(2)}, u32[]{:S(2)}) async-start(bf16[16,1,2]{2,1,0:T(2,128)(2,1)} %all_to_all.48), calls=%async_computation | async-start | bytes 16384 | tf_op jit(solution)/shard_map/all_to_all | solution.py:104
  62.2 16.9 %all-to-all-start.1 = ((bf16[16,2,7168]{2,1,0:T(2,128)(2,1)}), bf16[16,2,7168]{2,1,0:T(2,128)(2,1)S(1)}, u32[]{:S(2)}, u32[]{:S(2)}) async-start(bf16[16,2,7168]{2,1,0:T(2,128)(2,1)} %reshape.232), calls=%async_computation.1 | async-start | bytes 917504 | tf_op jit(solution)/shard_map/all_to_all | solution.py:103
  79.1 0.8 copy-start.4
  79.9 54.3 %all-to-all-start.5 = ((bf16[16,448,256]{2,1,0:T(8,128)(2,1)}), bf16[16,448,256]{2,1,0:T(8,128)(2,1)}, u32[]{:S(2)}, u32[]{:S(2)}) async-start(bf16[16,448,256]{2,1,0:T(8,128)(2,1)} %get-tuple-element.44), calls=%async_computation.5 | async-start | bytes 7340032 | tf_op jit(solution)/shard_map/all_to_all | solution.py:95
  84.5 131.0 %all-gather.6.cloned.1.call-start = ((), (), s32[]{:S(2)}) async-start(), calls=%async_computation.15 | async-start | bytes 4128768 | tf_op jit(solution)/shard_map/all_gather | solution.py:109
  134.2 4.7 copy-start.3
  134.2 54.7 %all-to-all-start.4 = ((bf16[16,448,256]{2,1,0:T(8,128)(2,1)}), bf16[16,448,256]{2,1,0:T(8,128)(2,1)}, u32[]{:S(2)}, u32[]{:S(2)}) async-start(bf16[16,448,256]{2,1,0:T(8,128)(2,1)} %get-tuple-element.43), calls=%async_computation.4 | async-start | bytes 7340032 | tf_op jit(solution)/shard_map/all_to_all | solution.py:96
  188.9 54.3 %all-to-all-start.2 = ((bf16[16,256,448]{1,2,0:T(8,128)(2,1)}), bf16[16,256,448]{1,2,0:T(8,128)(2,1)}, u32[]{:S(2)}, u32[]{:S(2)}) async-start(bf16[16,256,448]{1,2,0:T(8,128)(2,1)} %broadcast_select_fusion.2), calls=%async_computation.2 | async-start | bytes 7340032 | tf_op jit(solution)/shard_map/all_to_all | solution.py:97
  193.4 100.0 %reduce-scatter.5.cloned.1.call-start = ((), (), s32[]{:S(2)}) async-start(), calls=%async_computation.14 | async-start | bytes 73728 | tf_op jit(solution)/shard_map/reduce_scatter | solution.py:119
  225.1 4.8 copy-start.2
  258.4 164.8 %reduce-scatter.3.cloned.1.call-start = ((), (), s32[]{:S(2)}) async-start(), calls=%async_computation.13 | async-start | bytes 8257536 | tf_op jit(solution)/shard_map/reduce_scatter | solution.py:118
  293.4 11.8 %all-to-all-start.7 = ((f32[1,16,2]{2,0,1:T(1,128)}), f32[1,16,2]{2,0,1:T(1,128)S(1)}, u32[]{:S(2)}, u32[]{:S(2)}) async-start(f32[1,16,2]{2,0,1:T(1,128)} %bitcast.76), calls=%async_computation.9 | async-start | bytes 16384 | tf_op jit(solution)/shard_map/all_to_all | solution.py:123
  305.2 54.4 %all-to-all-start.10 = ((bf16[16,256,448]{1,2,0:T(8,128)(2,1)}), bf16[16,256,448]{1,2,0:T(8,128)(2,1)}, u32[]{:S(2)}, u32[]{:S(2)}) async-start(bf16[16,256,448]{1,2,0:T(8,128)(2,1)} %copy.104), calls=%async_computation.12 | async-start | bytes 7340032 | tf_op jit(solution)/shard_map/all_to_all | solution.py:144
  359.6 55.9 %all-to-all-start.8 = ((bf16[16,448,256]{2,1,0:T(8,128)(2,1)}), bf16[16,448,256]{2,1,0:T(8,128)(2,1)}, u32[]{:S(2)}, u32[]{:S(2)}) async-start(bf16[16,448,256]{2,1,0:T(8,128)(2,1)} %bitcast.72), calls=%async_computation.10 | async-start | bytes 7340032 | tf_op jit(solution)/shard_map/all_to_all | solution.py:142
  415.5 52.3 %all-to-all-start.9 = ((bf16[16,448,256]{2,1,0:T(8,128)(2,1)}), bf16[16,448,256]{2,1,0:T(8,128)(2,1)}, u32[]{:S(2)}, u32[]{:S(2)}) async-start(bf16[16,448,256]{2,1,0:T(8,128)(2,1)} %bitcast.71), calls=%async_computation.11 | async-start | bytes 7340032 | tf_op jit(solution)/shard_map/all_to_all | solution.py:143
  467.9 21.7 %all-to-all-start.6 = ((f32[1,16,2,7168]{3,2,0,1:T(2,128)}), f32[1,16,2,7168]{3,2,0,1:T(2,128)S(1)}, u32[]{:S(2)}, u32[]{:S(2)}) async-start(f32[1,16,2,7168]{3,2,0,1:T(2,128)} %copy.97), calls=%async_computation.7 | async-start | bytes 1835008 | tf_op jit(solution)/shard_map/all_to_all | solution.py:122
  488.0 11.7 %copy-start.1 = (bf16[8,448,256]{2,1,0:T(8,128)(2,1)S(1)}, bf16[8,448,256]{2,1,0:T(8,128)(2,1)}, u32[]{:S(2)}) copy-start(bf16[8,448,256]{2,1,0:T(8,128)(2,1)} %param.16) | copy-start | bytes 5505028
Sparse Core Ops, SparseCore 0:
  46.2 27.3 all-gather.7
  87.6 31.3 all-gather.5
  258.6 29.2 reduce-scatter.4
  290.1 46.3 reduce-scatter.2
where the time goes:
time: 516 us; the launch traced here: 506 us
  waiting for transfers between devices  237 us (46%)
  local copies, waits for them, and re-layouts  74.5 us (14%)
  matrix products  73 us (14%)
  starting transfers between devices  48.7 us (9%)
  blocking collectives  32.2 us (6%)
  other arithmetic  27.2 us (5%)
  between operations  14.3 us (3%)
    all_to_all x1, waiting for transfers between devices, local(): lax.all_to_all(copy_gate, 'dev', split_axis=0, concat_axis=0, tiled=True)  48.9 us
    all_to_all x1, waiting for transfers between devices, local(): lax.all_to_all(send_gate, 'dev', split_axis=0, concat_axis=0, tiled=True)  46.3 us
    all_to_all x1, waiting for transfers between devices, local(): lax.all_to_all(copy_up, 'dev', split_axis=0, concat_axis=0, tiled=True)  43.1 us
    all_to_all x1, waiting for transfers between devices, local(): lax.all_to_all(send_down, 'dev', split_axis=0, concat_axis=0, tiled=True)  42.8 us
    all_to_all x1, waiting for transfers between devices, local(): lax.all_to_all(send_up, 'dev', split_axis=0, concat_axis=0, tiled=True)  41.8 us
    all_to_all x1, blocking collectives, local(): lax.all_to_all(x_send, 'dev', split_axis=0, concat_axis=0, tiled=True)  18.9 us
    reshape x2, local copies, waits for them, and re-layouts, expert_pass(): dy_split = dy_piece.reshape(-1, slot_count, model_width // slot_count)  18.1 us
    reshape x2, local copies, waits for them, and re-layouts, expert_pass(): row_acc = row_terms.reshape(lead_count, slot_count, -1, model_width)  18 us
  transfers between devices with their start and end apart: 14, of which 8 were waited for; matrix products, arithmetic and copies ran while one was open for 25% of the time, Pallas kernels for 0%

commit v1 on v0

v1 whole, which is shorter than its diff:
```python
import jax
import jax.numpy as jnp
from jax import lax
from jax.sharding import PartitionSpec as P

TOP = 8
CAP = 2
REPS = 2


def routing(expert_ids, slot_plan, slot_count, round_total):
    expert_count = slot_plan.shape[0]
    in_round = (slot_plan[:, 0] < slot_count).astype(jnp.int32)
    expert_rank = jnp.cumsum(in_round) - 1
    rank_match = (in_round[:, None] > 0) & (
        expert_rank[:, None] == jnp.arange(round_total, dtype=jnp.int32)[None, :]
    )
    hot_ids = jnp.sum(
        jnp.where(rank_match, jnp.arange(expert_count, dtype=jnp.int32)[:, None], 0), axis=0
    )
    match = expert_ids[:, :, None] == hot_ids[None, None, :]
    named = jnp.sum(match.astype(jnp.int32), axis=1)
    tok_rows = expert_ids.shape[0]
    earlier = (
        jnp.arange(tok_rows, dtype=jnp.int32)[None, :] < jnp.arange(tok_rows, dtype=jnp.int32)[:, None]
    ).astype(jnp.bfloat16)
    before = jnp.dot(earlier, named.astype(jnp.bfloat16), preferred_element_type=jnp.float32).astype(
        jnp.int32
    )
    rank_ids = jnp.arange(round_total, dtype=jnp.int32)[None, :]
    column = REPS * rank_ids + before % REPS
    target = column * CAP + before // REPS
    return match, named, target


def local(tokens, grad_out, router_gates, expert_ids, slot_plan, w_gate, w_up, w_down):
    slot_count = lax.axis_size("dev")
    tok_rows, model_width = tokens.shape
    hidden_width = w_gate.shape[2]
    round_total = w_gate.shape[0]
    row_slots = slot_count * CAP
    chunk = model_width // slot_count

    send_wg = jnp.broadcast_to(w_gate[:, None], (round_total, REPS) + w_gate.shape[1:]).reshape(
        slot_count, chunk, hidden_width
    )
    send_wu = jnp.broadcast_to(w_up[:, None], (round_total, REPS) + w_up.shape[1:]).reshape(
        slot_count, chunk, hidden_width
    )
    down_t = jnp.swapaxes(w_down, 1, 2)
    send_wd = jnp.broadcast_to(down_t[:, None], (round_total, REPS) + down_t.shape[1:]).reshape(
        slot_count, chunk, hidden_width
    )
    slot_gate = lax.all_to_all(send_wg, "dev", 0, 0, tiled=True).reshape(model_width, hidden_width)
    slot_up = lax.all_to_all(send_wu, "dev", 0, 0, tiled=True).reshape(model_width, hidden_width)
    slot_down_t = lax.all_to_all(send_wd, "dev", 0, 0, tiled=True).reshape(model_width, hidden_width)

    match, named, target = routing(expert_ids, slot_plan, slot_count, round_total)
    q_ids = jnp.arange(row_slots, dtype=jnp.int32)
    chooser = (named[None, :, :] > 0) & (target[None, :, :] == q_ids[:, None, None])
    pick_rows = jnp.sum(chooser.astype(jnp.float32), axis=-1)
    pick_half = pick_rows.astype(jnp.bfloat16)
    gates_f = router_gates.astype(jnp.float32)
    rank_gate = jnp.sum(jnp.where(match, gates_f[:, :, None], 0.0), axis=1)
    gate_send = jnp.sum(jnp.where(chooser, rank_gate[None, :, :], 0.0), axis=(1, 2)).astype(jnp.bfloat16)

    x_send = jnp.dot(pick_half, tokens, preferred_element_type=jnp.float32).astype(jnp.bfloat16)
    dy_send = jnp.dot(pick_half, grad_out, preferred_element_type=jnp.float32).astype(jnp.bfloat16)
    got_x = lax.all_to_all(x_send.reshape(slot_count, CAP, model_width), "dev", 0, 0, tiled=True)
    got_dy = lax.all_to_all(dy_send.reshape(slot_count, CAP, model_width), "dev", 0, 0, tiled=True)
    got_gate = lax.all_to_all(gate_send.reshape(slot_count, CAP), "dev", 0, 0, tiled=True)
    x_rows = lax.all_gather(got_x.reshape(row_slots, model_width), "node", axis=0, tiled=True)
    dy_rows = lax.all_gather(got_dy.reshape(row_slots, model_width), "node", axis=0, tiled=True)
    gate_rows = lax.all_gather(got_gate.reshape(row_slots), "node", axis=0, tiled=True).astype(
        jnp.float32
    )[:, None]

    gate_pre = jnp.dot(x_rows, slot_gate, preferred_element_type=jnp.float32)
    up_pre = jnp.dot(x_rows, slot_up, preferred_element_type=jnp.float32)
    back_proj = jnp.dot(dy_rows, slot_down_t, preferred_element_type=jnp.float32)
    sigmoid_gate = jax.nn.sigmoid(gate_pre)
    active = gate_pre * sigmoid_gate
    hidden = active * up_pre
    scaled_back = gate_rows * back_proj
    d_gate = (scaled_back * up_pre * sigmoid_gate * (1.0 + gate_pre * (1.0 - sigmoid_gate))).astype(
        jnp.bfloat16
    )
    d_up = (scaled_back * active).astype(jnp.bfloat16)
    scaled_hidden = (gate_rows * hidden).astype(jnp.bfloat16)
    gate_terms = jnp.sum(back_proj * hidden, axis=-1)

    acc_gate = jnp.einsum("rd,rh->dh", x_rows, d_gate, preferred_element_type=jnp.float32)
    acc_up = jnp.einsum("rd,rh->dh", x_rows, d_up, preferred_element_type=jnp.float32)
    acc_down = jnp.einsum("rd,rh->dh", dy_rows, scaled_hidden, preferred_element_type=jnp.float32)
    row_terms = jnp.einsum("rh,dh->rd", d_gate, slot_gate, preferred_element_type=jnp.float32)
    row_terms = row_terms + jnp.einsum("rh,dh->rd", d_up, slot_up, preferred_element_type=jnp.float32)

    summed_rows = lax.psum_scatter(row_terms, "node", scatter_dimension=0, tiled=True)
    summed_gates = lax.psum_scatter(gate_terms, "node", scatter_dimension=0, tiled=True)
    back_rows = lax.all_to_all(summed_rows.reshape(slot_count, CAP, model_width), "dev", 0, 0, tiled=True)
    back_gates = lax.all_to_all(summed_gates.reshape(slot_count, CAP), "dev", 0, 0, tiled=True)

    grad_tokens = jnp.einsum(
        "qt,qd->td",
        pick_rows,
        back_rows.reshape(row_slots, model_width),
        precision=lax.Precision.HIGHEST,
    ).astype(jnp.bfloat16)
    back_q = back_gates.reshape(row_slots)
    rank_back = jnp.sum(jnp.where(chooser, back_q[:, None, None], 0.0), axis=0)
    grad_gates = jnp.sum(jnp.where(match, rank_back[:, None, :], 0.0), axis=-1)

    def pair_sum(acc):
        sent = acc.astype(jnp.bfloat16).reshape(slot_count, chunk, hidden_width)
        got = lax.all_to_all(sent, "dev", 0, 0, tiled=True)
        got = got.reshape(round_total, REPS, chunk, hidden_width).astype(jnp.float32)
        return jnp.sum(got, axis=1).astype(jnp.bfloat16)

    grad_w_gate = pair_sum(acc_gate)
    grad_w_up = pair_sum(acc_up)
    grad_w_down = jnp.swapaxes(pair_sum(acc_down), 1, 2)
    return (grad_tokens, grad_gates, grad_w_gate, grad_w_up, grad_w_down)


def solution(mesh):
    return jax.shard_map(
        local,
        mesh=mesh,
        in_specs=(
            P(("node", "dev"), None),
            P(("node", "dev"), None),
            P(("node", "dev"), None),
            P(("node", "dev"), None),
            P(),
            P(None, "dev", "node"),
            P(None, "dev", "node"),
            P(None, "node", "dev"),
        ),
        out_specs=(
            P(("node", "dev"), None),
            P(("node", "dev"), None),
            P(None, "dev", "node"),
            P(None, "dev", "node"),
            P(None, "node", "dev"),
        ),
        check_vma=False,
    )
```

time: 516 us -> 488 us (0.946); the launches traced: 506 us -> 486 us
  blocking collectives: 32.2 us -> 104 us
  local copies, waits for them, and re-layouts: 74.5 us -> 13.5 us
  matrix products: 73 us -> 51.1 us
  starting transfers between devices: 48.7 us -> 34.5 us
  waiting for transfers between devices: 237 us -> 250 us
  other arithmetic: 27.2 us -> 17.8 us
    all_to_all x1 -> x3, blocking collectives: 18.9 us -> 79 us  [the longest x1 47.3 us: local(): lax.all_to_all(send_wg, 'dev', 0, 0, tiled=True)]
    reshape x12 -> x7, local copies, waits for them, and re-layouts: 48.3 us -> 5.59 us  [the longest x1 2.63 us: local(): summed_rows.reshape(slot_count, CAP, model_width)]
    unnamed x0 -> x2, blocking collectives: none -> 25 us
    dot_general x14 -> x10, matrix products: 67.3 us -> 45.6 us  [the longest x1 7.37 us: local(): jnp.einsum('qt,qd->td', pick_rows, back_rows.reshape(row_slots, model_wid...]
    all_to_all x10 -> x8, starting transfers between devices: 48.5 us -> 34.4 us  [the longest x3 13.7 us: pair_sum(): got = lax.all_to_all(sent, 'dev', 0, 0, tiled=True)]
    all_to_all x10 -> x8, waiting for transfers between devices: 236 us -> 250 us  [the longest x3 147 us: pair_sum(): got = lax.all_to_all(sent, 'dev', 0, 0, tiled=True)]
    all_gather x1 -> x0, blocking collectives: 13.3 us -> none  [local(): lax.all_gather(got_gate[None], 'node', axis=0, tiled=True)]
    select_n x4 -> x0, other arithmetic: 11.4 us -> none  [the longest x1 7.07 us: local(): copy_up = jnp.take(w_up, slot_rank, axis=0)]
  transfers between devices with their start and end apart: 14 -> 11, of which waited for: 8 -> 8; matrix products, arithmetic and copies ran while one was open for 25% -> 10% of each run, Pallas kernels for 0% -> 0%
where the time goes in v1:
time: 488 us; the launch traced here: 486 us
  waiting for transfers between devices  250 us (51%)
  blocking collectives  104 us (21%)
  matrix products  51.1 us (10%)
  starting transfers between devices  34.5 us (7%)
  other arithmetic  17.8 us (4%)
  between operations  15.3 us (3%)
  local copies, waits for them, and re-layouts  13.5 us (3%)
    all_to_all x3, waiting for transfers between devices, pair_sum(): got = lax.all_to_all(sent, 'dev', 0, 0, tiled=True)  147 us
    all_to_all x1, blocking collectives, local(): lax.all_to_all(send_wg, 'dev', 0, 0, tiled=True)  47.3 us
    all_to_all x1, waiting for transfers between devices, local(): lax.all_to_all(send_wu, 'dev', 0, 0, tiled=True)  46.6 us
    all_to_all x1, waiting for transfers between devices, local(): lax.all_to_all(send_wd, 'dev', 0, 0, tiled=True)  41.6 us
    unnamed x2, blocking collectives  25 us
    all_to_all x1, blocking collectives, local(): lax.all_to_all(x_send.reshape(slot_count, CAP, model_width), 'dev', 0, 0,...  18.7 us
    all_to_all x3, starting transfers between devices, pair_sum(): got = lax.all_to_all(sent, 'dev', 0, 0, tiled=True)  13.7 us
    reduce_sum x3, other arithmetic, pair_sum(): return jnp.sum(got, axis=1).astype(jnp.bfloat16)  13.7 us
  transfers between devices with their start and end apart: 11, of which 8 were waited for; matrix products, arithmetic and copies ran while one was open for 10% of the time, Pallas kernels for 0%

profile of v1, /device:TPU:0, one launch (start us, length us, event | category | flops | bytes accessed | tf_op | source)
XLA Modules:
  0.0 486.1 jit_solution(14651455129305589135)
XLA Ops:
  12.7 18.7 %all_to_all.60 = bf16[16,2,7168]{2,1,0:T(2,128)(2,1)S(1)} all-to-all(bf16[16,2,7168]{2,1,0:T(2,128)(2,1)S(1)} %reshape.145), channel_id=1, replica_groups=mesh['node'=8,'dev'=16] {'dev'}, dimensions={0} | all-to-all | bytes 917504 | tf_op jit(solution)/shard_map/all_to_all | solution.py:69
  35.4 13.0 %all_to_all.61 = bf16[16,2,7168]{2,1,0:T(2,128)(2,1)S(1)} all-to-all(bf16[16,2,7168]{2,1,0:T(2,128)(2,1)S(1)} %reshape.141), channel_id=1, replica_groups=mesh['node'=8,'dev'=16] {'dev'}, dimensions={0} | all-to-all | bytes 917504 | tf_op jit(solution)/shard_map/all_to_all | solution.py:70
  48.7 47.3 %all_to_all.62 = bf16[16,448,256]{2,1,0:T(8,128)(2,1)} all-to-all(bf16[16,448,256]{2,1,0:T(8,128)(2,1)S(1)} %bitcast.49), channel_id=1, replica_groups=mesh['node'=8,'dev'=16] {'dev'}, dimensions={0} | all-to-all | bytes 7340032 | tf_op jit(solution)/shard_map/all_to_all | solution.py:54
  98.2 4.6 all-to-all-start.4
  103.9 46.6 %all-to-all-done.4 = bf16[16,448,256]{2,1,0:T(8,128)(2,1)} async-done(((bf16[16,448,256]{2,1,0:T(8,128)(2,1)}), bf16[16,448,256]{2,1,0:T(8,128)(2,1)}, u32[]{:S(2)}, u32[]{:S(2)}) %all-to-all-start.4) | async-done | bytes 3670048 | tf_op jit(solution)/shard_map/all_to_all | solution.py:55
  152.7 4.6 all-to-all-start.2
  158.7 4.8 fusion.21
  163.5 3.7 fusion.20
  167.2 41.6 %all-to-all-done.2 = bf16[16,448,256]{2,1,0:T(8,128)(2,1)} async-done(((bf16[16,448,256]{2,1,0:T(8,128)(2,1)}), bf16[16,448,256]{2,1,0:T(8,128)(2,1)}, u32[]{:S(2)}, u32[]{:S(2)}) %all-to-all-start.2) | async-done | bytes 3670048 | tf_op jit(solution)/shard_map/all_to_all | solution.py:56
  208.8 4.7 multiply_reduce_fusion
  213.5 12.4 %all-reduce.1 = f32[256]{0:T(256)S(1)} all-reduce(f32[256]{0:T(256)S(1)} %get-tuple-element.13), channel_id=3, replica_groups=mesh['node'=8,'dev'=16] {'node'}, use_global_device_ids=true, to_apply=%region_9.10.clone | all-reduce | flops 256 | bytes 2048
  226.7 3.9 all-to-all-start.7
  230.7 7.4 %all-to-all-done.7 = f32[16,1,2]{2,1,0:T(1,128)S(1)} async-done(((f32[16,1,2]{2,1,0:T(1,128)}), f32[16,1,2]{2,1,0:T(1,128)S(1)}, u32[]{:S(2)}, u32[]{:S(2)}) %all-to-all-start.7) | async-done | bytes 160 | tf_op jit(solution)/shard_map/all_to_all | solution.py:101
  240.4 3.5 all-to-all-start
  244.6 6.7 %all-to-all-done = bf16[16,1,2]{2,1,0:T(2,128)(2,1)S(1)} async-done(((bf16[16,1,2]{2,1,0:T(2,128)(2,1)}), bf16[16,1,2]{2,1,0:T(2,128)(2,1)S(1)}, u32[]{:S(2)}, u32[]{:S(2)}) %all-to-all-start) | async-done | bytes 96 | tf_op jit(solution)/shard_map/all_to_all | solution.py:71
  251.7 12.6 %all-reduce = bf16[256]{0:T(256)(128)(2,1)S(1)} all-reduce(bf16[256]{0:T(256)(128)(2,1)S(1)} %dynamic-update-slice), channel_id=1, replica_groups=mesh['node'=8,'dev'=16] {'node'}, use_global_device_ids=true, to_apply=%add | all-reduce | flops 256 | bytes 1024
  264.5 3.2 fusion.22
  267.7 6.3 %convolution_add_fusion = f32[256,7168]{1,0:T(8,128)} fusion(f32[256,7168]{1,0:T(8,128)S(1)} %fusion.22, bf16[256,256]{0,1:T(8,128)(2,1)S(1)} %get-tuple-element.7, bf16[7168,256]{1,0:T(8,128)(2,1)} %bitcast.7), kind=kOutput, calls=%fused_computation | convolution fusion | flops 941359104 | bytes 18481152 | tf_op jit(solution)/shard_map/rh,dh->rd/dot_general | solution.py:96
  274.0 5.1 %convolution_convert_fusion = bf16[7168,256]{1,0:T(8,128)(2,1)} fusion(bf16[256,7168]{1,0:T(8,128)(2,1)} %all-gather.3.cloned.1.call-done, f32[256]{0:T(256)S(1)} %convert_element_type.89, f32[256,256]{0,1:T(8,128)S(1)} %fusion.20, f32[256,256]{0,1:T(8,128)S(1)} %fusion.21), kind=kOutput, calls=%fused_computation.1 | convolution fusion | flops 941817856 | bytes 7865344 | tf_op jit(solution)/shard_map/rd,rh->dh/dot_general | solution.py:94
  279.1 4.5 all-to-all-start.10
  283.6 5.1 %convolution_convert_fusion.1 = bf16[7168,256]{1,0:T(8,128)(2,1)} fusion(bf16[256,7168]{1,0:T(8,128)(2,1)} %all-gather.5.cloned.1.call-done, bf16[256,256]{0,1:T(8,128)(2,1)S(1)} %get-tuple-element.7), kind=kOutput, calls=%fused_computation.2 | convolution fusion | flops 941359104 | bytes 7471104 | tf_op jit(solution)/shard_map/rd,rh->dh/dot_general | solution.py:93
  288.7 51.1 %all-to-all-done.10 = bf16[16,448,256]{2,1,0:T(8,128)(2,1)} async-done(((bf16[16,448,256]{2,1,0:T(8,128)(2,1)}), bf16[16,448,256]{2,1,0:T(8,128)(2,1)}, u32[]{:S(2)}, u32[]{:S(2)}) %all-to-all-start.10) | async-done | bytes 3670048 | tf_op jit(solution)/shard_map/all_to_all | solution.py:115
  339.8 4.7 all-to-all-start.9
  344.5 5.1 %convolution_convert_fusion.2 = bf16[7168,256]{1,0:T(8,128)(2,1)} fusion(bf16[256,7168]{1,0:T(8,128)(2,1)} %all-gather.5.cloned.1.call-done, bf16[256,256]{0,1:T(8,128)(2,1)S(1)} %get-tuple-element.8), kind=kOutput, calls=%fused_computation.3 | convolution fusion | flops 941359104 | bytes 7471104 | tf_op jit(solution)/shard_map/rd,rh->dh/dot_general | solution.py:92
  349.6 48.6 %all-to-all-done.9 = bf16[16,448,256]{2,1,0:T(8,128)(2,1)} async-done(((bf16[16,448,256]{2,1,0:T(8,128)(2,1)}), bf16[16,448,256]{2,1,0:T(8,128)(2,1)}, u32[]{:S(2)}, u32[]{:S(2)}) %all-to-all-start.9) | async-done | bytes 3670048 | tf_op jit(solution)/shard_map/all_to_all | solution.py:115
  398.1 4.5 all-to-all-start.8
  406.0 47.7 %all-to-all-done.8 = bf16[16,448,256]{2,1,0:T(8,128)(2,1)} async-done(((bf16[16,448,256]{2,1,0:T(8,128)(2,1)}), bf16[16,448,256]{2,1,0:T(8,128)(2,1)}, u32[]{:S(2)}, u32[]{:S(2)}) %all-to-all-start.8) | async-done | bytes 3670048 | tf_op jit(solution)/shard_map/all_to_all | solution.py:115
  453.6 4.0 all-to-all-start.6
  457.7 4.6 bitcast_reduce_fusion
  462.2 4.6 bitcast_reduce_fusion.1
  466.8 4.6 bitcast_reduce_fusion.2
  472.2 7.4 %convolution_convert_fusion.3 = bf16[256,7168]{1,0:T(8,128)(2,1)} fusion(f32[32,256]{1,0:T(8,128)S(1)} %convert_reduce_fusion, f32[32,7168]{1,0:T(8,128)S(1)} %reshape.152), kind=kOutput, calls=%fused_computation.4 | convolution fusion | flops 706478080 | bytes 4620288 | tf_op jit(solution)/shard_map/qt,qd->td/dot_general | solution.py:103
  (64 shorter events, 23.8 us)
Async XLA Ops:
  7.2 151.5 %all-gather.5.cloned.1.call-start = ((), (), s32[]{:S(2)}) async-start(), calls=%async_computation.13 | async-start | bytes 4128768 | tf_op jit(solution)/shard_map/all_gather | solution.py:72
  31.5 16.9 %copy-start.1 = (bf16[8,448,256]{2,1,0:T(8,128)(2,1)S(1)}, bf16[8,448,256]{2,1,0:T(8,128)(2,1)}, u32[]{:S(2)}) copy-start(bf16[8,448,256]{2,1,0:T(8,128)(2,1)} %param.13) | copy-start | bytes 5505028
  48.7 47.3 %copy-start.2 = (bf16[8,448,256]{2,1,0:T(8,128)(2,1)S(1)}, bf16[8,448,256]{2,1,0:T(8,128)(2,1)}, u32[]{:S(2)}) copy-start(bf16[8,448,256]{2,1,0:T(8,128)(2,1)} %param.14) | copy-start | bytes 5505028
  98.2 52.2 %copy-start.3 = (bf16[8,256,448]{1,2,0:T(8,128)(2,1)S(1)}, bf16[8,256,448]{1,2,0:T(8,128)(2,1)}, u32[]{:S(2)}) copy-start(bf16[8,256,448]{1,2,0:T(8,128)(2,1)} %param.15) | copy-start | bytes 5505028
  98.2 52.2 %all-to-all-start.4 = ((bf16[16,448,256]{2,1,0:T(8,128)(2,1)}), bf16[16,448,256]{2,1,0:T(8,128)(2,1)}, u32[]{:S(2)}, u32[]{:S(2)}) async-start(bf16[16,448,256]{2,1,0:T(8,128)(2,1)} %bitcast.48), calls=%async_computation.4 | async-start | bytes 7340032 | tf_op jit(solution)/shard_map/all_to_all | solution.py:55
  102.9 105.9 %all-gather.3.cloned.1.call-start = ((), (), s32[]{:S(2)}) async-start(), calls=%async_computation.12 | async-start | bytes 4128768 | tf_op jit(solution)/shard_map/all_gather | solution.py:73
  152.7 4.7 copy-start.5
  152.7 4.7 copy-start.6
  152.7 56.1 %all-to-all-start.2 = ((bf16[16,448,256]{2,1,0:T(8,128)(2,1)}), bf16[16,448,256]{2,1,0:T(8,128)(2,1)}, u32[]{:S(2)}, u32[]{:S(2)}) async-start(bf16[16,448,256]{2,1,0:T(8,128)(2,1)} %bitcast.47), calls=%async_computation.2 | async-start | bytes 7340032 | tf_op jit(solution)/shard_map/all_to_all | solution.py:56
  158.7 4.8 copy-start
  208.8 21.8 %copy-start.4 = (s32[256,8]{0,1:T(8,128)S(1)}, s32[256,8]{0,1:T(8,128)}, u32[]{:S(2)}) copy-start(s32[256,8]{0,1:T(8,128)} %param.11) | copy-start | bytes 24580
  226.7 11.4 %all-to-all-start.7 = ((f32[16,1,2]{2,1,0:T(1,128)}), f32[16,1,2]{2,1,0:T(1,128)S(1)}, u32[]{:S(2)}, u32[]{:S(2)}) async-start(f32[16,1,2]{2,1,0:T(1,128)} %bitcast.10), calls=%async_computation.8 | async-start | bytes 16384 | tf_op jit(solution)/shard_map/all_to_all | solution.py:101
  240.4 10.9 %all-to-all-start = ((bf16[16,1,2]{2,1,0:T(2,128)(2,1)}), bf16[16,1,2]{2,1,0:T(2,128)(2,1)S(1)}, u32[]{:S(2)}, u32[]{:S(2)}) async-start(bf16[16,1,2]{2,1,0:T(2,128)(2,1)} %convert_element_type.101), calls=%async_computation | async-start | bytes 16384 | tf_op jit(solution)/shard_map/all_to_all | solution.py:71
  243.9 159.5 %reduce-scatter.2.cloned.1.call-start = ((), (), s32[]{:S(2)}) async-start(), calls=%async_computation.14 | async-start | bytes 8257536 | tf_op jit(solution)/shard_map/reduce_scatter | solution.py:98
  279.1 60.7 %all-to-all-start.10 = ((bf16[16,448,256]{2,1,0:T(8,128)(2,1)}), bf16[16,448,256]{2,1,0:T(8,128)(2,1)}, u32[]{:S(2)}, u32[]{:S(2)}) async-start(bf16[16,448,256]{2,1,0:T(8,128)(2,1)} %bitcast.46), calls=%async_computation.11 | async-start | bytes 7340032 | tf_op jit(solution)/shard_map/all_to_all | solution.py:115
  339.8 58.3 %all-to-all-start.9 = ((bf16[16,448,256]{2,1,0:T(8,128)(2,1)}), bf16[16,448,256]{2,1,0:T(8,128)(2,1)}, u32[]{:S(2)}, u32[]{:S(2)}) async-start(bf16[16,448,256]{2,1,0:T(8,128)(2,1)} %bitcast.45), calls=%async_computation.10 | async-start | bytes 7340032 | tf_op jit(solution)/shard_map/all_to_all | solution.py:115
  398.1 55.5 %all-to-all-start.8 = ((bf16[16,448,256]{2,1,0:T(8,128)(2,1)}), bf16[16,448,256]{2,1,0:T(8,128)(2,1)}, u32[]{:S(2)}, u32[]{:S(2)}) async-start(bf16[16,448,256]{2,1,0:T(8,128)(2,1)} %bitcast.44), calls=%async_computation.9 | async-start | bytes 7340032 | tf_op jit(solution)/shard_map/all_to_all | solution.py:115
  453.6 17.9 %all-to-all-start.6 = ((f32[16,2,7168]{2,1,0:T(2,128)}), f32[16,2,7168]{2,1,0:T(2,128)S(1)}, u32[]{:S(2)}, u32[]{:S(2)}) async-start(f32[16,2,7168]{2,1,0:T(2,128)} %reshape.151), calls=%async_computation.7 | async-start | bytes 1835008 | tf_op jit(solution)/shard_map/all_to_all | solution.py:100
Sparse Core Ops, SparseCore 0:
  32.6 27.3 all-gather.4
  106.0 31.2 all-gather.2
  274.1 42.5 reduce-scatter.1

commit v2 on v1

v2 whole, which is shorter than its diff:
```python
import jax
import jax.numpy as jnp
from jax import lax
from jax.sharding import PartitionSpec as P

TOP = 8
CAP = 2
REPS = 2
LANE = 128


def routing(expert_ids, slot_plan, slot_count, round_total):
    expert_count = slot_plan.shape[0]
    in_round = (slot_plan[:, 0] < slot_count).astype(jnp.int32)
    expert_rank = jnp.cumsum(in_round) - 1
    rank_match = (in_round[:, None] > 0) & (
        expert_rank[:, None] == jnp.arange(round_total, dtype=jnp.int32)[None, :]
    )
    hot_ids = jnp.sum(
        jnp.where(rank_match, jnp.arange(expert_count, dtype=jnp.int32)[:, None], 0), axis=0
    )
    match = expert_ids[:, :, None] == hot_ids[None, None, :]
    named = jnp.sum(match.astype(jnp.int32), axis=1)
    tok_rows = expert_ids.shape[0]
    earlier = (
        jnp.arange(tok_rows, dtype=jnp.int32)[None, :] < jnp.arange(tok_rows, dtype=jnp.int32)[:, None]
    ).astype(jnp.bfloat16)
    before = jnp.dot(earlier, named.astype(jnp.bfloat16), preferred_element_type=jnp.float32).astype(
        jnp.int32
    )
    per_rank = REPS * CAP
    target = per_rank * jnp.arange(round_total, dtype=jnp.int32)[None, :] + before
    return match, named, target


def local(tokens, grad_out, router_gates, expert_ids, slot_plan, w_gate, w_up, w_down):
    col_count = lax.axis_size("dev")
    node_count = lax.axis_size("node")
    tok_rows, model_width = tokens.shape
    round_total, chunk, node_hidden = w_gate.shape
    half = node_hidden // REPS
    per_rank = REPS * CAP
    row_slots = round_total * per_rank
    wide = model_width + LANE

    def split_cols(w):
        w = w.reshape(round_total, chunk, REPS, half)
        return jnp.swapaxes(w, 1, 2).reshape(col_count, chunk, half)

    send_wg = split_cols(w_gate)
    send_wu = split_cols(w_up)
    send_wd = split_cols(jnp.swapaxes(w_down, 1, 2))
    slot_gate = lax.all_to_all(send_wg, "dev", 0, 0, tiled=True).reshape(model_width, half)
    slot_up = lax.all_to_all(send_wu, "dev", 0, 0, tiled=True).reshape(model_width, half)
    slot_down_t = lax.all_to_all(send_wd, "dev", 0, 0, tiled=True).reshape(model_width, half)

    match, named, target = routing(expert_ids, slot_plan, col_count, round_total)
    q_ids = jnp.arange(row_slots, dtype=jnp.int32)
    chooser = (named[None, :, :] > 0) & (target[None, :, :] == q_ids[:, None, None])
    pick_rows = jnp.sum(chooser.astype(jnp.float32), axis=-1)
    pick_half = pick_rows.astype(jnp.bfloat16)
    gates_f = router_gates.astype(jnp.float32)
    rank_gate = jnp.sum(jnp.where(match, gates_f[:, :, None], 0.0), axis=1)
    gate_send = jnp.sum(jnp.where(chooser, rank_gate[None, :, :], 0.0), axis=(1, 2)).astype(jnp.bfloat16)

    x_send = jnp.dot(pick_half, tokens, preferred_element_type=jnp.float32).astype(jnp.bfloat16)
    dy_send = jnp.dot(pick_half, grad_out, preferred_element_type=jnp.float32).astype(jnp.bfloat16)
    gate_block = jnp.zeros((row_slots, LANE), jnp.bfloat16).at[:, 0].set(gate_send)
    dy_send = jnp.concatenate([dy_send, gate_block], axis=1)

    def to_cols(rows, width):
        rows = rows.reshape(round_total, 1, per_rank, width)
        rows = jnp.broadcast_to(rows, (round_total, REPS, per_rank, width))
        rows = rows.reshape(col_count, per_rank, width)
        got = lax.all_to_all(rows, "dev", 0, 0, tiled=True)
        return lax.all_gather(got.reshape(col_count * per_rank, width), "node", axis=0, tiled=True)

    x_rows = to_cols(x_send, model_width)
    dy_ext = to_cols(dy_send, wide)
    dy_rows = dy_ext[:, :model_width]
    gate_rows = dy_ext[:, model_width].astype(jnp.float32)[:, None]

    gate_pre = jnp.dot(x_rows, slot_gate, preferred_element_type=jnp.float32)
    up_pre = jnp.dot(x_rows, slot_up, preferred_element_type=jnp.float32)
    back_proj = jnp.dot(dy_rows, slot_down_t, preferred_element_type=jnp.float32)
    sigmoid_gate = jax.nn.sigmoid(gate_pre)
    active = gate_pre * sigmoid_gate
    hidden = active * up_pre
    scaled_back = gate_rows * back_proj
    d_gate = (scaled_back * up_pre * sigmoid_gate * (1.0 + gate_pre * (1.0 - sigmoid_gate))).astype(
        jnp.bfloat16
    )
    d_up = (scaled_back * active).astype(jnp.bfloat16)
    scaled_hidden = (gate_rows * hidden).astype(jnp.bfloat16)
    gate_terms = jnp.sum(back_proj * hidden, axis=-1)

    row_count = x_rows.shape[0]
    first_slot = (jnp.arange(row_count, dtype=jnp.int32) % REPS == 0)[:, None]

    def by_slot(d):
        zero = jnp.zeros((), d.dtype)
        return jnp.concatenate([jnp.where(first_slot, d, zero), jnp.where(first_slot, zero, d)], axis=1)

    def slot_pair_sum(rows, d):
        acc = jnp.einsum("rd,rh->dh", rows, by_slot(d), preferred_element_type=jnp.float32)
        acc = acc.astype(jnp.bfloat16).astype(jnp.float32)
        return (acc[:, :half] + acc[:, half:]).astype(jnp.bfloat16)

    grad_gate_cols = slot_pair_sum(x_rows, d_gate)
    grad_up_cols = slot_pair_sum(x_rows, d_up)
    grad_down_cols = slot_pair_sum(dy_rows, scaled_hidden)

    row_terms = jnp.einsum("rh,dh->rd", d_gate, slot_gate, preferred_element_type=jnp.float32)
    row_terms = row_terms + jnp.einsum("rh,dh->rd", d_up, slot_up, preferred_element_type=jnp.float32)
    term_block = jnp.zeros((row_count, LANE), jnp.float32).at[:, 0].set(gate_terms)
    row_ext = jnp.concatenate([row_terms, term_block], axis=1)

    summed = lax.psum_scatter(row_ext, "node", scatter_dimension=0, tiled=True)
    back = lax.all_to_all(summed.reshape(col_count, per_rank, wide), "dev", 0, 0, tiled=True)
    back = jnp.sum(back.reshape(round_total, REPS, per_rank, wide), axis=1).reshape(row_slots, wide)

    grad_tokens = jnp.einsum(
        "qt,qd->td",
        pick_rows,
        back[:, :model_width],
        precision=lax.Precision.HIGHEST,
    ).astype(jnp.bfloat16)
    back_q = back[:, model_width]
    rank_back = jnp.sum(jnp.where(chooser, back_q[:, None, None], 0.0), axis=0)
    grad_gates = jnp.sum(jnp.where(match, rank_back[:, None, :], 0.0), axis=-1)

    def home(cols):
        sent = cols.reshape(col_count, chunk, half)
        got = lax.all_to_all(sent, "dev", 0, 0, tiled=True)
        return jnp.swapaxes(got.reshape(round_total, REPS, chunk, half), 1, 2).reshape(
            round_total, chunk, node_hidden
        )

    grad_w_gate = home(grad_gate_cols)
    grad_w_up = home(grad_up_cols)
    grad_w_down = jnp.swapaxes(home(grad_down_cols), 1, 2)
    del node_count
    return (grad_tokens, grad_gates, grad_w_gate, grad_w_up, grad_w_down)


def solution(mesh):
    return jax.shard_map(
        local,
        mesh=mesh,
        in_specs=(
            P(("node", "dev"), None),
            P(("node", "dev"), None),
            P(("node", "dev"), None),
            P(("node", "dev"), None),
            P(),
            P(None, "dev", "node"),
            P(None, "dev", "node"),
            P(None, "node", "dev"),
        ),
        out_specs=(
            P(("node", "dev"), None),
            P(("node", "dev"), None),
            P(None, "dev", "node"),
            P(None, "dev", "node"),
            P(None, "node", "dev"),
        ),
        check_vma=False,
    )
```

time: 488 us -> 341 us (0.70)
  waiting for transfers between devices: 250 us -> 122 us
  blocking collectives: 104 us -> 42.1 us
  local copies, waits for them, and re-layouts: 13.5 us -> 41.4 us
  other arithmetic: 17.8 us -> 29.7 us
  matrix products: 51.1 us -> 57.1 us
  starting transfers between devices: 34.5 us -> 28.7 us
    all_to_all x8 -> x7, waiting for transfers between devices: 250 us -> 112 us  [the longest x3 53.1 us: home(): got = lax.all_to_all(sent, 'dev', 0, 0, tiled=True)]
    all_to_all x3 -> x2, blocking collectives: 79 us -> 42.1 us  [to_cols(): got = lax.all_to_all(rows, 'dev', 0, 0, tiled=True)]
    reshape x7 -> x10, local copies, waits for them, and re-layouts: 5.59 us -> 35.1 us  [the longest x3 15.8 us: home(): jnp.swapaxes(got.reshape(round_total, REPS, chunk, half), 1, 2)]
    unnamed x2 -> x0, blocking collectives: 25 us -> none
    reduce_sum x4 -> x2, other arithmetic: 13.8 us -> 0.74 us  [the longest x1 0.41 us: local(): jnp.sum(back.reshape(round_total, REPS, per_rank, wide), axis=1)]
    concatenate x0 -> x2, other arithmetic: none -> 11.6 us  [the longest x1 11.6 us: local(): row_ext = jnp.concatenate([row_terms, term_block], axis=1)]
    reduce_scatter x1, waiting for transfers between devices: 0.01 us -> 9.62 us  [local(): summed = lax.psum_scatter(row_ext, 'node', scatter_dimension=0, tiled=True)]
    all_to_all x8 -> x7, starting transfers between devices: 34.4 us -> 28.4 us  [the longest x3 11.9 us: home(): got = lax.all_to_all(sent, 'dev', 0, 0, tiled=True)]
  transfers between devices with their start and end apart: 11 -> 10, of which waited for: 8 -> 7; matrix products, arithmetic and copies ran while one was open for 10% -> 23% of each run, Pallas kernels for 0% -> 0%
where the time goes in v2:
time: 341 us; the launch traced here: 336 us
  waiting for transfers between devices  122 us (36%)
  matrix products  57.1 us (17%)
  blocking collectives  42.1 us (12%)
  local copies, waits for them, and re-layouts  41.4 us (12%)
  other arithmetic  29.7 us (9%)
  starting transfers between devices  28.7 us (8%)
  between operations  14.5 us (4%)
    all_to_all x3, waiting for transfers between devices, home(): got = lax.all_to_all(sent, 'dev', 0, 0, tiled=True)  53.1 us
    all_to_all x2, blocking collectives, to_cols(): got = lax.all_to_all(rows, 'dev', 0, 0, tiled=True)  42.1 us
    all_to_all x1, waiting for transfers between devices, local(): lax.all_to_all(send_wg, 'dev', 0, 0, tiled=True).reshape(model_width, half)  22.3 us
    all_to_all x1, waiting for transfers between devices, local(): lax.all_to_all(send_wu, 'dev', 0, 0, tiled=True).reshape(model_width, half)  22.2 us
    dot_general x3, matrix products, slot_pair_sum(): jnp.einsum('rd,rh->dh', rows, by_slot(d), preferred_element_type=jnp.floa...  16.1 us
    reshape x3, local copies, waits for them, and re-layouts, home(): jnp.swapaxes(got.reshape(round_total, REPS, chunk, half), 1, 2)  15.8 us
    all_to_all x1, waiting for transfers between devices, local(): lax.all_to_all(send_wd, 'dev', 0, 0, tiled=True).reshape(model_width, half)  14.8 us
    reshape x3, local copies, waits for them, and re-layouts, home(): got.reshape(round_total, REPS, chunk, half)  13.8 us
  transfers between devices with their start and end apart: 10, of which 7 were waited for; matrix products, arithmetic and copies ran while one was open for 23% of the time, Pallas kernels for 0%

profile of v2, /device:TPU:0, one launch (start us, length us, event | category | flops | bytes accessed | tf_op | source)
XLA Modules:
  0.0 335.7 jit_solution(6776212073196806073)
XLA Ops:
  14.6 23.7 %all_to_all.45 = bf16[16,4,7168]{2,1,0:T(4,128)(2,1)S(1)} all-to-all(bf16[16,4,7168]{2,1,0:T(4,128)(2,1)S(1)} %bitcast.61), channel_id=1, replica_groups=mesh['node'=8,'dev'=16] {'dev'}, dimensions={0} | all-to-all | bytes 1835008 | tf_op jit(solution)/shard_map/all_to_all | solution.py:75
  44.1 18.4 %all_to_all.46 = bf16[16,4,7296]{2,1,0:T(4,128)(2,1)S(1)} all-to-all(bf16[16,4,7296]{2,1,0:T(4,128)(2,1)S(1)} %bitcast.60), channel_id=1, replica_groups=mesh['node'=8,'dev'=16] {'dev'}, dimensions={0} | all-to-all | bytes 1867776 | tf_op jit(solution)/shard_map/all_to_all | solution.py:75
  65.5 3.7 %all-to-all-start.4 = ((bf16[16,448,128]{2,1,0:T(8,128)(2,1)}), bf16[16,448,128]{2,1,0:T(8,128)(2,1)S(1)}, u32[]{:S(2)}, u32[]{:S(2)}) async-start(bf16[16,448,128]{2,1,0:T(8,128)(2,1)} %bitcast.53), calls=%async_computation.4 | async-start | bytes 3670016 | tf_op jit(solution)/shard_map/all_to_all | solution.py:53
  72.2 22.3 %all-to-all-done.4 = bf16[16,448,128]{2,1,0:T(8,128)(2,1)S(1)} async-done(((bf16[16,448,128]{2,1,0:T(8,128)(2,1)}), bf16[16,448,128]{2,1,0:T(8,128)(2,1)S(1)}, u32[]{:S(2)}, u32[]{:S(2)}) %all-to-all-start.4) | async-done | bytes 1835040 | tf_op jit(solution)/shard_map/all_to_all | solution.py:53
  94.5 4.4 %all-to-all-start.3 = ((bf16[16,448,128]{2,1,0:T(8,128)(2,1)}), bf16[16,448,128]{2,1,0:T(8,128)(2,1)}, u32[]{:S(2)}, u32[]{:S(2)}) async-start(bf16[16,448,128]{2,1,0:T(8,128)(2,1)} %bitcast.52), calls=%async_computation.3 | async-start | bytes 3670016 | tf_op jit(solution)/shard_map/all_to_all | solution.py:54
  101.9 22.2 %all-to-all-done.3 = bf16[16,448,128]{2,1,0:T(8,128)(2,1)} async-done(((bf16[16,448,128]{2,1,0:T(8,128)(2,1)}), bf16[16,448,128]{2,1,0:T(8,128)(2,1)}, u32[]{:S(2)}, u32[]{:S(2)}) %all-to-all-start.3) | async-done | bytes 1835040 | tf_op jit(solution)/shard_map/all_to_all | solution.py:54
  124.1 4.4 %all-to-all-start.1 = ((bf16[16,448,128]{2,1,0:T(8,128)(2,1)}), bf16[16,448,128]{2,1,0:T(8,128)(2,1)}, u32[]{:S(2)}, u32[]{:S(2)}) async-start(bf16[16,448,128]{2,1,0:T(8,128)(2,1)} %bitcast.51), calls=%async_computation.1 | async-start | bytes 3670016 | tf_op jit(solution)/shard_map/all_to_all | solution.py:55
  128.8 5.8 %fusion.43 = f32[512,128]{0,1:T(8,128)S(1)} fusion(bf16[512,7168]{1,0:T(8,128)(2,1)} %all-gather.5.cloned.1.call-done, bf16[7168,128]{1,0:T(8,128)(2,1)S(1)} %bitcast.47), kind=kOutput, calls=%fused_computation.98 | convolution fusion | flops 939524096 | bytes 9437184 | tf_op jit(solution)/shard_map/dot_general | solution.py:83
  134.6 4.1 %fusion.42 = f32[512,128]{0,1:T(8,128)S(1)} fusion(bf16[512,7168]{1,0:T(8,128)(2,1)S(1)} %copy-done, bf16[7168,128]{1,0:T(8,128)(2,1)} %bitcast.9), kind=kOutput, calls=%fused_computation.97 | convolution fusion | flops 939524096 | bytes 9437184 | tf_op jit(solution)/shard_map/dot_general | solution.py:84
  138.7 14.8 %all-to-all-done.1 = bf16[16,448,128]{2,1,0:T(8,128)(2,1)} async-done(((bf16[16,448,128]{2,1,0:T(8,128)(2,1)}), bf16[16,448,128]{2,1,0:T(8,128)(2,1)}, u32[]{:S(2)}, u32[]{:S(2)}) %all-to-all-start.1) | async-done | bytes 1835040 | tf_op jit(solution)/shard_map/all_to_all | solution.py:55
  153.5 6.8 %multiply_reduce_fusion = (f32[512]{0:T(512)S(1)}, f32[512,128]{0,1:T(8,128)}) fusion(f32[512,128]{0,1:T(8,128)S(1)} %fusion.42, f32[512,128]{0,1:T(8,128)S(1)} %fusion.43, bf16[7168,128]{1,0:T(8,128)(2,1)} %bitcast.6, bf16[512,7296]{1,0:T(8,128)(2,1)} %all-gather.3.cloned.1.call-done), kind=kOutput, calls=%fused_computation.46 | convolution fusion | flops 939982336 | bytes 9963520 | tf_op jit(solution)/shard_map/dot_general | solution.py:85
  165.5 8.8 %convolution_add_fusion = f32[512,7168]{1,0:T(8,128)} fusion(f32[512,7168]{1,0:T(8,128)S(1)} %fusion.44, bf16[512,128]{0,1:T(8,128)(2,1)S(1)} %get-tuple-element.46, bf16[7168,128]{1,0:T(8,128)(2,1)} %bitcast.9), kind=kOutput, calls=%fused_computation.2 | convolution fusion | flops 943194112 | bytes 31326208 | tf_op jit(solution)/shard_map/rh,dh->rd/dot_general | solution.py:114
  174.3 11.6 %select_maximum_fusion = f32[512,7296]{1,0:T(8,128)} fusion(f32[512,1]{1,0:T(8,128)S(1)} %copy.38, f32[512,7168]{1,0:T(8,128)} %convolution_add_fusion), kind=kLoop, calls=%fused_computation | loop fusion | flops 11206656 | bytes 29624320 | tf_op jit(solution)/shard_map/concatenate | solution.py:116
  185.9 5.4 %fusion = f32[7168,256]{1,0:T(8,128)S(1)} fusion(bf16[512,7296]{1,0:T(8,128)(2,1)} %all-gather.3.cloned.1.call-done, bf16[512,128]{0,1:T(8,128)(2,1)S(1)} %get-tuple-element.49, bf16[512,128]{0,1:T(8,128)(2,1)S(1)} %get-tuple-element.31), kind=kOutput, calls=%fused_computation.4 | convolution fusion | flops 1883242496 | bytes 14942208 | tf_op jit(solution)/shard_map/rd,rh->dh/dot_general | solution.py:105
  193.0 3.7 %all-to-all-start.8 = ((bf16[16,448,128]{2,1,0:T(8,128)(2,1)}), bf16[16,448,128]{2,1,0:T(8,128)(2,1)S(1)}, u32[]{:S(2)}, u32[]{:S(2)}) async-start(bf16[16,448,128]{2,1,0:T(8,128)(2,1)} %bitcast.59), calls=%async_computation.9 | async-start | bytes 3670016 | tf_op jit(solution)/shard_map/all_to_all | solution.py:134
  196.7 5.3 %fusion.2 = f32[7168,256]{1,0:T(8,128)S(1)} fusion(bf16[512,7168]{1,0:T(8,128)(2,1)} %all-gather.5.cloned.1.call-done, bf16[512,128]{0,1:T(8,128)(2,1)S(1)} %get-tuple-element.50, bf16[512,128]{0,1:T(8,128)(2,1)S(1)} %get-tuple-element.43), kind=kOutput, calls=%fused_computation.8 | convolution fusion | flops 1883242496 | bytes 14942208 | tf_op jit(solution)/shard_map/rd,rh->dh/dot_general | solution.py:105
  203.6 19.4 %all-to-all-done.8 = bf16[16,448,128]{2,1,0:T(8,128)(2,1)S(1)} async-done(((bf16[16,448,128]{2,1,0:T(8,128)(2,1)}), bf16[16,448,128]{2,1,0:T(8,128)(2,1)S(1)}, u32[]{:S(2)}, u32[]{:S(2)}) %all-to-all-start.8) | async-done | bytes 1835040 | tf_op jit(solution)/shard_map/all_to_all | solution.py:134
  223.0 4.4 %all-to-all-start.6 = ((bf16[16,448,128]{2,1,0:T(8,128)(2,1)}), bf16[16,448,128]{2,1,0:T(8,128)(2,1)}, u32[]{:S(2)}, u32[]{:S(2)}) async-start(bf16[16,448,128]{2,1,0:T(8,128)(2,1)} %bitcast.57), calls=%async_computation.7 | async-start | bytes 3670016 | tf_op jit(solution)/shard_map/all_to_all | solution.py:134
  227.4 5.4 %fusion.1 = f32[7168,256]{1,0:T(8,128)S(1)} fusion(bf16[512,7168]{1,0:T(8,128)(2,1)} %all-gather.5.cloned.1.call-done, bf16[512,128]{0,1:T(8,128)(2,1)S(1)} %get-tuple-element.51, bf16[512,128]{0,1:T(8,128)(2,1)S(1)} %get-tuple-element.45), kind=kOutput, calls=%fused_computation.6 | convolution fusion | flops 1883242496 | bytes 14942208 | tf_op jit(solution)/shard_map/rd,rh->dh/dot_general | solution.py:105
  234.4 19.2 %all-to-all-done.6 = bf16[16,448,128]{2,1,0:T(8,128)(2,1)} async-done(((bf16[16,448,128]{2,1,0:T(8,128)(2,1)}), bf16[16,448,128]{2,1,0:T(8,128)(2,1)}, u32[]{:S(2)}, u32[]{:S(2)}) %all-to-all-start.6) | async-done | bytes 1835040 | tf_op jit(solution)/shard_map/all_to_all | solution.py:134
  253.6 3.7 %all-to-all-start.7 = ((bf16[16,448,128]{2,1,0:T(8,128)(2,1)}), bf16[16,448,128]{2,1,0:T(8,128)(2,1)S(1)}, u32[]{:S(2)}, u32[]{:S(2)}) async-start(bf16[16,448,128]{2,1,0:T(8,128)(2,1)} %bitcast.58), calls=%async_computation.8 | async-start | bytes 3670016 | tf_op jit(solution)/shard_map/all_to_all | solution.py:134
  257.3 9.6 %reduce-scatter.2.cloned.1.call-done = f32[64,7296]{1,0:T(8,128)} async-done(((f32[512,7296]{1,0:T(8,128)}), f32[64,7296]{1,0:T(8,128)}) %reduce-scatter.2.cloned.1.call-update) | async-done | bytes 1867792 | tf_op jit(solution)/shard_map/reduce_scatter | solution.py:118
  266.9 2.9 reshape.225
  269.8 14.6 %all-to-all-done.7 = bf16[16,448,128]{2,1,0:T(8,128)(2,1)S(1)} async-done(((bf16[16,448,128]{2,1,0:T(8,128)(2,1)}), bf16[16,448,128]{2,1,0:T(8,128)(2,1)S(1)}, u32[]{:S(2)}, u32[]{:S(2)}) %all-to-all-start.7) | async-done | bytes 1835040 | tf_op jit(solution)/shard_map/all_to_all | solution.py:134
  285.6 4.0 %all-to-all-start.5 = ((f32[16,4,7296]{2,1,0:T(4,128)}), f32[16,4,7296]{2,1,0:T(4,128)S(1)}, u32[]{:S(2)}, u32[]{:S(2)}) async-start(f32[16,4,7296]{2,1,0:T(4,128)} %reshape.225), calls=%async_computation.6 | async-start | bytes 3735552 | tf_op jit(solution)/shard_map/all_to_all | solution.py:119
  289.6 4.6 %copy.45 = bf16[8,2,448,128]{3,1,2,0:T(2,128)(2,1)} copy(bf16[8,2,448,128]{3,2,1,0:T(8,128)(2,1)} %bitcast.49) | data formatting | bytes 3670016 | tf_op jit(solution)/shard_map/reshape | solution.py:135
  294.2 5.3 %reshape.236 = bf16[8,448,256]{2,1,0:T(8,128)(2,1)} reshape(bf16[8,448,2,128]{3,2,1,0:T(2,128)(2,1)} %bitcast.54) | data formatting | bytes 3670016 | tf_op jit(solution)/shard_map/reshape | solution.py:135
  299.5 4.6 %copy.47 = bf16[8,2,448,128]{3,1,2,0:T(2,128)(2,1)} copy(bf16[8,2,448,128]{3,2,1,0:T(8,128)(2,1)} %bitcast.15) | data formatting | bytes 3670016 | tf_op jit(solution)/shard_map/reshape | solution.py:135
  304.1 5.3 %reshape.230 = bf16[8,448,256]{2,1,0:T(8,128)(2,1)} reshape(bf16[8,448,2,128]{3,2,1,0:T(2,128)(2,1)} %bitcast.55) | data formatting | bytes 3670016 | tf_op jit(solution)/shard_map/reshape | solution.py:135
  309.4 4.6 %copy.46 = bf16[8,2,448,128]{3,1,2,0:T(2,128)(2,1)} copy(bf16[8,2,448,128]{3,2,1,0:T(8,128)(2,1)} %bitcast.50) | data formatting | bytes 3670016 | tf_op jit(solution)/shard_map/reshape | solution.py:135
  314.0 5.3 %reshape.233 = bf16[8,448,256]{2,1,0:T(8,128)(2,1)} reshape(bf16[8,448,2,128]{3,2,1,0:T(2,128)(2,1)} %bitcast.56) | data formatting | bytes 3670016 | tf_op jit(solution)/shard_map/reshape | solution.py:135
  320.2 7.7 %convolution_convert_fusion.3 = bf16[256,7168]{1,0:T(8,128)(2,1)} fusion(f32[32,256]{1,0:T(8,128)S(1)} %get-tuple-element.30, f32[32,7296]{1,0:T(8,128)S(1)} %reshape.227), kind=kOutput, calls=%fused_computation.9 | convolution fusion | flops 706478080 | bytes 4620288 | tf_op jit(solution)/shard_map/qt,qd->td/dot_general | solution.py:122
  (66 shorter events, 35.1 us)
Async XLA Ops:
  7.2 121.6 %all-gather.5.cloned.1.call-start = ((), (), s32[]{:S(2)}) async-start(), calls=%async_computation.11 | async-start | bytes 8257536 | tf_op jit(solution)/shard_map/all_gather | solution.py:76
  39.5 114.0 %all-gather.3.cloned.1.call-start = ((), (), s32[]{:S(2)}) async-start(), calls=%async_computation.10 | async-start | bytes 8404992 | tf_op jit(solution)/shard_map/all_gather | solution.py:76
  43.8 19.9 %copy-start.3 = (bf16[8,448,256]{2,1,0:T(8,128)(2,1)S(1)}, bf16[8,448,256]{2,1,0:T(8,128)(2,1)}, u32[]{:S(2)}) copy-start(bf16[8,448,256]{2,1,0:T(8,128)(2,1)} %param.17) | copy-start | bytes 5505028
  65.5 29.0 %all-to-all-start.4 = ((bf16[16,448,128]{2,1,0:T(8,128)(2,1)}), bf16[16,448,128]{2,1,0:T(8,128)(2,1)S(1)}, u32[]{:S(2)}, u32[]{:S(2)}) async-start(bf16[16,448,128]{2,1,0:T(8,128)(2,1)} %bitcast.53), calls=%async_computation.4 | async-start | bytes 3670016 | tf_op jit(solution)/shard_map/all_to_all | solution.py:53
  94.5 29.6 %all-to-all-start.3 = ((bf16[16,448,128]{2,1,0:T(8,128)(2,1)}), bf16[16,448,128]{2,1,0:T(8,128)(2,1)}, u32[]{:S(2)}, u32[]{:S(2)}) async-start(bf16[16,448,128]{2,1,0:T(8,128)(2,1)} %bitcast.52), calls=%async_computation.3 | async-start | bytes 3670016 | tf_op jit(solution)/shard_map/all_to_all | solution.py:54
  124.1 29.5 %all-to-all-start.1 = ((bf16[16,448,128]{2,1,0:T(8,128)(2,1)}), bf16[16,448,128]{2,1,0:T(8,128)(2,1)}, u32[]{:S(2)}, u32[]{:S(2)}) async-start(bf16[16,448,128]{2,1,0:T(8,128)(2,1)} %bitcast.51), calls=%async_computation.1 | async-start | bytes 3670016 | tf_op jit(solution)/shard_map/all_to_all | solution.py:55
  128.5 138.4 %reduce-scatter.2.cloned.1.call-start = ((), (), s32[]{:S(2)}) async-start(), calls=%async_computation.12 | async-start | bytes 16809984 | tf_op jit(solution)/shard_map/reduce_scatter | solution.py:118
  128.8 5.9 %copy-start = (bf16[512,7168]{1,0:T(8,128)(2,1)S(1)}, bf16[512,7168]{1,0:T(8,128)(2,1)}, u32[]{:S(2)}) copy-start(bf16[512,7168]{1,0:T(8,128)(2,1)} %all-gather.5.cloned.1.call-done) | copy-start | bytes 22020100
  193.0 30.0 %all-to-all-start.8 = ((bf16[16,448,128]{2,1,0:T(8,128)(2,1)}), bf16[16,448,128]{2,1,0:T(8,128)(2,1)S(1)}, u32[]{:S(2)}, u32[]{:S(2)}) async-start(bf16[16,448,128]{2,1,0:T(8,128)(2,1)} %bitcast.59), calls=%async_computation.9 | async-start | bytes 3670016 | tf_op jit(solution)/shard_map/all_to_all | solution.py:134
  223.0 9.8 %copy-start.1 = (bf16[16,448,128]{2,1,0:T(8,128)(2,1)}, bf16[16,448,128]{2,1,0:T(8,128)(2,1)S(1)}, u32[]{:S(2)}) copy-start(bf16[16,448,128]{2,1,0:T(8,128)(2,1)S(1)} %all-to-all-done.8) | copy-start | bytes 5505028
  223.0 30.6 %all-to-all-start.6 = ((bf16[16,448,128]{2,1,0:T(8,128)(2,1)}), bf16[16,448,128]{2,1,0:T(8,128)(2,1)}, u32[]{:S(2)}, u32[]{:S(2)}) async-start(bf16[16,448,128]{2,1,0:T(8,128)(2,1)} %bitcast.57), calls=%async_computation.7 | async-start | bytes 3670016 | tf_op jit(solution)/shard_map/all_to_all | solution.py:134
  253.6 30.8 %all-to-all-start.7 = ((bf16[16,448,128]{2,1,0:T(8,128)(2,1)}), bf16[16,448,128]{2,1,0:T(8,128)(2,1)S(1)}, u32[]{:S(2)}, u32[]{:S(2)}) async-start(bf16[16,448,128]{2,1,0:T(8,128)(2,1)} %bitcast.58), calls=%async_computation.8 | async-start | bytes 3670016 | tf_op jit(solution)/shard_map/all_to_all | solution.py:134
  284.4 1.3 copy-start.2
  285.6 33.7 %all-to-all-start.5 = ((f32[16,4,7296]{2,1,0:T(4,128)}), f32[16,4,7296]{2,1,0:T(4,128)S(1)}, u32[]{:S(2)}, u32[]{:S(2)}) async-start(f32[16,4,7296]{2,1,0:T(4,128)} %reshape.225), calls=%async_computation.6 | async-start | bytes 3735552 | tf_op jit(solution)/shard_map/all_to_all | solution.py:119
  319.7 8.2 %copy-start.4 = (s32[256,8]{0,1:T(8,128)S(1)}, s32[256,8]{0,1:T(8,128)}, u32[]{:S(2)}) copy-start(s32[256,8]{0,1:T(8,128)} %param.15) | copy-start | bytes 24580
Sparse Core Ops, SparseCore 0:
  39.6 42.5 all-gather.4
  84.5 45.8 all-gather.2
  186.0 80.8 reduce-scatter.1

commit v3 on v2

--- a/solution.py
+++ b/solution.py
@@ -68,15 +68,14 @@
     gate_block = jnp.zeros((row_slots, LANE), jnp.bfloat16).at[:, 0].set(gate_send)
     dy_send = jnp.concatenate([dy_send, gate_block], axis=1)
 
-    def to_cols(rows, width):
-        rows = rows.reshape(round_total, 1, per_rank, width)
-        rows = jnp.broadcast_to(rows, (round_total, REPS, per_rank, width))
-        rows = rows.reshape(col_count, per_rank, width)
-        got = lax.all_to_all(rows, "dev", 0, 0, tiled=True)
-        return lax.all_gather(got.reshape(col_count * per_rank, width), "node", axis=0, tiled=True)
-
-    x_rows = to_cols(x_send, model_width)
-    dy_ext = to_cols(dy_send, wide)
+    both_send = jnp.concatenate([x_send, dy_send], axis=1)
+    both_width = model_width + wide
+    both = both_send.reshape(round_total, 1, per_rank, both_width)
+    both = jnp.broadcast_to(both, (round_total, REPS, per_rank, both_width))
+    both = lax.all_to_all(both.reshape(col_count, per_rank, both_width), "dev", 0, 0, tiled=True)
+    both = both.reshape(col_count * per_rank, both_width)
+    x_rows = lax.all_gather(both[:, :model_width], "node", axis=0, tiled=True)
+    dy_ext = lax.all_gather(both[:, model_width:], "node", axis=0, tiled=True)
     dy_rows = dy_ext[:, :model_width]
     gate_rows = dy_ext[:, model_width].astype(jnp.float32)[:, None]
 
@@ -103,17 +102,20 @@
 
     def slot_pair_sum(rows, d):
         acc = jnp.einsum("rd,rh->dh", rows, by_slot(d), preferred_element_type=jnp.float32)
-        acc = acc.astype(jnp.bfloat16).astype(jnp.float32)
+        acc = lax.reduce_precision(acc, exponent_bits=8, mantissa_bits=7)
         return (acc[:, :half] + acc[:, half:]).astype(jnp.bfloat16)
 
     grad_gate_cols = slot_pair_sum(x_rows, d_gate)
     grad_up_cols = slot_pair_sum(x_rows, d_up)
     grad_down_cols = slot_pair_sum(dy_rows, scaled_hidden)
 
-    row_terms = jnp.einsum("rh,dh->rd", d_gate, slot_gate, preferred_element_type=jnp.float32)
-    row_terms = row_terms + jnp.einsum("rh,dh->rd", d_up, slot_up, preferred_element_type=jnp.float32)
-    term_block = jnp.zeros((row_count, LANE), jnp.float32).at[:, 0].set(gate_terms)
-    row_ext = jnp.concatenate([row_terms, term_block], axis=1)
+    pad_rows = ((0, LANE), (0, 0))
+    row_ext = jnp.einsum("rh,dh->rd", d_gate, jnp.pad(slot_gate, pad_rows), preferred_element_type=jnp.float32)
+    row_ext = row_ext + jnp.einsum(
+        "rh,dh->rd", d_up, jnp.pad(slot_up, pad_rows), preferred_element_type=jnp.float32
+    )
+    term_col = jnp.arange(wide, dtype=jnp.int32)[None, :] == model_width
+    row_ext = row_ext + jnp.where(term_col, gate_terms[:, None], 0.0)
 
     summed = lax.psum_scatter(row_ext, "node", scatter_dimension=0, tiled=True)
     back = lax.all_to_all(summed.reshape(col_count, per_rank, wide), "dev", 0, 0, tiled=True)
@@ -131,14 +133,14 @@
 
     def home(cols):
         sent = cols.reshape(col_count, chunk, half)
-        got = lax.all_to_all(sent, "dev", 0, 0, tiled=True)
-        return jnp.swapaxes(got.reshape(round_total, REPS, chunk, half), 1, 2).reshape(
-            round_total, chunk, node_hidden
-        )
+        got = lax.all_to_all(sent, "dev", 0, 0, tiled=True).reshape(round_total, REPS, chunk, half)
+        return jnp.concatenate([got[:, h] for h in range(REPS)], axis=-1)
 
     grad_w_gate = home(grad_gate_cols)
     grad_w_up = home(grad_up_cols)
-    grad_w_down = jnp.swapaxes(home(grad_down_cols), 1, 2)
+    got_down = lax.all_to_all(grad_down_cols.reshape(col_count, chunk, half), "dev", 0, 0, tiled=True)
+    got_down = got_down.reshape(round_total, REPS, chunk, half)
+    grad_w_down = jnp.concatenate([jnp.swapaxes(got_down[:, h], 1, 2) for h in range(REPS)], axis=1)
     del node_count
     return (grad_tokens, grad_gates, grad_w_gate, grad_w_up, grad_w_down)
 

time: 341 us -> 325 us (0.953); the launches traced: 336 us -> 324 us
  waiting for transfers between devices: 122 us -> 149 us
  local copies, waits for them, and re-layouts: 41.4 us -> 18.8 us
  other arithmetic: 29.7 us -> 20.1 us
  blocking collectives: 42.1 us -> 33.8 us
    reshape x8 -> x1, local copies, waits for them, and re-layouts: 32 us -> 2.85 us  [local(): both = both.reshape(col_count * per_rank, both_width)]
    all_to_all x1, waiting for transfers between devices: 22.2 us -> 0.01 us  [local(): lax.all_to_all(send_wu, 'dev', 0, 0, tiled=True).reshape(model_width, half)]
    all_to_all x1, waiting for transfers between devices: 0.01 us -> 19.9 us  [local(): lax.all_to_all(summed.reshape(col_count, per_rank, wide), 'dev', 0, 0, ti...]
    all_gather x2, waiting for transfers between devices: 0.02 us -> 15.7 us  [the longest x1 15.7 us: local(): dy_ext = lax.all_gather(both[:, model_width:], 'node', axis=0, tiled=True)]
    all_to_all x1, waiting for transfers between devices: 14.8 us -> 23.1 us  [local(): lax.all_to_all(send_wd, 'dev', 0, 0, tiled=True).reshape(model_width, half)]
    all_to_all x2 -> x1, blocking collectives: 42.1 us -> 33.8 us  [local(): lax.all_to_all(both.reshape(col_count, per_rank, both_width), 'dev', 0, 0...]
    all_to_all x3, waiting for transfers between devices: 53.1 us -> 61 us  [the longest x2 38.8 us: home(): lax.all_to_all(sent, 'dev', 0, 0, tiled=True)]
    concatenate x2 -> x3, other arithmetic: 11.6 us -> 3.83 us  [the longest x1 2.34 us: home(): return jnp.concatenate([got[:, h] for h in range(REPS)], axis=-1)]
  transfers between devices with their start and end apart: 10 -> 10, of which waited for: 7 -> 8; matrix products, arithmetic and copies ran while one was open for 23% -> 17% of each run, Pallas kernels for 0% -> 0%
where the time goes in v3:
time: 325 us; the launch traced here: 324 us
  waiting for transfers between devices  149 us (46%)
  matrix products  56.2 us (17%)
  blocking collectives  33.8 us (10%)
  starting transfers between devices  32 us (10%)
  other arithmetic  20.1 us (6%)
  local copies, waits for them, and re-layouts  18.8 us (6%)
  between operations  14 us (4%)
    all_to_all x2, waiting for transfers between devices, home(): lax.all_to_all(sent, 'dev', 0, 0, tiled=True)  38.8 us
    all_to_all x1, blocking collectives, local(): lax.all_to_all(both.reshape(col_count, per_rank, both_width), 'dev', 0, 0...  33.8 us
    all_to_all x1, waiting for transfers between devices, local(): lax.all_to_all(send_wg, 'dev', 0, 0, tiled=True).reshape(model_width, half)  23.4 us
    all_to_all x1, waiting for transfers between devices, local(): lax.all_to_all(send_wd, 'dev', 0, 0, tiled=True).reshape(model_width, half)  23.1 us
    all_to_all x1, waiting for transfers between devices, local(): lax.all_to_all(grad_down_cols.reshape(col_count, chunk, half), 'dev', 0,...  22.3 us
    all_to_all x1, waiting for transfers between devices, local(): lax.all_to_all(summed.reshape(col_count, per_rank, wide), 'dev', 0, 0, ti...  19.9 us
    dot_general x3, matrix products, slot_pair_sum(): jnp.einsum('rd,rh->dh', rows, by_slot(d), preferred_element_type=jnp.floa...  15.9 us
    all_gather x1, waiting for transfers between devices, local(): dy_ext = lax.all_gather(both[:, model_width:], 'node', axis=0, tiled=True)  15.7 us
  transfers between devices with their start and end apart: 10, of which 8 were waited for; matrix products, arithmetic and copies ran while one was open for 17% of the time, Pallas kernels for 0%

profile of v3, /device:TPU:0, one launch (start us, length us, event | category | flops | bytes accessed | tf_op | source)
XLA Modules:
  0.0 323.7 jit_solution(1086430408114335553)
XLA Ops:
  12.8 2.9 convolution_convert_fusion.1
  17.5 33.8 %all_to_all.40 = bf16[16,4,14464]{2,1,0:T(4,128)(2,1)} all-to-all(bf16[16,4,14464]{2,1,0:T(4,128)(2,1)S(1)} %bitcast.57), channel_id=1, replica_groups=mesh['node'=8,'dev'=16] {'dev'}, dimensions={0} | all-to-all | bytes 3702784 | tf_op jit(solution)/shard_map/all_to_all | solution.py:75
  51.3 2.8 reshape.171
  59.2 3.7 %all-to-all-start.3 = ((bf16[16,448,128]{2,1,0:T(8,128)(2,1)}), bf16[16,448,128]{2,1,0:T(8,128)(2,1)S(1)}, u32[]{:S(2)}, u32[]{:S(2)}) async-start(bf16[16,448,128]{2,1,0:T(8,128)(2,1)} %bitcast.62), calls=%async_computation.3 | async-start | bytes 3670016 | tf_op jit(solution)/shard_map/all_to_all | solution.py:53
  62.9 1.8 fusion.41
  66.0 23.4 %all-to-all-done.3 = bf16[16,448,128]{2,1,0:T(8,128)(2,1)S(1)} async-done(((bf16[16,448,128]{2,1,0:T(8,128)(2,1)}), bf16[16,448,128]{2,1,0:T(8,128)(2,1)S(1)}, u32[]{:S(2)}, u32[]{:S(2)}) %all-to-all-start.3) | async-done | bytes 1835040 | tf_op jit(solution)/shard_map/all_to_all | solution.py:53
  89.5 4.4 %all-to-all-start.1 = ((bf16[16,448,128]{2,1,0:T(8,128)(2,1)}), bf16[16,448,128]{2,1,0:T(8,128)(2,1)}, u32[]{:S(2)}, u32[]{:S(2)}) async-start(bf16[16,448,128]{2,1,0:T(8,128)(2,1)} %bitcast.61), calls=%async_computation.1 | async-start | bytes 3670016 | tf_op jit(solution)/shard_map/all_to_all | solution.py:55
  93.9 1.6 fusion.42
  96.8 23.1 %all-to-all-done.1 = bf16[16,448,128]{2,1,0:T(8,128)(2,1)} async-done(((bf16[16,448,128]{2,1,0:T(8,128)(2,1)}), bf16[16,448,128]{2,1,0:T(8,128)(2,1)}, u32[]{:S(2)}, u32[]{:S(2)}) %all-to-all-start.1) | async-done | bytes 1835040 | tf_op jit(solution)/shard_map/all_to_all | solution.py:55
  120.0 4.4 %all-to-all-start.2 = ((bf16[16,448,128]{2,1,0:T(8,128)(2,1)}), bf16[16,448,128]{2,1,0:T(8,128)(2,1)}, u32[]{:S(2)}, u32[]{:S(2)}) async-start(bf16[16,448,128]{2,1,0:T(8,128)(2,1)} %bitcast.60), calls=%async_computation.2 | async-start | bytes 3670016 | tf_op jit(solution)/shard_map/all_to_all | solution.py:54
  124.7 5.8 %fusion.44 = f32[512,128]{0,1:T(8,128)S(1)} fusion(bf16[512,7168]{1,0:T(8,128)(2,1)} %all-gather.5.cloned.1.call-done, bf16[7168,128]{1,0:T(8,128)(2,1)S(1)} %bitcast.55), kind=kOutput, calls=%fused_computation.103 | convolution fusion | flops 939524096 | bytes 9437184 | tf_op jit(solution)/shard_map/dot_general | solution.py:82
  130.5 15.7 %all-gather.3.cloned.1.call-done = bf16[512,7296]{1,0:T(8,128)(2,1)} async-done(((bf16[64,7296]{1,0:T(8,128)(2,1)}), bf16[512,7296]{1,0:T(8,128)(2,1)}) %all-gather.3.cloned.1.call-update) | async-done | bytes 7471120 | tf_op jit(solution)/shard_map/all_gather | solution.py:78
  147.2 6.1 %fusion.1 = f32[512,128]{0,1:T(8,128)S(1)} fusion(bf16[7168,128]{1,0:T(8,128)(2,1)} %bitcast.6, bf16[512,7296]{1,0:T(8,128)(2,1)} %all-gather.3.cloned.1.call-done), kind=kOutput, calls=%fused_computation.8 | convolution fusion | flops 939524096 | bytes 9437184 | tf_op jit(solution)/shard_map/dot_general | solution.py:84
  153.3 6.2 %broadcast_select_fusion.1 = (bf16[512,128]{0,1:T(8,128)(2,1)S(1)}, bf16[512,128]{0,1:T(8,128)(2,1)S(1)}, bf16[512,128]{0,1:T(8,128)(2,1)S(1)}, bf16[512,128]{0,...) fusion(pred[512]{0:T(512)(128)(4,1)S(1)} %fusion.31, ...), kind=kOutput, calls=%fused_computation.61 | convolution fusion | flops 940834816 | bytes 10750464 | tf_op jit(solution)/shard_map/dot_general | solution.py:83
  159.6 2.1 fusion.7
  161.8 8.9 %select_add_fusion = f32[512,7296]{1,0:T(8,128)} fusion(f32[512,7296]{1,0:T(8,128)S(1)} %fusion.7, bf16[512,128]{0,1:T(8,128)(2,1)S(1)} %get-tuple-element.40, f32[512]{0:T(512)S(1)} %multiply_reduce_fusion, pred[7296]{0:T(1024)(128)(4,1)S(1)} %iota_compare_fusion.4, bf16[7168,128]{1,0:T(8,128)(2,1)} %bitcast.8), kind=kOutput, calls=%fused_computation | convolution fusion | flops 967507968 | bytes 31859840 | tf_op jit(solution)/shard_map/rh,dh->rd/dot_general | solution.py:114
  170.7 5.2 %convolution_reduce-precision_fusion = f32[7168,256]{1,0:T(8,128)S(1)} fusion(bf16[512,7296]{1,0:T(8,128)(2,1)} %all-gather.3.cloned.1.call-done, bf16[512,128]{0,1:T(8,128)(2,1)S(1)} %get-tuple-element.43, bf16[512,128]{0,1:T(8,128)(2,1)S(1)} %get-tuple-element.19), kind=kOutput, calls=%fused_computation.1 | convolution fusion | flops 1881407488 | bytes 14942208 | tf_op jit(solution)/shard_map/rd,rh->dh/dot_general | solution.py:104
  177.5 7.0 %all-to-all-start.7 = ((bf16[16,448,128]{2,1,0:T(8,128)(2,1)}), bf16[16,448,128]{2,1,0:T(8,128)(2,1)S(1)}, u32[]{:S(2)}, u32[]{:S(2)}) async-start(bf16[16,448,128]{2,1,0:T(8,128)(2,1)} %bitcast.65), calls=%async_computation.8 | async-start | bytes 3670016 | tf_op jit(solution)/shard_map/all_to_all | solution.py:141
  184.5 5.3 %convolution_reduce-precision_fusion.2 = f32[7168,256]{1,0:T(8,128)S(1)} fusion(bf16[512,7168]{1,0:T(8,128)(2,1)} %all-gather.5.cloned.1.call-done, bf16[512,128]{0,1:T(8,128)(2,1)S(1)} %get-tuple-element.44, bf16[512,128]{0,1:T(8,128)(2,1)S(1)} %get-tuple-element.37), kind=kOutput, calls=%fused_computation.3 | convolution fusion | flops 1881407488 | bytes 14942208 | tf_op jit(solution)/shard_map/rd,rh->dh/dot_general | solution.py:104
  191.4 22.3 %all-to-all-done.7 = bf16[16,448,128]{2,1,0:T(8,128)(2,1)S(1)} async-done(((bf16[16,448,128]{2,1,0:T(8,128)(2,1)}), bf16[16,448,128]{2,1,0:T(8,128)(2,1)S(1)}, u32[]{:S(2)}, u32[]{:S(2)}) %all-to-all-start.7) | async-done | bytes 1835040 | tf_op jit(solution)/shard_map/all_to_all | solution.py:141
  213.7 4.4 %all-to-all-start.5 = ((bf16[16,448,128]{2,1,0:T(8,128)(2,1)}), bf16[16,448,128]{2,1,0:T(8,128)(2,1)}, u32[]{:S(2)}, u32[]{:S(2)}) async-start(bf16[16,448,128]{2,1,0:T(8,128)(2,1)} %bitcast.63), calls=%async_computation.6 | async-start | bytes 3670016 | tf_op jit(solution)/shard_map/all_to_all | solution.py:136
  218.1 5.4 %convolution_reduce-precision_fusion.1 = f32[7168,256]{1,0:T(8,128)S(1)} fusion(bf16[512,7168]{1,0:T(8,128)(2,1)} %all-gather.5.cloned.1.call-done, bf16[512,128]{0,1:T(8,128)(2,1)S(1)} %get-tuple-element.45, bf16[512,128]{0,1:T(8,128)(2,1)S(1)} %get-tuple-element.39), kind=kOutput, calls=%fused_computation.2 | convolution fusion | flops 1881407488 | bytes 14942208 | tf_op jit(solution)/shard_map/rd,rh->dh/dot_general | solution.py:104
  225.1 20.3 %all-to-all-done.5 = bf16[16,448,128]{2,1,0:T(8,128)(2,1)} async-done(((bf16[16,448,128]{2,1,0:T(8,128)(2,1)}), bf16[16,448,128]{2,1,0:T(8,128)(2,1)}, u32[]{:S(2)}, u32[]{:S(2)}) %all-to-all-start.5) | async-done | bytes 1835040 | tf_op jit(solution)/shard_map/all_to_all | solution.py:136
  245.4 3.7 %all-to-all-start.6 = ((bf16[16,448,128]{2,1,0:T(8,128)(2,1)}), bf16[16,448,128]{2,1,0:T(8,128)(2,1)S(1)}, u32[]{:S(2)}, u32[]{:S(2)}) async-start(bf16[16,448,128]{2,1,0:T(8,128)(2,1)} %bitcast.64), calls=%async_computation.7 | async-start | bytes 3670016 | tf_op jit(solution)/shard_map/all_to_all | solution.py:136
  249.1 5.5 %reduce-scatter.2.cloned.1.call-done = f32[64,7296]{1,0:T(8,128)} async-done(((f32[512,7296]{1,0:T(8,128)}), f32[64,7296]{1,0:T(8,128)}) %reduce-scatter.2.cloned.1.call-update) | async-done | bytes 1867792 | tf_op jit(solution)/shard_map/reduce_scatter | solution.py:120
  254.6 2.9 reshape.178
  257.4 18.5 %all-to-all-done.6 = bf16[16,448,128]{2,1,0:T(8,128)(2,1)S(1)} async-done(((bf16[16,448,128]{2,1,0:T(8,128)(2,1)}), bf16[16,448,128]{2,1,0:T(8,128)(2,1)S(1)}, u32[]{:S(2)}, u32[]{:S(2)}) %all-to-all-start.6) | async-done | bytes 1835040 | tf_op jit(solution)/shard_map/all_to_all | solution.py:136
  277.2 4.0 %all-to-all-start.4 = ((f32[16,4,7296]{2,1,0:T(4,128)}), f32[16,4,7296]{2,1,0:T(4,128)S(1)}, u32[]{:S(2)}, u32[]{:S(2)}) async-start(f32[16,4,7296]{2,1,0:T(4,128)} %reshape.178), calls=%async_computation.5 | async-start | bytes 3735552 | tf_op jit(solution)/shard_map/all_to_all | solution.py:121
  281.1 1.6 slice_bitcast_fusion.1
  285.9 2.3 pad_maximum_fusion.3
  288.2 19.9 %all-to-all-done.4 = f32[16,4,7296]{2,1,0:T(4,128)S(1)} async-done(((f32[16,4,7296]{2,1,0:T(4,128)}), f32[16,4,7296]{2,1,0:T(4,128)S(1)}, u32[]{:S(2)}, u32[]{:S(2)}) %all-to-all-start.4) | async-done | bytes 1867808 | tf_op jit(solution)/shard_map/all_to_all | solution.py:121
  309.0 7.4 %convolution_convert_fusion = bf16[256,7168]{1,0:T(8,128)(2,1)} fusion(f32[32,256]{1,0:T(8,128)S(1)} %get-tuple-element.18, f32[32,7296]{1,0:T(8,128)S(1)} %reshape.180), kind=kOutput, calls=%fused_computation.4 | convolution fusion | flops 706478080 | bytes 4620288 | tf_op jit(solution)/shard_map/qt,qd->td/dot_general | solution.py:124
  (61 shorter events, 27.2 us)
Async XLA Ops:
  7.2 117.5 %all-gather.5.cloned.1.call-start = ((), (), s32[]{:S(2)}) async-start(), calls=%async_computation.10 | async-start | bytes 8257536 | tf_op jit(solution)/shard_map/all_gather | solution.py:77
  12.8 3.1 copy-start.3
  55.2 91.0 %all-gather.3.cloned.1.call-start = ((), (), s32[]{:S(2)}) async-start(), calls=%async_computation.9 | async-start | bytes 8404992 | tf_op jit(solution)/shard_map/all_gather | solution.py:78
  59.2 30.3 %all-to-all-start.3 = ((bf16[16,448,128]{2,1,0:T(8,128)(2,1)}), bf16[16,448,128]{2,1,0:T(8,128)(2,1)S(1)}, u32[]{:S(2)}, u32[]{:S(2)}) async-start(bf16[16,448,128]{2,1,0:T(8,128)(2,1)} %bitcast.62), calls=%async_computation.3 | async-start | bytes 3670016 | tf_op jit(solution)/shard_map/all_to_all | solution.py:53
  89.5 30.5 %all-to-all-start.1 = ((bf16[16,448,128]{2,1,0:T(8,128)(2,1)}), bf16[16,448,128]{2,1,0:T(8,128)(2,1)}, u32[]{:S(2)}, u32[]{:S(2)}) async-start(bf16[16,448,128]{2,1,0:T(8,128)(2,1)} %bitcast.61), calls=%async_computation.1 | async-start | bytes 3670016 | tf_op jit(solution)/shard_map/all_to_all | solution.py:55
  120.0 33.3 %all-to-all-start.2 = ((bf16[16,448,128]{2,1,0:T(8,128)(2,1)}), bf16[16,448,128]{2,1,0:T(8,128)(2,1)}, u32[]{:S(2)}, u32[]{:S(2)}) async-start(bf16[16,448,128]{2,1,0:T(8,128)(2,1)} %bitcast.60), calls=%async_computation.2 | async-start | bytes 3670016 | tf_op jit(solution)/shard_map/all_to_all | solution.py:54
  124.4 130.2 %reduce-scatter.2.cloned.1.call-start = ((), (), s32[]{:S(2)}) async-start(), calls=%async_computation.11 | async-start | bytes 16809984 | tf_op jit(solution)/shard_map/reduce_scatter | solution.py:120
  177.5 36.2 %all-to-all-start.7 = ((bf16[16,448,128]{2,1,0:T(8,128)(2,1)}), bf16[16,448,128]{2,1,0:T(8,128)(2,1)S(1)}, u32[]{:S(2)}, u32[]{:S(2)}) async-start(bf16[16,448,128]{2,1,0:T(8,128)(2,1)} %bitcast.65), calls=%async_computation.8 | async-start | bytes 3670016 | tf_op jit(solution)/shard_map/all_to_all | solution.py:141
  213.7 9.8 %copy-start = (bf16[16,448,128]{2,1,0:T(8,128)(2,1)}, bf16[16,448,128]{2,1,0:T(8,128)(2,1)S(1)}, u32[]{:S(2)}) copy-start(bf16[16,448,128]{2,1,0:T(8,128)(2,1)S(1)} %all-to-all-done.7) | copy-start | bytes 5505028
  213.7 31.7 %all-to-all-start.5 = ((bf16[16,448,128]{2,1,0:T(8,128)(2,1)}), bf16[16,448,128]{2,1,0:T(8,128)(2,1)}, u32[]{:S(2)}, u32[]{:S(2)}) async-start(bf16[16,448,128]{2,1,0:T(8,128)(2,1)} %bitcast.63), calls=%async_computation.6 | async-start | bytes 3670016 | tf_op jit(solution)/shard_map/all_to_all | solution.py:136
  245.4 30.5 %all-to-all-start.6 = ((bf16[16,448,128]{2,1,0:T(8,128)(2,1)}), bf16[16,448,128]{2,1,0:T(8,128)(2,1)S(1)}, u32[]{:S(2)}, u32[]{:S(2)}) async-start(bf16[16,448,128]{2,1,0:T(8,128)(2,1)} %bitcast.64), calls=%async_computation.7 | async-start | bytes 3670016 | tf_op jit(solution)/shard_map/all_to_all | solution.py:136
  275.9 1.2 copy-start.1
  277.2 31.0 %all-to-all-start.4 = ((f32[16,4,7296]{2,1,0:T(4,128)}), f32[16,4,7296]{2,1,0:T(4,128)S(1)}, u32[]{:S(2)}, u32[]{:S(2)}) async-start(f32[16,4,7296]{2,1,0:T(4,128)} %reshape.178), calls=%async_computation.5 | async-start | bytes 3735552 | tf_op jit(solution)/shard_map/all_to_all | solution.py:121
  282.7 3.0 copy-start.2
  308.6 7.9 %copy-start.4 = (s32[256,8]{0,1:T(8,128)S(1)}, s32[256,8]{0,1:T(8,128)}, u32[]{:S(2)}) copy-start(s32[256,8]{0,1:T(8,128)} %param.13) | copy-start | bytes 24580
Sparse Core Ops, SparseCore 0:
  55.3 42.6 all-gather.4
  100.2 45.8 all-gather.2
  170.8 83.7 reduce-scatter.1

commit v4 on v3

--- a/solution.py
+++ b/solution.py
@@ -47,12 +47,13 @@
         w = w.reshape(round_total, chunk, REPS, half)
         return jnp.swapaxes(w, 1, 2).reshape(col_count, chunk, half)
 
-    send_wg = split_cols(w_gate)
-    send_wu = split_cols(w_up)
-    send_wd = split_cols(jnp.swapaxes(w_down, 1, 2))
-    slot_gate = lax.all_to_all(send_wg, "dev", 0, 0, tiled=True).reshape(model_width, half)
-    slot_up = lax.all_to_all(send_wu, "dev", 0, 0, tiled=True).reshape(model_width, half)
-    slot_down_t = lax.all_to_all(send_wd, "dev", 0, 0, tiled=True).reshape(model_width, half)
+    send_w = jnp.concatenate(
+        [split_cols(w_gate), split_cols(w_up), split_cols(jnp.swapaxes(w_down, 1, 2))], axis=1
+    )
+    got_w = lax.all_to_all(send_w, "dev", 0, 0, tiled=True).reshape(col_count, 3, chunk, half)
+    slot_gate = got_w[:, 0].reshape(model_width, half)
+    slot_up = got_w[:, 1].reshape(model_width, half)
+    slot_down_t = got_w[:, 2].reshape(model_width, half)
 
     match, named, target = routing(expert_ids, slot_plan, col_count, round_total)
     q_ids = jnp.arange(row_slots, dtype=jnp.int32)
@@ -125,22 +126,19 @@
         "qt,qd->td",
         pick_rows,
         back[:, :model_width],
-        precision=lax.Precision.HIGHEST,
+        precision=lax.Precision.HIGH,
     ).astype(jnp.bfloat16)
     back_q = back[:, model_width]
     rank_back = jnp.sum(jnp.where(chooser, back_q[:, None, None], 0.0), axis=0)
     grad_gates = jnp.sum(jnp.where(match, rank_back[:, None, :], 0.0), axis=-1)
 
-    def home(cols):
-        sent = cols.reshape(col_count, chunk, half)
-        got = lax.all_to_all(sent, "dev", 0, 0, tiled=True).reshape(round_total, REPS, chunk, half)
-        return jnp.concatenate([got[:, h] for h in range(REPS)], axis=-1)
-
-    grad_w_gate = home(grad_gate_cols)
-    grad_w_up = home(grad_up_cols)
-    got_down = lax.all_to_all(grad_down_cols.reshape(col_count, chunk, half), "dev", 0, 0, tiled=True)
-    got_down = got_down.reshape(round_total, REPS, chunk, half)
-    grad_w_down = jnp.concatenate([jnp.swapaxes(got_down[:, h], 1, 2) for h in range(REPS)], axis=1)
+    cols = jnp.concatenate(
+        [c.reshape(col_count, chunk, half) for c in (grad_gate_cols, grad_up_cols, grad_down_cols)], axis=1
+    )
+    got = lax.all_to_all(cols, "dev", 0, 0, tiled=True).reshape(round_total, REPS, 3, chunk, half)
+    grad_w_gate = jnp.concatenate([got[:, h, 0] for h in range(REPS)], axis=-1)
+    grad_w_up = jnp.concatenate([got[:, h, 1] for h in range(REPS)], axis=-1)
+    grad_w_down = jnp.concatenate([jnp.swapaxes(got[:, h, 2], 1, 2) for h in range(REPS)], axis=1)
     del node_count
     return (grad_tokens, grad_gates, grad_w_gate, grad_w_up, grad_w_down)
 

time: 325 us -> 332 us (1.022)
  waiting for transfers between devices: 149 us -> 173 us
  starting transfers between devices: 32 us -> 15.4 us
  matrix products: 56.2 us -> 46.6 us
  other arithmetic: 20.1 us -> 25.6 us
    reduce_scatter x1, waiting for transfers between devices: 5.47 us -> 55.6 us  [local(): summed = lax.psum_scatter(row_ext, 'node', scatter_dimension=0, tiled=True)]
    all_to_all x6 -> x2, starting transfers between devices: 27.7 us -> 10.2 us  [the longest x1 5.63 us: local(): lax.all_to_all(cols, 'dev', 0, 0, tiled=True)]
    all_gather x1, waiting for transfers between devices: 15.7 us -> 0.02 us  [local(): dy_ext = lax.all_gather(both[:, model_width:], 'node', axis=0, tiled=True)]
    concatenate x2 -> x4, other arithmetic: 3.77 us -> 15 us  [the longest x1 5.64 us: local(): jnp.concatenate([c.reshape(col_count, chunk, half) for c in (grad_gate_co...]
    all_to_all x6 -> x2, waiting for transfers between devices: 108 us -> 99.4 us  [the longest x1 79.9 us: local(): lax.all_to_all(send_w, 'dev', 0, 0, tiled=True)]
    slice x0 -> x1, local copies, waits for them, and re-layouts: none -> 5.18 us  [local(): slot_down_t = got_w[:, 2].reshape(model_width, half)]
    convert_element_type x3, other arithmetic: 4.76 us -> 1.07 us  [slot_pair_sum(): return (acc[:, :half] + acc[:, half:]).astype(jnp.bfloat16)]
    another operation x7, other arithmetic: 5.68 us -> 2.01 us
  transfers between devices with their start and end apart: 10 -> 6, of which waited for: 8 -> 4; matrix products, arithmetic and copies ran while one was open for 17% -> 16% of each run, Pallas kernels for 0% -> 0%
where the time goes in v4:
time: 332 us; the launch traced here: 331 us
  waiting for transfers between devices  173 us (52%)
  matrix products  46.6 us (14%)
  blocking collectives  33.8 us (10%)
  other arithmetic  25.6 us (8%)
  local copies, waits for them, and re-layouts  22.1 us (7%)
  starting transfers between devices  15.4 us (5%)
  between operations  14.2 us (4%)
    all_to_all x1, waiting for transfers between devices, local(): lax.all_to_all(send_w, 'dev', 0, 0, tiled=True)  79.9 us
    reduce_scatter x1, waiting for transfers between devices, local(): summed = lax.psum_scatter(row_ext, 'node', scatter_dimension=0, tiled=True)  55.6 us
    all_to_all x1, blocking collectives, local(): lax.all_to_all(both.reshape(col_count, per_rank, both_width), 'dev', 0, 0...  33.8 us
    all_to_all x1, waiting for transfers between devices, local(): lax.all_to_all(cols, 'dev', 0, 0, tiled=True)  19.5 us
    all_to_all x1, waiting for transfers between devices, local(): lax.all_to_all(summed.reshape(col_count, per_rank, wide), 'dev', 0, 0, ti...  18.3 us
    dot_general x3, matrix products, slot_pair_sum(): jnp.einsum('rd,rh->dh', rows, by_slot(d), preferred_element_type=jnp.floa...  12.8 us
    dot_general x1, matrix products, local(): jnp.einsum('rh,dh->rd', d_up, jnp.pad(slot_up, pad_rows), preferred_eleme...  7.42 us
  transfers between devices with their start and end apart: 6, of which 4 were waited for; matrix products, arithmetic and copies ran while one was open for 16% of the time, Pallas kernels for 0%

profile of v4, /device:TPU:0, one launch (start us, length us, event | category | flops | bytes accessed | tf_op | source)
XLA Modules:
  0.0 331.1 jit_solution(3431668949597468028)
XLA Ops:
  12.9 2.9 convolution_convert_fusion.1
  17.5 33.8 %all_to_all.20 = bf16[16,4,14464]{2,1,0:T(4,128)(2,1)} all-to-all(bf16[16,4,14464]{2,1,0:T(4,128)(2,1)S(1)} %bitcast.62), channel_id=1, replica_groups=mesh['node'=8,'dev'=16] {'dev'}, dimensions={0} | all-to-all | bytes 3702784 | tf_op jit(solution)/shard_map/all_to_all | solution.py:76
  51.3 2.8 reshape.159
  54.2 1.0 slice.141
  55.2 1.0 slice.135
  56.3 1.7 fusion.42
  58.9 0.9 copy-done.5
  60.4 5.6 %pad_maximum_fusion = bf16[16,1344,128]{2,1,0:T(8,128)(2,1)} fusion(bf16[16,448,128]{2,1,0:T(8,128)(2,1)S(1)} %bitcast.65, bf16[16,448,128]{2,1,0:T(8,128)(2,1)S(1)} %bitcast.64, bf16[16,448,128]{2,1,0:T(8,128)(2,1)S(1)} %bitcast.63), kind=kLoop, calls=%fused_computation.10 | loop fusion | flops 16515072 | bytes 11010048 | tf_op jit(solution)/shard_map/concatenate | solution.py:50
  66.0 4.6 %all-to-all-start.1 = ((bf16[16,1344,128]{2,1,0:T(8,128)(2,1)}), bf16[16,1344,128]{2,1,0:T(8,128)(2,1)}, u32[]{:S(2)}, u32[]{:S(2)}) async-start(bf16[16,1344,128]{2,1,0:T(8,128)(2,1)} %pad_maximum_fusion), calls=%async_computation.1 | async-start | bytes 11010048 | tf_op jit(solution)/shard_map/all_to_all | solution.py:53
  71.4 79.9 %all-to-all-done.1 = bf16[16,1344,128]{2,1,0:T(8,128)(2,1)} async-done(((bf16[16,1344,128]{2,1,0:T(8,128)(2,1)}), bf16[16,1344,128]{2,1,0:T(8,128)(2,1)}, u32[]{:S(2)}, u32[]{:S(2)}) %all-to-all-start.1) | async-done | bytes 5505056 | tf_op jit(solution)/shard_map/all_to_all | solution.py:53
  151.2 5.2 %fusion.41 = (bf16[16,1,448,128]{3,2,1,0:T(8,128)(2,1)}, bf16[16,1,448,128]{3,2,1,0:T(8,128)(2,1)}, bf16[16,1,448,128]{3,2,1,0:T(8,128)(2,1)}) fusion(bf16[16,3,448,128]{3,2,1,0:T(8,128)(2,1)} %bitcast.8), kind=kLoop, calls=%fused_computation.102 | loop fusion | bytes 11010048 | tf_op jit(solution)/shard_map/slice | solution.py:56
  156.4 6.3 %fusion.45 = f32[512,128]{0,1:T(8,128)S(1)} fusion(bf16[512,7168]{1,0:T(8,128)(2,1)} %all-gather.5.cloned.1.call-done, bf16[7168,128]{1,0:T(8,128)(2,1)} %bitcast.60), kind=kOutput, calls=%fused_computation.106 | convolution fusion | flops 939524096 | bytes 9437184 | tf_op jit(solution)/shard_map/dot_general | solution.py:83
  162.7 1.0 convert_reduce_fusion
  163.8 6.3 %fusion.1 = f32[512,128]{0,1:T(8,128)S(1)} fusion(bf16[7168,128]{1,0:T(8,128)(2,1)} %bitcast.70, bf16[512,7296]{1,0:T(8,128)(2,1)} %all-gather.3.cloned.1.call-done), kind=kOutput, calls=%fused_computation.8 | convolution fusion | flops 939524096 | bytes 9437184 | tf_op jit(solution)/shard_map/dot_general | solution.py:85
  170.1 3.4 %broadcast_select_fusion.1 = (bf16[512,128]{0,1:T(8,128)(2,1)}, bf16[512,128]{0,1:T(8,128)(2,1)}, bf16[512,128]{0,1:T(8,128)(2,1)}, bf16[512,128]{0,1:T(8,128)(2...) fusion(pred[512]{0:T(512)(128)(4,1)S(1)} %copy-done.16, ...), kind=kOutput, calls=%fused_computation.63 | convolution fusion | flops 940834816 | bytes 10750464 | tf_op jit(solution)/shard_map/dot_general | solution.py:84
  173.7 2.1 fusion.7
  175.8 7.4 %select_add_fusion = f32[512,7296]{1,0:T(8,128)} fusion(f32[512,7296]{1,0:T(8,128)S(1)} %fusion.7, bf16[512,128]{0,1:T(8,128)(2,1)S(1)} %get-tuple-element.43, f32[512]{0:T(512)S(1)} %multiply_reduce_fusion, pred[7296]{0:T(1024)(128)(4,1)S(1)} %iota_compare_fusion.4, bf16[7168,128]{1,0:T(8,128)(2,1)S(1)} %bitcast.59), kind=kOutput, calls=%fused_computation | convolution fusion | flops 967507968 | bytes 31859840 | tf_op jit(solution)/shard_map/rh,dh->rd/dot_general | solution.py:115
  184.1 1.1 broadcast_select_fusion.4
  185.3 5.4 %convolution_reduce-precision_fusion.2 = f32[7168,256]{1,0:T(8,128)S(1)} fusion(bf16[512,7168]{1,0:T(8,128)(2,1)} %all-gather.5.cloned.1.call-done, bf16[512,128]{0,1:T(8,128)(2,1)S(1)} %get-tuple-element.46, bf16[512,128]{0,1:T(8,128)(2,1)S(1)} %copy-done.9), kind=kOutput, calls=%fused_computation.3 | convolution fusion | flops 1881407488 | bytes 14942208 | tf_op jit(solution)/shard_map/rd,rh->dh/dot_general | solution.py:105
  190.7 2.1 convolution_reduce-precision_fusion.1
  192.8 5.3 %convolution_reduce-precision_fusion = f32[7168,256]{1,0:T(8,128)S(1)} fusion(bf16[512,7296]{1,0:T(8,128)(2,1)} %all-gather.3.cloned.1.call-done, bf16[512,128]{0,1:T(8,128)(2,1)S(1)} %get-tuple-element.48, bf16[512,128]{0,1:T(8,128)(2,1)S(1)} %copy-done.12), kind=kOutput, calls=%fused_computation.1 | convolution fusion | flops 1881407488 | bytes 14942208 | tf_op jit(solution)/shard_map/rd,rh->dh/dot_general | solution.py:105
  199.2 5.6 %pad_maximum_fusion.1 = bf16[16,1344,128]{2,1,0:T(8,128)(2,1)} fusion(bf16[16,448,128]{2,1,0:T(8,128)(2,1)S(1)} %bitcast.66, bf16[16,448,128]{2,1,0:T(8,128)(2,1)S(1)} %bitcast.68, bf16[16,448,128]{2,1,0:T(8,128)(2,1)S(1)} %bitcast.67), kind=kLoop, calls=%fused_computation.11 | loop fusion | flops 16515072 | bytes 11010048 | tf_op jit(solution)/shard_map/concatenate | solution.py:135
  204.9 5.6 %all-to-all-start.3 = ((bf16[16,1344,128]{2,1,0:T(8,128)(2,1)}), bf16[16,1344,128]{2,1,0:T(8,128)(2,1)}, u32[]{:S(2)}, u32[]{:S(2)}) async-start(bf16[16,1344,128]{2,1,0:T(8,128)(2,1)} %pad_maximum_fusion.1), calls=%async_computation.4 | async-start | bytes 11010048 | tf_op jit(solution)/shard_map/all_to_all | solution.py:138
  210.5 55.6 %reduce-scatter.2.cloned.1.call-done = f32[64,7296]{1,0:T(8,128)} async-done(((f32[512,7296]{1,0:T(8,128)}), f32[64,7296]{1,0:T(8,128)}) %reduce-scatter.2.cloned.1.call-update) | async-done | bytes 1867792 | tf_op jit(solution)/shard_map/reduce_scatter | solution.py:121
  266.1 2.9 reshape.164
  268.9 19.5 %all-to-all-done.3 = bf16[16,1344,128]{2,1,0:T(8,128)(2,1)} async-done(((bf16[16,1344,128]{2,1,0:T(8,128)(2,1)}), bf16[16,1344,128]{2,1,0:T(8,128)(2,1)}, u32[]{:S(2)}, u32[]{:S(2)}) %all-to-all-start.3) | async-done | bytes 5505056 | tf_op jit(solution)/shard_map/all_to_all | solution.py:138
  288.4 4.9 %all-to-all-start.2 = ((f32[16,4,7296]{2,1,0:T(4,128)}), f32[16,4,7296]{2,1,0:T(4,128)S(1)}, u32[]{:S(2)}, u32[]{:S(2)}) async-start(f32[16,4,7296]{2,1,0:T(4,128)} %reshape.164), calls=%async_computation.3 | async-start | bytes 3735552 | tf_op jit(solution)/shard_map/all_to_all | solution.py:122
  293.3 2.9 slice_bitcast_fusion.1
  296.3 1.4 pad_maximum_fusion.7
  297.7 2.3 pad_maximum_fusion.5
  300.0 18.3 %all-to-all-done.2 = f32[16,4,7296]{2,1,0:T(4,128)S(1)} async-done(((f32[16,4,7296]{2,1,0:T(4,128)}), f32[16,4,7296]{2,1,0:T(4,128)S(1)}, u32[]{:S(2)}, u32[]{:S(2)}) %all-to-all-start.2) | async-done | bytes 1867808 | tf_op jit(solution)/shard_map/all_to_all | solution.py:122
  319.2 4.5 %convolution_convert_fusion = bf16[256,7168]{1,0:T(8,128)(2,1)} fusion(f32[32,256]{1,0:T(8,128)S(1)} %copy-done.11, f32[32,7296]{1,0:T(8,128)S(1)} %reshape.166), kind=kOutput, calls=%fused_computation.4 | convolution fusion | flops 354156544 | bytes 4620288 | tf_op jit(solution)/shard_map/qt,qd->td/dot_general | solution.py:125
  (94 shorter events, 13.5 us)
Async XLA Ops:
  7.2 149.2 %all-gather.5.cloned.1.call-start = ((), (), s32[]{:S(2)}) async-start(), calls=%async_computation.6 | async-start | bytes 8257536 | tf_op jit(solution)/shard_map/all_gather | solution.py:78
  9.3 6.5 %copy-start.18 = (s32[8]{0:T(128)}, s32[8]{0:T(128)S(1)}, u32[]{:S(2)}) copy-start(s32[8]{0:T(128)S(1)} %select_reduce_fusion.2) | copy-start | bytes 100
  10.1 5.7 %copy-start.14 = (pred[256,8]{0,1:T(8,128)(4,1)}, pred[256,8]{0,1:T(8,128)(4,1)S(1)}, u32[]{:S(2)}) copy-start(pred[256,8]{0,1:T(8,128)(4,1)S(1)} %broadcast_compare_fusion) | copy-start | bytes 6148
  12.1 3.7 %copy-start.10 = (f32[32,256]{1,0:T(8,128)}, f32[32,256]{1,0:T(8,128)S(1)}, u32[]{:S(2)}) copy-start(f32[32,256]{1,0:T(8,128)S(1)} %get-tuple-element.18) | copy-start | bytes 98308
  12.8 3.1 copy-start.3
  55.2 107.5 %all-gather.3.cloned.1.call-start = ((), (), s32[]{:S(2)}) async-start(), calls=%async_computation.5 | async-start | bytes 8404992 | tf_op jit(solution)/shard_map/all_gather | solution.py:79
  56.3 2.1 copy-start.4
  58.3 1.5 copy-start.5
  66.0 85.2 %all-to-all-start.1 = ((bf16[16,1344,128]{2,1,0:T(8,128)(2,1)}), bf16[16,1344,128]{2,1,0:T(8,128)(2,1)}, u32[]{:S(2)}, u32[]{:S(2)}) async-start(bf16[16,1344,128]{2,1,0:T(8,128)(2,1)} %pad_maximum_fusion), calls=%async_computation.1 | async-start | bytes 11010048 | tf_op jit(solution)/shard_map/all_to_all | solution.py:53
  70.6 195.5 %reduce-scatter.2.cloned.1.call-start = ((), (), s32[]{:S(2)}) async-start(), calls=%async_computation.7 | async-start | bytes 16809984 | tf_op jit(solution)/shard_map/reduce_scatter | solution.py:121
  156.4 13.6 %slice-start = ((s8[7340032]{0:T(1024)(128)(4,1)}), s8[3145728]{0:T(1024)(128)(4,1)S(1)}, s32[]{:S(2)}) async-start(s8[7340032]{0:T(1024)(128)(4,1)} %bitcast.54), calls=%async_computation.8 | async-start | bytes 6291456
  163.7 6.3 %slice-start.1 = ((s8[7340032]{0:T(1024)(128)(4,1)}), s8[4194304]{0:T(1024)(128)(4,1)S(1)}, s32[]{:S(2)}) async-start(s8[7340032]{0:T(1024)(128)(4,1)} %bitcast.54), calls=%async_computation.9 | async-start | bytes 8388608
  163.7 6.3 %copy-start = (bf16[16,1,448,128]{3,2,1,0:T(8,128)(2,1)S(1)}, bf16[16,1,448,128]{3,2,1,0:T(8,128)(2,1)}, u32[]{:S(2)}) copy-start(bf16[16,1,448,128]{3,2,1,0:T(8,128)(2,1)} %get-tuple-element.33) | copy-start | bytes 5505028
  163.7 6.3 %copy-start.16 = (pred[512]{0:T(512)(128)(4,1)S(1)}, pred[512]{0:T(512)(128)(4,1)}, u32[]{:S(2)}) copy-start(pred[512]{0:T(512)(128)(4,1)} %fusion.31) | copy-start | bytes 1540
  170.1 3.6 %copy-start.2 = (bf16[16,1,448,128]{3,2,1,0:T(8,128)(2,1)S(1)}, bf16[16,1,448,128]{3,2,1,0:T(8,128)(2,1)}, u32[]{:S(2)}) copy-start(bf16[16,1,448,128]{3,2,1,0:T(8,128)(2,1)} %get-tuple-element.32) | copy-start | bytes 5505028
  173.5 2.3 copy-start.6
  173.6 2.2 copy-start.1
  183.2 0.9 copy-start.7
  183.2 0.9 copy-start.17
  183.2 2.0 copy-start.9
  183.2 7.4 %slice-start.2 = ((s8[7340032]{0:T(1024)(128)(4,1)}), s8[3145728]{0:T(1024)(128)(4,1)S(1)}, s32[]{:S(2)}) async-start(s8[7340032]{0:T(1024)(128)(4,1)} %bitcast.56), calls=%async_computation.10 | async-start | bytes 6291456
  185.3 5.4 %slice-start.3 = ((s8[7340032]{0:T(1024)(128)(4,1)}), s8[4194304]{0:T(1024)(128)(4,1)S(1)}, s32[]{:S(2)}) async-start(s8[7340032]{0:T(1024)(128)(4,1)} %bitcast.56), calls=%async_computation.11 | async-start | bytes 8388608
  185.3 5.4 %copy-start.8 = (bf16[512,128]{0,1:T(8,128)(2,1)S(1)}, bf16[512,128]{0,1:T(8,128)(2,1)}, u32[]{:S(2)}) copy-start(bf16[512,128]{0,1:T(8,128)(2,1)} %get-tuple-element.42) | copy-start | bytes 393220
  190.7 2.1 copy-start.12
  204.9 83.6 %all-to-all-start.3 = ((bf16[16,1344,128]{2,1,0:T(8,128)(2,1)}), bf16[16,1344,128]{2,1,0:T(8,128)(2,1)}, u32[]{:S(2)}, u32[]{:S(2)}) async-start(bf16[16,1344,128]{2,1,0:T(8,128)(2,1)} %pad_maximum_fusion.1), calls=%async_computation.4 | async-start | bytes 11010048 | tf_op jit(solution)/shard_map/all_to_all | solution.py:138
  288.4 29.8 %all-to-all-start.2 = ((f32[16,4,7296]{2,1,0:T(4,128)}), f32[16,4,7296]{2,1,0:T(4,128)S(1)}, u32[]{:S(2)}, u32[]{:S(2)}) async-start(f32[16,4,7296]{2,1,0:T(4,128)} %reshape.164), calls=%async_computation.3 | async-start | bytes 3735552 | tf_op jit(solution)/shard_map/all_to_all | solution.py:122
  300.0 19.2 %copy-start.11 = (f32[32,256]{1,0:T(8,128)S(1)}, f32[32,256]{1,0:T(8,128)}, u32[]{:S(2)}) copy-start(f32[32,256]{1,0:T(8,128)} %copy-done.10) | copy-start | bytes 98308
  318.7 5.0 %copy-start.15 = (pred[256,8]{0,1:T(8,128)(4,1)S(1)}, pred[256,8]{0,1:T(8,128)(4,1)}, u32[]{:S(2)}) copy-start(pred[256,8]{0,1:T(8,128)(4,1)} %copy-done.14) | copy-start | bytes 6148
  318.7 5.1 %copy-start.13 = (s32[256,8]{0,1:T(8,128)S(1)}, s32[256,8]{0,1:T(8,128)}, u32[]{:S(2)}) copy-start(s32[256,8]{0,1:T(8,128)} %param.13) | copy-start | bytes 24580
  318.7 5.1 %copy-start.19 = (s32[8]{0:T(128)S(1)}, s32[8]{0:T(128)}, u32[]{:S(2)}) copy-start(s32[8]{0:T(128)} %copy-done.18) | copy-start | bytes 100
Sparse Core Ops, SparseCore 0:
  55.3 42.6 all-gather.4
  100.2 45.8 all-gather.2
  183.4 82.6 reduce-scatter.1

commit v5 on v3

--- a/solution.py
+++ b/solution.py
@@ -43,16 +43,12 @@
     row_slots = round_total * per_rank
     wide = model_width + LANE
 
-    def split_cols(w):
-        w = w.reshape(round_total, chunk, REPS, half)
-        return jnp.swapaxes(w, 1, 2).reshape(col_count, chunk, half)
-
-    send_wg = split_cols(w_gate)
-    send_wu = split_cols(w_up)
-    send_wd = split_cols(jnp.swapaxes(w_down, 1, 2))
-    slot_gate = lax.all_to_all(send_wg, "dev", 0, 0, tiled=True).reshape(model_width, half)
-    slot_up = lax.all_to_all(send_wu, "dev", 0, 0, tiled=True).reshape(model_width, half)
-    slot_down_t = lax.all_to_all(send_wd, "dev", 0, 0, tiled=True).reshape(model_width, half)
+    stacked = jnp.stack([w_gate, w_up, jnp.swapaxes(w_down, 1, 2)], axis=2)
+    stacked = stacked.reshape(round_total, chunk, 3, REPS, half).transpose(0, 3, 1, 2, 4)
+    send_w = stacked.reshape(col_count, chunk, 3 * half)
+    got_w = lax.all_to_all(send_w, "dev", 0, 0, tiled=True).reshape(model_width, 3 * half)
+    slot_gate_up = got_w[:, : 2 * half]
+    slot_down_t = got_w[:, 2 * half :]
 
     match, named, target = routing(expert_ids, slot_plan, col_count, round_total)
     q_ids = jnp.arange(row_slots, dtype=jnp.int32)
@@ -79,8 +75,9 @@
     dy_rows = dy_ext[:, :model_width]
     gate_rows = dy_ext[:, model_width].astype(jnp.float32)[:, None]
 
-    gate_pre = jnp.dot(x_rows, slot_gate, preferred_element_type=jnp.float32)
-    up_pre = jnp.dot(x_rows, slot_up, preferred_element_type=jnp.float32)
+    gate_up = jnp.dot(x_rows, slot_gate_up, preferred_element_type=jnp.float32)
+    gate_pre = gate_up[:, :half]
+    up_pre = gate_up[:, half:]
     back_proj = jnp.dot(dy_rows, slot_down_t, preferred_element_type=jnp.float32)
     sigmoid_gate = jax.nn.sigmoid(gate_pre)
     active = gate_pre * sigmoid_gate
@@ -100,20 +97,22 @@
         zero = jnp.zeros((), d.dtype)
         return jnp.concatenate([jnp.where(first_slot, d, zero), jnp.where(first_slot, zero, d)], axis=1)
 
-    def slot_pair_sum(rows, d):
-        acc = jnp.einsum("rd,rh->dh", rows, by_slot(d), preferred_element_type=jnp.float32)
+    def pair_sum(acc):
         acc = lax.reduce_precision(acc, exponent_bits=8, mantissa_bits=7)
         return (acc[:, :half] + acc[:, half:]).astype(jnp.bfloat16)
 
-    grad_gate_cols = slot_pair_sum(x_rows, d_gate)
-    grad_up_cols = slot_pair_sum(x_rows, d_up)
-    grad_down_cols = slot_pair_sum(dy_rows, scaled_hidden)
+    acc_gu = jnp.einsum(
+        "rd,rh->dh", x_rows, jnp.concatenate([by_slot(d_gate), by_slot(d_up)], axis=1),
+        preferred_element_type=jnp.float32,
+    )
+    grad_gate_cols = pair_sum(acc_gu[:, : 2 * half])
+    grad_up_cols = pair_sum(acc_gu[:, 2 * half :])
+    acc_down = jnp.einsum("rd,rh->dh", dy_rows, by_slot(scaled_hidden), preferred_element_type=jnp.float32)
+    grad_down_cols = pair_sum(acc_down)
 
+    d_both = jnp.concatenate([d_gate, d_up], axis=1)
     pad_rows = ((0, LANE), (0, 0))
-    row_ext = jnp.einsum("rh,dh->rd", d_gate, jnp.pad(slot_gate, pad_rows), preferred_element_type=jnp.float32)
-    row_ext = row_ext + jnp.einsum(
-        "rh,dh->rd", d_up, jnp.pad(slot_up, pad_rows), preferred_element_type=jnp.float32
-    )
+    row_ext = jnp.einsum("rh,dh->rd", d_both, jnp.pad(slot_gate_up, pad_rows), preferred_element_type=jnp.float32)
     term_col = jnp.arange(wide, dtype=jnp.int32)[None, :] == model_width
     row_ext = row_ext + jnp.where(term_col, gate_terms[:, None], 0.0)
 
@@ -125,7 +124,7 @@
         "qt,qd->td",
         pick_rows,
         back[:, :model_width],
-        precision=lax.Precision.HIGHEST,
+        precision=lax.Precision.HIGH,
     ).astype(jnp.bfloat16)
     back_q = back[:, model_width]
     rank_back = jnp.sum(jnp.where(chooser, back_q[:, None, None], 0.0), axis=0)

time: 325 us -> 340 us (1.046)
  other arithmetic: 20.1 us -> 40.3 us
  local copies, waits for them, and re-layouts: 18.8 us -> 36.8 us
  matrix products: 56.2 us -> 45.9 us
  starting transfers between devices: 32 us -> 24.4 us
  waiting for transfers between devices: 149 us -> 144 us
    all_to_all x3 -> x1, waiting for transfers between devices: 46.6 us -> 80.8 us  [local(): lax.all_to_all(send_w, 'dev', 0, 0, tiled=True)]
    all_to_all x1, waiting for transfers between devices: 22.3 us -> 0.01 us  [local(): lax.all_to_all(grad_down_cols.reshape(col_count, chunk, half), 'dev', 0,...]
    all_gather x1, waiting for transfers between devices: 15.7 us -> 0.02 us  [local(): dy_ext = lax.all_gather(both[:, model_width:], 'node', axis=0, tiled=True)]
    reduce_precision x0 -> x1, other arithmetic: none -> 11.8 us  [pair_sum(): acc = lax.reduce_precision(acc, exponent_bits=8, mantissa_bits=7)]
    reshape x0 -> x1, local copies, waits for them, and re-layouts: none -> 8.29 us  [local(): send_w = stacked.reshape(col_count, chunk, 3 * half)]
    all_to_all x3 -> x1, starting transfers between devices: 12.6 us -> 4.62 us  [local(): lax.all_to_all(send_w, 'dev', 0, 0, tiled=True)]
    dot_general x7 -> x4, matrix products: 38.9 us -> 31.3 us  [the longest x1 11.1 us: local(): jnp.einsum('rd,rh->dh', x_rows, jnp.concatenate([by_slot(d_gate), by_slot...]
    convert_element_type x3, other arithmetic: 4.76 us -> 11.3 us  [pair_sum(): return (acc[:, :half] + acc[:, half:]).astype(jnp.bfloat16)]
  transfers between devices with their start and end apart: 10 -> 8, of which waited for: 8 -> 5; matrix products, arithmetic and copies ran while one was open for 17% -> 25% of each run, Pallas kernels for 0% -> 0%
where the time goes in v5:
time: 340 us; the launch traced here: 339 us
  waiting for transfers between devices  144 us (42%)
  matrix products  45.9 us (14%)
  other arithmetic  40.3 us (12%)
  local copies, waits for them, and re-layouts  36.8 us (11%)
  blocking collectives  33.8 us (10%)
  starting transfers between devices  24.4 us (7%)
  between operations  14 us (4%)
    all_to_all x1, waiting for transfers between devices, local(): lax.all_to_all(send_w, 'dev', 0, 0, tiled=True)  80.8 us
    all_to_all x2, waiting for transfers between devices, home(): lax.all_to_all(sent, 'dev', 0, 0, tiled=True)  35.3 us
    all_to_all x1, blocking collectives, local(): lax.all_to_all(both.reshape(col_count, per_rank, both_width), 'dev', 0, 0...  33.8 us
    all_to_all x1, waiting for transfers between devices, local(): lax.all_to_all(summed.reshape(col_count, per_rank, wide), 'dev', 0, 0, ti...  20.2 us
    reduce_precision x1, other arithmetic, pair_sum(): acc = lax.reduce_precision(acc, exponent_bits=8, mantissa_bits=7)  11.8 us
    convert_element_type x3, other arithmetic, pair_sum(): return (acc[:, :half] + acc[:, half:]).astype(jnp.bfloat16)  11.3 us
    dot_general x1, matrix products, local(): jnp.einsum('rd,rh->dh', x_rows, jnp.concatenate([by_slot(d_gate), by_slot...  11.1 us
    all_to_all x2, starting transfers between devices, home(): lax.all_to_all(sent, 'dev', 0, 0, tiled=True)  11 us
  transfers between devices with their start and end apart: 8, of which 5 were waited for; matrix products, arithmetic and copies ran while one was open for 25% of the time, Pallas kernels for 0%

profile of v5, /device:TPU:0, one launch (start us, length us, event | category | flops | bytes accessed | tf_op | source)
XLA Modules:
  0.0 338.8 jit_solution(8228583389339511207)
XLA Ops:
  12.8 2.9 convolution_convert_fusion.1
  17.5 33.8 %all_to_all.30 = bf16[16,4,14464]{2,1,0:T(4,128)(2,1)} all-to-all(bf16[16,4,14464]{2,1,0:T(4,128)(2,1)S(1)} %bitcast.53), channel_id=1, replica_groups=mesh['node'=8,'dev'=16] {'dev'}, dimensions={0} | all-to-all | bytes 3702784 | tf_op jit(solution)/shard_map/all_to_all | solution.py:71
  51.3 2.8 reshape.163
  56.2 2.8 copy.58
  59.0 3.9 %copy.59 = bf16[8,448,256]{1,2,0:T(8,128)(2,1)} copy(bf16[8,448,256]{2,1,0:T(8,128)(2,1)} %param.16) | data formatting | bytes 3670016 | tf_op jit(solution)/shard_map/stack | solution.py:46
  62.9 3.9 %copy.60 = bf16[8,448,256]{1,2,0:T(8,128)(2,1)} copy(bf16[8,448,256]{2,1,0:T(8,128)(2,1)} %bitcast.59) | data formatting | bytes 3670016 | tf_op jit(solution)/shard_map/stack | solution.py:46
  66.8 5.7 %pad_maximum_fusion = bf16[8,448,3,2,128]{1,4,2,3,0:T(8,128)(2,1)} fusion(bf16[8,448,1,2,128]{1,4,2,3,0:T(8,128)(2,1)} %bitcast.52, bf16[8,448,1,2,128]{1,4,2,3,0:T(8,128)(2,1)} %bitcast.51, bf16[8,448,1,2,128]{1,4,2,3,0:T(8,128)(2,1)S(1)} %bitcast.50), kind=kLoop, calls=%fused_computation.10 | loop fusion | flops 5505024 | bytes 11010048 | tf_op jit(solution)/shard_map/stack | solution.py:46
  72.5 8.3 %copy.54 = bf16[16,448,384]{2,1,0:T(8,128)(2,1)} copy(bf16[16,448,384]{1,2,0:T(8,128)(2,1)} %bitcast.49) | data formatting | bytes 11010048 | tf_op jit(solution)/shard_map/reshape | solution.py:48
  80.8 4.6 %all-to-all-start.1 = ((bf16[16,448,384]{2,1,0:T(8,128)(2,1)}), bf16[16,448,384]{2,1,0:T(8,128)(2,1)}, u32[]{:S(2)}, u32[]{:S(2)}) async-start(bf16[16,448,384]{2,1,0:T(8,128)(2,1)} %copy.54), calls=%async_computation.1 | async-start | bytes 11010048 | tf_op jit(solution)/shard_map/all_to_all | solution.py:49
  85.7 80.8 %all-to-all-done.1 = bf16[16,448,384]{2,1,0:T(8,128)(2,1)} async-done(((bf16[16,448,384]{2,1,0:T(8,128)(2,1)}), bf16[16,448,384]{2,1,0:T(8,128)(2,1)}, u32[]{:S(2)}, u32[]{:S(2)}) %all-to-all-start.1) | async-done | bytes 5505056 | tf_op jit(solution)/shard_map/all_to_all | solution.py:49
  166.5 4.1 %slice.128 = bf16[7168,256]{1,0:T(8,128)(2,1)} slice(bf16[7168,384]{1,0:T(8,128)(2,1)} %bitcast.10), slice={[0:7168], [0:256]} | slice | bytes 7340032 | tf_op jit(solution)/shard_map/slice | solution.py:50
  170.6 6.2 %fusion.44 = f32[512,256]{0,1:T(8,128)S(1)} fusion(bf16[512,7168]{1,0:T(8,128)(2,1)} %all-gather.5.cloned.1.call-done, bf16[7168,384]{1,0:T(8,128)(2,1)} %bitcast.10), kind=kOutput, calls=%fused_computation.102 | convolution fusion | flops 1879048192 | bytes 11534336 | tf_op jit(solution)/shard_map/dot_general | solution.py:78
  177.9 6.3 %multiply_reduce_fusion = (f32[512]{0:T(512)S(1)}, f32[512,128]{0,1:T(8,128)S(1)}) fusion(f32[512,256]{0,1:T(8,128)S(1)} %fusion.44, bf16[7168,384]{1,0:T(8,128)(2,1)} %bitcast.10, bf16[512,7296]{1,0:T(8,128)(2,1)} %all-gather.3.cloned.1.call-done), kind=kOutput, calls=%fused_computation.52 | convolution fusion | flops 939982336 | bytes 9963520 | tf_op jit(solution)/shard_map/dot_general | solution.py:81
  184.4 8.7 %select_add_fusion = f32[512,7296]{1,0:T(8,128)} fusion(f32[512]{0:T(512)S(1)} %get-tuple-element.44, pred[7296]{0:T(1024)(128)(4,1)S(1)} %iota_compare_fusion.4, bf16[7168,256]{1,0:T(8,128)(2,1)S(1)} %copy-done, bf16[512,128]{0,1:T(8,128)(2,1)S(1)} %get-tuple-element.36, bf16[512,128]{0,1:T(8,128)(2,1)S(1)} %get-tuple-element.38), kind=kOutput, calls=%fused_computation | convolution fusion | flops 1920598016 | bytes 18883712 | tf_op jit(solution)/shard_map/rh,dh->rd/dot_general | solution.py:115
  193.2 5.2 %convolution_reduce-precision_fusion = f32[7168,256]{1,0:T(8,128)S(1)} fusion(bf16[512,7296]{1,0:T(8,128)(2,1)} %all-gather.3.cloned.1.call-done, bf16[512,128]{0,1:T(8,128)(2,1)S(1)} %get-tuple-element.41, bf16[512,128]{0,1:T(8,128)(2,1)S(1)} %get-tuple-element.19), kind=kOutput, calls=%fused_computation.1 | convolution fusion | flops 1881407488 | bytes 14942208 | tf_op jit(solution)/shard_map/rd,rh->dh/dot_general | solution.py:110
  198.4 1.6 fusion.4
  200.0 4.7 %all-to-all-start.5 = ((bf16[16,448,128]{2,1,0:T(8,128)(2,1)}), bf16[16,448,128]{2,1,0:T(8,128)(2,1)S(1)}, u32[]{:S(2)}, u32[]{:S(2)}) async-start(bf16[16,448,128]{2,1,0:T(8,128)(2,1)} %bitcast.56), calls=%async_computation.6 | async-start | bytes 3670016 | tf_op jit(solution)/shard_map/all_to_all | solution.py:140
  204.7 11.1 %fusion.12 = f32[7168,512]{1,0:T(8,128)} fusion(bf16[512,7168]{1,0:T(8,128)(2,1)} %all-gather.5.cloned.1.call-done, bf16[512,128]{0,1:T(8,128)(2,1)S(1)} %get-tuple-element.43, bf16[512,128]{0,1:T(8,128)(2,1)S(1)} %get-tuple-element.35, bf16[512,128]{0,1:T(8,128)(2,1)S(1)} %get-tuple-element.42, bf16[512,128]{0,1:T(8,128)(2,1)S(1)} %get-tuple-element.37), kind=kOutput, calls=%fused_computation.35 | convolution fusion | flops 3760193536 | bytes 22544384 | tf_op jit(solution)/shard_map/rd,rh->dh/dot_general | solution.py:104
  215.8 11.8 %slice_reduce-precision_fusion = (f32[7168,256]{1,0:T(8,128)}, f32[7168,256]{1,0:T(8,128)}) fusion(f32[7168,512]{1,0:T(8,128)} %fusion.12), kind=kLoop, calls=%fused_computation.5 | loop fusion | flops 3670016 | bytes 29360128 | tf_op jit(solution)/shard_map/reduce_precision | solution.py:101
  227.6 4.9 %fusion.5 = bf16[7168,128]{1,0:T(8,128)(2,1)} fusion(f32[7168,256]{1,0:T(8,128)} %get-tuple-element.25), kind=kLoop, calls=%fused_computation.15 | loop fusion | flops 1835008 | bytes 9175040 | tf_op jit(solution)/shard_map/convert_element_type | solution.py:102
  232.5 7.3 %all-to-all-start.4 = ((bf16[16,448,128]{2,1,0:T(8,128)(2,1)}), bf16[16,448,128]{2,1,0:T(8,128)(2,1)}, u32[]{:S(2)}, u32[]{:S(2)}) async-start(bf16[16,448,128]{2,1,0:T(8,128)(2,1)} %bitcast.58), calls=%async_computation.5 | async-start | bytes 3670016 | tf_op jit(solution)/shard_map/all_to_all | solution.py:135
  239.8 4.9 %fusion.6 = bf16[7168,128]{1,0:T(8,128)(2,1)} fusion(f32[7168,256]{1,0:T(8,128)} %get-tuple-element.26), kind=kLoop, calls=%fused_computation.17 | loop fusion | flops 1835008 | bytes 9175040 | tf_op jit(solution)/shard_map/convert_element_type | solution.py:102
  244.7 19.8 %all-to-all-done.4 = bf16[16,448,128]{2,1,0:T(8,128)(2,1)} async-done(((bf16[16,448,128]{2,1,0:T(8,128)(2,1)}), bf16[16,448,128]{2,1,0:T(8,128)(2,1)}, u32[]{:S(2)}, u32[]{:S(2)}) %all-to-all-start.4) | async-done | bytes 1835040 | tf_op jit(solution)/shard_map/all_to_all | solution.py:135
  264.5 3.7 %all-to-all-start.3 = ((bf16[16,448,128]{2,1,0:T(8,128)(2,1)}), bf16[16,448,128]{2,1,0:T(8,128)(2,1)S(1)}, u32[]{:S(2)}, u32[]{:S(2)}) async-start(bf16[16,448,128]{2,1,0:T(8,128)(2,1)} %bitcast.57), calls=%async_computation.4 | async-start | bytes 3670016 | tf_op jit(solution)/shard_map/all_to_all | solution.py:135
  268.2 7.2 %reduce-scatter.2.cloned.1.call-done = f32[64,7296]{1,0:T(8,128)} async-done(((f32[512,7296]{1,0:T(8,128)}), f32[64,7296]{1,0:T(8,128)}) %reduce-scatter.2.cloned.1.call-update) | async-done | bytes 1867792 | tf_op jit(solution)/shard_map/reduce_scatter | solution.py:119
  275.4 2.9 reshape.166
  278.3 15.5 %all-to-all-done.3 = bf16[16,448,128]{2,1,0:T(8,128)(2,1)S(1)} async-done(((bf16[16,448,128]{2,1,0:T(8,128)(2,1)}), bf16[16,448,128]{2,1,0:T(8,128)(2,1)S(1)}, u32[]{:S(2)}, u32[]{:S(2)}) %all-to-all-start.3) | async-done | bytes 1835040 | tf_op jit(solution)/shard_map/all_to_all | solution.py:135
  295.1 3.7 %all-to-all-start.2 = ((f32[16,4,7296]{2,1,0:T(4,128)}), f32[16,4,7296]{2,1,0:T(4,128)S(1)}, u32[]{:S(2)}, u32[]{:S(2)}) async-start(f32[16,4,7296]{2,1,0:T(4,128)} %reshape.166), calls=%async_computation.3 | async-start | bytes 3735552 | tf_op jit(solution)/shard_map/all_to_all | solution.py:120
  298.8 1.6 slice_bitcast_fusion.1
  303.5 2.3 pad_maximum_fusion.1
  305.9 20.2 %all-to-all-done.2 = f32[16,4,7296]{2,1,0:T(4,128)S(1)} async-done(((f32[16,4,7296]{2,1,0:T(4,128)}), f32[16,4,7296]{2,1,0:T(4,128)S(1)}, u32[]{:S(2)}, u32[]{:S(2)}) %all-to-all-start.2) | async-done | bytes 1867808 | tf_op jit(solution)/shard_map/all_to_all | solution.py:120
  327.0 4.5 %convolution_convert_fusion = bf16[256,7168]{1,0:T(8,128)(2,1)} fusion(f32[32,256]{1,0:T(8,128)S(1)} %get-tuple-element.18, f32[32,7296]{1,0:T(8,128)S(1)} %reshape.168), kind=kOutput, calls=%fused_computation.2 | convolution fusion | flops 354156544 | bytes 4620288 | tf_op jit(solution)/shard_map/qt,qd->td/dot_general | solution.py:123
  (57 shorter events, 17.0 us)
Async XLA Ops:
  7.2 163.4 %all-gather.5.cloned.1.call-start = ((), (), s32[]{:S(2)}) async-start(), calls=%async_computation.8 | async-start | bytes 8257536 | tf_op jit(solution)/shard_map/all_gather | solution.py:73
  12.8 3.1 copy-start.4
  55.2 121.7 %all-gather.3.cloned.1.call-start = ((), (), s32[]{:S(2)}) async-start(), calls=%async_computation.7 | async-start | bytes 8404992 | tf_op jit(solution)/shard_map/all_gather | solution.py:74
  80.8 85.7 %all-to-all-start.1 = ((bf16[16,448,384]{2,1,0:T(8,128)(2,1)}), bf16[16,448,384]{2,1,0:T(8,128)(2,1)}, u32[]{:S(2)}, u32[]{:S(2)}) async-start(bf16[16,448,384]{2,1,0:T(8,128)(2,1)} %copy.54), calls=%async_computation.1 | async-start | bytes 11010048 | tf_op jit(solution)/shard_map/all_to_all | solution.py:49
  85.4 190.0 %reduce-scatter.2.cloned.1.call-start = ((), (), s32[]{:S(2)}) async-start(), calls=%async_computation.9 | async-start | bytes 16809984 | tf_op jit(solution)/shard_map/reduce_scatter | solution.py:119
  177.8 6.5 %copy-start = (bf16[7168,256]{1,0:T(8,128)(2,1)S(1)}, bf16[7168,256]{1,0:T(8,128)(2,1)}, u32[]{:S(2)}) copy-start(bf16[7168,256]{1,0:T(8,128)(2,1)} %slice.128) | copy-start | bytes 11010052
  200.0 32.5 %all-to-all-start.5 = ((bf16[16,448,128]{2,1,0:T(8,128)(2,1)}), bf16[16,448,128]{2,1,0:T(8,128)(2,1)S(1)}, u32[]{:S(2)}, u32[]{:S(2)}) async-start(bf16[16,448,128]{2,1,0:T(8,128)(2,1)} %bitcast.56), calls=%async_computation.6 | async-start | bytes 3670016 | tf_op jit(solution)/shard_map/all_to_all | solution.py:140
  232.5 12.2 %copy-start.1 = (bf16[16,448,128]{2,1,0:T(8,128)(2,1)}, bf16[16,448,128]{2,1,0:T(8,128)(2,1)S(1)}, u32[]{:S(2)}) copy-start(bf16[16,448,128]{2,1,0:T(8,128)(2,1)S(1)} %all-to-all-done.5) | copy-start | bytes 5505028
  232.5 32.0 %all-to-all-start.4 = ((bf16[16,448,128]{2,1,0:T(8,128)(2,1)}), bf16[16,448,128]{2,1,0:T(8,128)(2,1)}, u32[]{:S(2)}, u32[]{:S(2)}) async-start(bf16[16,448,128]{2,1,0:T(8,128)(2,1)} %bitcast.58), calls=%async_computation.5 | async-start | bytes 3670016 | tf_op jit(solution)/shard_map/all_to_all | solution.py:135
  264.5 29.3 %all-to-all-start.3 = ((bf16[16,448,128]{2,1,0:T(8,128)(2,1)}), bf16[16,448,128]{2,1,0:T(8,128)(2,1)S(1)}, u32[]{:S(2)}, u32[]{:S(2)}) async-start(bf16[16,448,128]{2,1,0:T(8,128)(2,1)} %bitcast.57), calls=%async_computation.4 | async-start | bytes 3670016 | tf_op jit(solution)/shard_map/all_to_all | solution.py:135
  293.8 1.2 copy-start.2
  295.1 31.0 %all-to-all-start.2 = ((f32[16,4,7296]{2,1,0:T(4,128)}), f32[16,4,7296]{2,1,0:T(4,128)S(1)}, u32[]{:S(2)}, u32[]{:S(2)}) async-start(f32[16,4,7296]{2,1,0:T(4,128)} %reshape.166), calls=%async_computation.3 | async-start | bytes 3735552 | tf_op jit(solution)/shard_map/all_to_all | solution.py:120
  300.4 3.0 copy-start.3
  326.5 5.1 %copy-start.5 = (s32[256,8]{0,1:T(8,128)S(1)}, s32[256,8]{0,1:T(8,128)}, u32[]{:S(2)}) copy-start(s32[256,8]{0,1:T(8,128)} %param.13) | copy-start | bytes 24580
Sparse Core Ops, SparseCore 0:
  55.3 42.6 all-gather.4
  100.2 45.8 all-gather.2
  193.2 82.1 reduce-scatter.1

commit v6 on v3

--- a/solution.py
+++ b/solution.py
@@ -125,7 +125,7 @@
         "qt,qd->td",
         pick_rows,
         back[:, :model_width],
-        precision=lax.Precision.HIGHEST,
+        precision=lax.Precision.HIGH,
     ).astype(jnp.bfloat16)
     back_q = back[:, model_width]
     rank_back = jnp.sum(jnp.where(chooser, back_q[:, None, None], 0.0), axis=0)

time: 325 us -> 322 us (level)
  no operation moved by 1% of the time
where the time goes in v6:
time: 322 us; the launch traced here: 321 us
  waiting for transfers between devices  149 us (46%)
  matrix products  53.4 us (17%)
  blocking collectives  33.8 us (10%)
  starting transfers between devices  32 us (10%)
  other arithmetic  20.1 us (6%)
  local copies, waits for them, and re-layouts  18.8 us (6%)
  between operations  14 us (4%)
    all_to_all x2, waiting for transfers between devices, home(): lax.all_to_all(sent, 'dev', 0, 0, tiled=True)  38.8 us
    all_to_all x1, blocking collectives, local(): lax.all_to_all(both.reshape(col_count, per_rank, both_width), 'dev', 0, 0...  33.8 us
    all_to_all x1, waiting for transfers between devices, local(): lax.all_to_all(send_wg, 'dev', 0, 0, tiled=True).reshape(model_width, half)  23.4 us
    all_to_all x1, waiting for transfers between devices, local(): lax.all_to_all(send_wd, 'dev', 0, 0, tiled=True).reshape(model_width, half)  23.1 us
    all_to_all x1, waiting for transfers between devices, local(): lax.all_to_all(grad_down_cols.reshape(col_count, chunk, half), 'dev', 0,...  22.3 us
    all_to_all x1, waiting for transfers between devices, local(): lax.all_to_all(summed.reshape(col_count, per_rank, wide), 'dev', 0, 0, ti...  19.9 us
    dot_general x3, matrix products, slot_pair_sum(): jnp.einsum('rd,rh->dh', rows, by_slot(d), preferred_element_type=jnp.floa...  15.9 us
    all_gather x1, waiting for transfers between devices, local(): dy_ext = lax.all_gather(both[:, model_width:], 'node', axis=0, tiled=True)  15.7 us
  transfers between devices with their start and end apart: 10, of which 8 were waited for; matrix products, arithmetic and copies ran while one was open for 17% of the time, Pallas kernels for 0%

profile of v6, /device:TPU:0, one launch (start us, length us, event | category | flops | bytes accessed | tf_op | source)
XLA Modules:
  0.0 320.9 jit_solution(8365309489777812165)
XLA Ops:
  12.8 2.9 convolution_convert_fusion.1
  17.5 33.8 %all_to_all.40 = bf16[16,4,14464]{2,1,0:T(4,128)(2,1)} all-to-all(bf16[16,4,14464]{2,1,0:T(4,128)(2,1)S(1)} %bitcast.57), channel_id=1, replica_groups=mesh['node'=8,'dev'=16] {'dev'}, dimensions={0} | all-to-all | bytes 3702784 | tf_op jit(solution)/shard_map/all_to_all | solution.py:75
  51.3 2.8 reshape.171
  59.2 3.7 %all-to-all-start.3 = ((bf16[16,448,128]{2,1,0:T(8,128)(2,1)}), bf16[16,448,128]{2,1,0:T(8,128)(2,1)S(1)}, u32[]{:S(2)}, u32[]{:S(2)}) async-start(bf16[16,448,128]{2,1,0:T(8,128)(2,1)} %bitcast.62), calls=%async_computation.3 | async-start | bytes 3670016 | tf_op jit(solution)/shard_map/all_to_all | solution.py:53
  62.9 1.8 fusion.41
  66.0 23.4 %all-to-all-done.3 = bf16[16,448,128]{2,1,0:T(8,128)(2,1)S(1)} async-done(((bf16[16,448,128]{2,1,0:T(8,128)(2,1)}), bf16[16,448,128]{2,1,0:T(8,128)(2,1)S(1)}, u32[]{:S(2)}, u32[]{:S(2)}) %all-to-all-start.3) | async-done | bytes 1835040 | tf_op jit(solution)/shard_map/all_to_all | solution.py:53
  89.5 4.4 %all-to-all-start.1 = ((bf16[16,448,128]{2,1,0:T(8,128)(2,1)}), bf16[16,448,128]{2,1,0:T(8,128)(2,1)}, u32[]{:S(2)}, u32[]{:S(2)}) async-start(bf16[16,448,128]{2,1,0:T(8,128)(2,1)} %bitcast.61), calls=%async_computation.1 | async-start | bytes 3670016 | tf_op jit(solution)/shard_map/all_to_all | solution.py:55
  93.9 1.6 fusion.42
  96.8 23.1 %all-to-all-done.1 = bf16[16,448,128]{2,1,0:T(8,128)(2,1)} async-done(((bf16[16,448,128]{2,1,0:T(8,128)(2,1)}), bf16[16,448,128]{2,1,0:T(8,128)(2,1)}, u32[]{:S(2)}, u32[]{:S(2)}) %all-to-all-start.1) | async-done | bytes 1835040 | tf_op jit(solution)/shard_map/all_to_all | solution.py:55
  120.0 4.4 %all-to-all-start.2 = ((bf16[16,448,128]{2,1,0:T(8,128)(2,1)}), bf16[16,448,128]{2,1,0:T(8,128)(2,1)}, u32[]{:S(2)}, u32[]{:S(2)}) async-start(bf16[16,448,128]{2,1,0:T(8,128)(2,1)} %bitcast.60), calls=%async_computation.2 | async-start | bytes 3670016 | tf_op jit(solution)/shard_map/all_to_all | solution.py:54
  124.7 5.8 %fusion.44 = f32[512,128]{0,1:T(8,128)S(1)} fusion(bf16[512,7168]{1,0:T(8,128)(2,1)} %all-gather.5.cloned.1.call-done, bf16[7168,128]{1,0:T(8,128)(2,1)S(1)} %bitcast.55), kind=kOutput, calls=%fused_computation.103 | convolution fusion | flops 939524096 | bytes 9437184 | tf_op jit(solution)/shard_map/dot_general | solution.py:82
  130.5 15.7 %all-gather.3.cloned.1.call-done = bf16[512,7296]{1,0:T(8,128)(2,1)} async-done(((bf16[64,7296]{1,0:T(8,128)(2,1)}), bf16[512,7296]{1,0:T(8,128)(2,1)}) %all-gather.3.cloned.1.call-update) | async-done | bytes 7471120 | tf_op jit(solution)/shard_map/all_gather | solution.py:78
  147.2 6.1 %fusion.1 = f32[512,128]{0,1:T(8,128)S(1)} fusion(bf16[7168,128]{1,0:T(8,128)(2,1)} %bitcast.6, bf16[512,7296]{1,0:T(8,128)(2,1)} %all-gather.3.cloned.1.call-done), kind=kOutput, calls=%fused_computation.8 | convolution fusion | flops 939524096 | bytes 9437184 | tf_op jit(solution)/shard_map/dot_general | solution.py:84
  153.3 6.2 %broadcast_select_fusion.1 = (bf16[512,128]{0,1:T(8,128)(2,1)S(1)}, bf16[512,128]{0,1:T(8,128)(2,1)S(1)}, bf16[512,128]{0,1:T(8,128)(2,1)S(1)}, bf16[512,128]{0,...) fusion(pred[512]{0:T(512)(128)(4,1)S(1)} %fusion.31, ...), kind=kOutput, calls=%fused_computation.61 | convolution fusion | flops 940834816 | bytes 10750464 | tf_op jit(solution)/shard_map/dot_general | solution.py:83
  159.6 2.1 fusion.7
  161.8 8.9 %select_add_fusion = f32[512,7296]{1,0:T(8,128)} fusion(f32[512,7296]{1,0:T(8,128)S(1)} %fusion.7, bf16[512,128]{0,1:T(8,128)(2,1)S(1)} %get-tuple-element.40, f32[512]{0:T(512)S(1)} %multiply_reduce_fusion, pred[7296]{0:T(1024)(128)(4,1)S(1)} %iota_compare_fusion.4, bf16[7168,128]{1,0:T(8,128)(2,1)} %bitcast.8), kind=kOutput, calls=%fused_computation | convolution fusion | flops 967507968 | bytes 31859840 | tf_op jit(solution)/shard_map/rh,dh->rd/dot_general | solution.py:114
  170.7 5.2 %convolution_reduce-precision_fusion = f32[7168,256]{1,0:T(8,128)S(1)} fusion(bf16[512,7296]{1,0:T(8,128)(2,1)} %all-gather.3.cloned.1.call-done, bf16[512,128]{0,1:T(8,128)(2,1)S(1)} %get-tuple-element.43, bf16[512,128]{0,1:T(8,128)(2,1)S(1)} %get-tuple-element.19), kind=kOutput, calls=%fused_computation.1 | convolution fusion | flops 1881407488 | bytes 14942208 | tf_op jit(solution)/shard_map/rd,rh->dh/dot_general | solution.py:104
  177.5 7.0 %all-to-all-start.7 = ((bf16[16,448,128]{2,1,0:T(8,128)(2,1)}), bf16[16,448,128]{2,1,0:T(8,128)(2,1)S(1)}, u32[]{:S(2)}, u32[]{:S(2)}) async-start(bf16[16,448,128]{2,1,0:T(8,128)(2,1)} %bitcast.65), calls=%async_computation.8 | async-start | bytes 3670016 | tf_op jit(solution)/shard_map/all_to_all | solution.py:141
  184.5 5.3 %convolution_reduce-precision_fusion.2 = f32[7168,256]{1,0:T(8,128)S(1)} fusion(bf16[512,7168]{1,0:T(8,128)(2,1)} %all-gather.5.cloned.1.call-done, bf16[512,128]{0,1:T(8,128)(2,1)S(1)} %get-tuple-element.44, bf16[512,128]{0,1:T(8,128)(2,1)S(1)} %get-tuple-element.37), kind=kOutput, calls=%fused_computation.3 | convolution fusion | flops 1881407488 | bytes 14942208 | tf_op jit(solution)/shard_map/rd,rh->dh/dot_general | solution.py:104
  191.4 22.3 %all-to-all-done.7 = bf16[16,448,128]{2,1,0:T(8,128)(2,1)S(1)} async-done(((bf16[16,448,128]{2,1,0:T(8,128)(2,1)}), bf16[16,448,128]{2,1,0:T(8,128)(2,1)S(1)}, u32[]{:S(2)}, u32[]{:S(2)}) %all-to-all-start.7) | async-done | bytes 1835040 | tf_op jit(solution)/shard_map/all_to_all | solution.py:141
  213.7 4.4 %all-to-all-start.5 = ((bf16[16,448,128]{2,1,0:T(8,128)(2,1)}), bf16[16,448,128]{2,1,0:T(8,128)(2,1)}, u32[]{:S(2)}, u32[]{:S(2)}) async-start(bf16[16,448,128]{2,1,0:T(8,128)(2,1)} %bitcast.63), calls=%async_computation.6 | async-start | bytes 3670016 | tf_op jit(solution)/shard_map/all_to_all | solution.py:136
  218.1 5.4 %convolution_reduce-precision_fusion.1 = f32[7168,256]{1,0:T(8,128)S(1)} fusion(bf16[512,7168]{1,0:T(8,128)(2,1)} %all-gather.5.cloned.1.call-done, bf16[512,128]{0,1:T(8,128)(2,1)S(1)} %get-tuple-element.45, bf16[512,128]{0,1:T(8,128)(2,1)S(1)} %get-tuple-element.39), kind=kOutput, calls=%fused_computation.2 | convolution fusion | flops 1881407488 | bytes 14942208 | tf_op jit(solution)/shard_map/rd,rh->dh/dot_general | solution.py:104
  225.1 20.3 %all-to-all-done.5 = bf16[16,448,128]{2,1,0:T(8,128)(2,1)} async-done(((bf16[16,448,128]{2,1,0:T(8,128)(2,1)}), bf16[16,448,128]{2,1,0:T(8,128)(2,1)}, u32[]{:S(2)}, u32[]{:S(2)}) %all-to-all-start.5) | async-done | bytes 1835040 | tf_op jit(solution)/shard_map/all_to_all | solution.py:136
  245.4 3.7 %all-to-all-start.6 = ((bf16[16,448,128]{2,1,0:T(8,128)(2,1)}), bf16[16,448,128]{2,1,0:T(8,128)(2,1)S(1)}, u32[]{:S(2)}, u32[]{:S(2)}) async-start(bf16[16,448,128]{2,1,0:T(8,128)(2,1)} %bitcast.64), calls=%async_computation.7 | async-start | bytes 3670016 | tf_op jit(solution)/shard_map/all_to_all | solution.py:136
  249.1 5.5 %reduce-scatter.2.cloned.1.call-done = f32[64,7296]{1,0:T(8,128)} async-done(((f32[512,7296]{1,0:T(8,128)}), f32[64,7296]{1,0:T(8,128)}) %reduce-scatter.2.cloned.1.call-update) | async-done | bytes 1867792 | tf_op jit(solution)/shard_map/reduce_scatter | solution.py:120
  254.6 2.9 reshape.178
  257.4 18.5 %all-to-all-done.6 = bf16[16,448,128]{2,1,0:T(8,128)(2,1)S(1)} async-done(((bf16[16,448,128]{2,1,0:T(8,128)(2,1)}), bf16[16,448,128]{2,1,0:T(8,128)(2,1)S(1)}, u32[]{:S(2)}, u32[]{:S(2)}) %all-to-all-start.6) | async-done | bytes 1835040 | tf_op jit(solution)/shard_map/all_to_all | solution.py:136
  277.2 4.0 %all-to-all-start.4 = ((f32[16,4,7296]{2,1,0:T(4,128)}), f32[16,4,7296]{2,1,0:T(4,128)S(1)}, u32[]{:S(2)}, u32[]{:S(2)}) async-start(f32[16,4,7296]{2,1,0:T(4,128)} %reshape.178), calls=%async_computation.5 | async-start | bytes 3735552 | tf_op jit(solution)/shard_map/all_to_all | solution.py:121
  281.1 1.6 slice_bitcast_fusion.1
  285.9 2.3 pad_maximum_fusion.3
  288.2 19.9 %all-to-all-done.4 = f32[16,4,7296]{2,1,0:T(4,128)S(1)} async-done(((f32[16,4,7296]{2,1,0:T(4,128)}), f32[16,4,7296]{2,1,0:T(4,128)S(1)}, u32[]{:S(2)}, u32[]{:S(2)}) %all-to-all-start.4) | async-done | bytes 1867808 | tf_op jit(solution)/shard_map/all_to_all | solution.py:121
  309.0 4.5 %convolution_convert_fusion = bf16[256,7168]{1,0:T(8,128)(2,1)} fusion(f32[32,256]{1,0:T(8,128)S(1)} %get-tuple-element.18, f32[32,7296]{1,0:T(8,128)S(1)} %reshape.180), kind=kOutput, calls=%fused_computation.4 | convolution fusion | flops 354156544 | bytes 4620288 | tf_op jit(solution)/shard_map/qt,qd->td/dot_general | solution.py:124
  (61 shorter events, 27.2 us)
Async XLA Ops:
  7.2 117.5 %all-gather.5.cloned.1.call-start = ((), (), s32[]{:S(2)}) async-start(), calls=%async_computation.10 | async-start | bytes 8257536 | tf_op jit(solution)/shard_map/all_gather | solution.py:77
  12.8 3.1 copy-start.3
  55.2 91.0 %all-gather.3.cloned.1.call-start = ((), (), s32[]{:S(2)}) async-start(), calls=%async_computation.9 | async-start | bytes 8404992 | tf_op jit(solution)/shard_map/all_gather | solution.py:78
  59.2 30.3 %all-to-all-start.3 = ((bf16[16,448,128]{2,1,0:T(8,128)(2,1)}), bf16[16,448,128]{2,1,0:T(8,128)(2,1)S(1)}, u32[]{:S(2)}, u32[]{:S(2)}) async-start(bf16[16,448,128]{2,1,0:T(8,128)(2,1)} %bitcast.62), calls=%async_computation.3 | async-start | bytes 3670016 | tf_op jit(solution)/shard_map/all_to_all | solution.py:53
  89.5 30.5 %all-to-all-start.1 = ((bf16[16,448,128]{2,1,0:T(8,128)(2,1)}), bf16[16,448,128]{2,1,0:T(8,128)(2,1)}, u32[]{:S(2)}, u32[]{:S(2)}) async-start(bf16[16,448,128]{2,1,0:T(8,128)(2,1)} %bitcast.61), calls=%async_computation.1 | async-start | bytes 3670016 | tf_op jit(solution)/shard_map/all_to_all | solution.py:55
  120.0 33.3 %all-to-all-start.2 = ((bf16[16,448,128]{2,1,0:T(8,128)(2,1)}), bf16[16,448,128]{2,1,0:T(8,128)(2,1)}, u32[]{:S(2)}, u32[]{:S(2)}) async-start(bf16[16,448,128]{2,1,0:T(8,128)(2,1)} %bitcast.60), calls=%async_computation.2 | async-start | bytes 3670016 | tf_op jit(solution)/shard_map/all_to_all | solution.py:54
  124.4 130.2 %reduce-scatter.2.cloned.1.call-start = ((), (), s32[]{:S(2)}) async-start(), calls=%async_computation.11 | async-start | bytes 16809984 | tf_op jit(solution)/shard_map/reduce_scatter | solution.py:120
  177.5 36.2 %all-to-all-start.7 = ((bf16[16,448,128]{2,1,0:T(8,128)(2,1)}), bf16[16,448,128]{2,1,0:T(8,128)(2,1)S(1)}, u32[]{:S(2)}, u32[]{:S(2)}) async-start(bf16[16,448,128]{2,1,0:T(8,128)(2,1)} %bitcast.65), calls=%async_computation.8 | async-start | bytes 3670016 | tf_op jit(solution)/shard_map/all_to_all | solution.py:141
  213.7 9.8 %copy-start = (bf16[16,448,128]{2,1,0:T(8,128)(2,1)}, bf16[16,448,128]{2,1,0:T(8,128)(2,1)S(1)}, u32[]{:S(2)}) copy-start(bf16[16,448,128]{2,1,0:T(8,128)(2,1)S(1)} %all-to-all-done.7) | copy-start | bytes 5505028
  213.7 31.7 %all-to-all-start.5 = ((bf16[16,448,128]{2,1,0:T(8,128)(2,1)}), bf16[16,448,128]{2,1,0:T(8,128)(2,1)}, u32[]{:S(2)}, u32[]{:S(2)}) async-start(bf16[16,448,128]{2,1,0:T(8,128)(2,1)} %bitcast.63), calls=%async_computation.6 | async-start | bytes 3670016 | tf_op jit(solution)/shard_map/all_to_all | solution.py:136
  245.4 30.5 %all-to-all-start.6 = ((bf16[16,448,128]{2,1,0:T(8,128)(2,1)}), bf16[16,448,128]{2,1,0:T(8,128)(2,1)S(1)}, u32[]{:S(2)}, u32[]{:S(2)}) async-start(bf16[16,448,128]{2,1,0:T(8,128)(2,1)} %bitcast.64), calls=%async_computation.7 | async-start | bytes 3670016 | tf_op jit(solution)/shard_map/all_to_all | solution.py:136
  275.9 1.2 copy-start.1
  277.2 31.0 %all-to-all-start.4 = ((f32[16,4,7296]{2,1,0:T(4,128)}), f32[16,4,7296]{2,1,0:T(4,128)S(1)}, u32[]{:S(2)}, u32[]{:S(2)}) async-start(f32[16,4,7296]{2,1,0:T(4,128)} %reshape.178), calls=%async_computation.5 | async-start | bytes 3735552 | tf_op jit(solution)/shard_map/all_to_all | solution.py:121
  282.7 3.0 copy-start.2
  308.6 5.1 %copy-start.4 = (s32[256,8]{0,1:T(8,128)S(1)}, s32[256,8]{0,1:T(8,128)}, u32[]{:S(2)}) copy-start(s32[256,8]{0,1:T(8,128)} %param.13) | copy-start | bytes 24580
Sparse Core Ops, SparseCore 0:
  55.3 42.6 all-gather.4
  100.2 45.8 all-gather.2
  170.8 83.7 reduce-scatter.1

commit v7 on v6

--- a/solution.py
+++ b/solution.py
@@ -72,7 +72,8 @@
     both_width = model_width + wide
     both = both_send.reshape(round_total, 1, per_rank, both_width)
     both = jnp.broadcast_to(both, (round_total, REPS, per_rank, both_width))
-    both = lax.all_to_all(both.reshape(col_count, per_rank, both_width), "dev", 0, 0, tiled=True)
+    flat = per_rank * both_width // LANE
+    both = lax.all_to_all(both.reshape(col_count, flat, LANE), "dev", 0, 0, tiled=True)
     both = both.reshape(col_count * per_rank, both_width)
     x_rows = lax.all_gather(both[:, :model_width], "node", axis=0, tiled=True)
     dy_ext = lax.all_gather(both[:, model_width:], "node", axis=0, tiled=True)

time: 322 us -> 327 us (1.016)
  local copies, waits for them, and re-layouts: 18.8 us -> 23.7 us
  transfers between devices with their start and end apart: 10 -> 10, of which waited for: 8 -> 8; matrix products, arithmetic and copies ran while one was open for 17% -> 16% of each run, Pallas kernels for 0% -> 0%
where the time goes in v7:
time: 327 us; the launch traced here: 326 us
  waiting for transfers between devices  149 us (46%)
  matrix products  53.4 us (16%)
  blocking collectives  34 us (10%)
  starting transfers between devices  32 us (10%)
  local copies, waits for them, and re-layouts  23.7 us (7%)
  other arithmetic  20.1 us (6%)
  between operations  14 us (4%)
    all_to_all x2, waiting for transfers between devices, home(): lax.all_to_all(sent, 'dev', 0, 0, tiled=True)  38.8 us
    all_to_all x1, blocking collectives, local(): lax.all_to_all(both.reshape(col_count, flat, LANE), 'dev', 0, 0, tiled=True)  34 us
    all_to_all x1, waiting for transfers between devices, local(): lax.all_to_all(send_wg, 'dev', 0, 0, tiled=True).reshape(model_width, half)  23.4 us
    all_to_all x1, waiting for transfers between devices, local(): lax.all_to_all(send_wd, 'dev', 0, 0, tiled=True).reshape(model_width, half)  23.1 us
    all_to_all x1, waiting for transfers between devices, local(): lax.all_to_all(grad_down_cols.reshape(col_count, chunk, half), 'dev', 0,...  22.3 us
    all_to_all x1, waiting for transfers between devices, local(): lax.all_to_all(summed.reshape(col_count, per_rank, wide), 'dev', 0, 0, ti...  19.9 us
    dot_general x3, matrix products, slot_pair_sum(): jnp.einsum('rd,rh->dh', rows, by_slot(d), preferred_element_type=jnp.floa...  15.9 us
    all_gather x1, waiting for transfers between devices, local(): dy_ext = lax.all_gather(both[:, model_width:], 'node', axis=0, tiled=True)  15.6 us
  transfers between devices with their start and end apart: 10, of which 8 were waited for; matrix products, arithmetic and copies ran while one was open for 16% of the time, Pallas kernels for 0%

profile of v7, /device:TPU:0, one launch (start us, length us, event | category | flops | bytes accessed | tf_op | source)
XLA Modules:
  0.0 326.0 jit_solution(14126615847056119134)
XLA Ops:
  12.8 2.9 convolution_convert_fusion.1
  17.0 1.7 broadcast_in_dim.158
  18.7 3.1 reshape.170
  21.8 34.0 %all_to_all.40 = bf16[16,452,128]{2,1,0:T(8,128)(2,1)} all-to-all(bf16[16,452,128]{2,1,0:T(8,128)(2,1)S(1)} %reshape.170), channel_id=1, replica_groups=mesh['node'=8,'dev'=16] {'dev'}, dimensions={0} | all-to-all | bytes 3702784 | tf_op jit(solution)/shard_map/all_to_all | solution.py:76
  55.8 3.4 %reshape.171 = bf16[64,14464]{1,0:T(8,128)(2,1)S(1)} reshape(bf16[16,452,128]{2,1,0:T(8,128)(2,1)} %all_to_all.40) | data formatting | bytes 3702784 | tf_op jit(solution)/shard_map/reshape | solution.py:77
  64.2 3.7 %all-to-all-start.3 = ((bf16[16,448,128]{2,1,0:T(8,128)(2,1)}), bf16[16,448,128]{2,1,0:T(8,128)(2,1)S(1)}, u32[]{:S(2)}, u32[]{:S(2)}) async-start(bf16[16,448,128]{2,1,0:T(8,128)(2,1)} %bitcast.60), calls=%async_computation.3 | async-start | bytes 3670016 | tf_op jit(solution)/shard_map/all_to_all | solution.py:53
  68.0 1.8 fusion.41
  71.1 23.4 %all-to-all-done.3 = bf16[16,448,128]{2,1,0:T(8,128)(2,1)S(1)} async-done(((bf16[16,448,128]{2,1,0:T(8,128)(2,1)}), bf16[16,448,128]{2,1,0:T(8,128)(2,1)S(1)}, u32[]{:S(2)}, u32[]{:S(2)}) %all-to-all-start.3) | async-done | bytes 1835040 | tf_op jit(solution)/shard_map/all_to_all | solution.py:53
  94.6 4.4 %all-to-all-start.1 = ((bf16[16,448,128]{2,1,0:T(8,128)(2,1)}), bf16[16,448,128]{2,1,0:T(8,128)(2,1)}, u32[]{:S(2)}, u32[]{:S(2)}) async-start(bf16[16,448,128]{2,1,0:T(8,128)(2,1)} %bitcast.59), calls=%async_computation.1 | async-start | bytes 3670016 | tf_op jit(solution)/shard_map/all_to_all | solution.py:55
  101.9 23.1 %all-to-all-done.1 = bf16[16,448,128]{2,1,0:T(8,128)(2,1)} async-done(((bf16[16,448,128]{2,1,0:T(8,128)(2,1)}), bf16[16,448,128]{2,1,0:T(8,128)(2,1)}, u32[]{:S(2)}, u32[]{:S(2)}) %all-to-all-start.1) | async-done | bytes 1835040 | tf_op jit(solution)/shard_map/all_to_all | solution.py:55
  125.1 4.4 %all-to-all-start.2 = ((bf16[16,448,128]{2,1,0:T(8,128)(2,1)}), bf16[16,448,128]{2,1,0:T(8,128)(2,1)}, u32[]{:S(2)}, u32[]{:S(2)}) async-start(bf16[16,448,128]{2,1,0:T(8,128)(2,1)} %bitcast.58), calls=%async_computation.2 | async-start | bytes 3670016 | tf_op jit(solution)/shard_map/all_to_all | solution.py:54
  129.8 5.8 %fusion.44 = f32[512,128]{0,1:T(8,128)S(1)} fusion(bf16[512,7168]{1,0:T(8,128)(2,1)} %all-gather.5.cloned.1.call-done, bf16[7168,128]{1,0:T(8,128)(2,1)S(1)} %bitcast.54), kind=kOutput, calls=%fused_computation.103 | convolution fusion | flops 939524096 | bytes 9437184 | tf_op jit(solution)/shard_map/dot_general | solution.py:83
  135.6 15.6 %all-gather.3.cloned.1.call-done = bf16[512,7296]{1,0:T(8,128)(2,1)} async-done(((bf16[64,7296]{1,0:T(8,128)(2,1)}), bf16[512,7296]{1,0:T(8,128)(2,1)}) %all-gather.3.cloned.1.call-update) | async-done | bytes 7471120 | tf_op jit(solution)/shard_map/all_gather | solution.py:79
  152.2 6.1 %fusion.1 = f32[512,128]{0,1:T(8,128)S(1)} fusion(bf16[7168,128]{1,0:T(8,128)(2,1)} %bitcast.5, bf16[512,7296]{1,0:T(8,128)(2,1)} %all-gather.3.cloned.1.call-done), kind=kOutput, calls=%fused_computation.8 | convolution fusion | flops 939524096 | bytes 9437184 | tf_op jit(solution)/shard_map/dot_general | solution.py:85
  158.4 6.2 %broadcast_select_fusion.1 = (bf16[512,128]{0,1:T(8,128)(2,1)S(1)}, bf16[512,128]{0,1:T(8,128)(2,1)S(1)}, bf16[512,128]{0,1:T(8,128)(2,1)S(1)}, bf16[512,128]{0,...) fusion(pred[512]{0:T(512)(128)(4,1)S(1)} %fusion.31, ...), kind=kOutput, calls=%fused_computation.61 | convolution fusion | flops 940834816 | bytes 10750464 | tf_op jit(solution)/shard_map/dot_general | solution.py:84
  164.7 2.1 fusion.7
  166.8 8.9 %select_add_fusion = f32[512,7296]{1,0:T(8,128)} fusion(f32[512,7296]{1,0:T(8,128)S(1)} %fusion.7, bf16[512,128]{0,1:T(8,128)(2,1)S(1)} %get-tuple-element.40, f32[512]{0:T(512)S(1)} %multiply_reduce_fusion, pred[7296]{0:T(1024)(128)(4,1)S(1)} %iota_compare_fusion.4, bf16[7168,128]{1,0:T(8,128)(2,1)} %bitcast.7), kind=kOutput, calls=%fused_computation | convolution fusion | flops 967507968 | bytes 31859840 | tf_op jit(solution)/shard_map/rh,dh->rd/dot_general | solution.py:115
  175.8 5.2 %convolution_reduce-precision_fusion = f32[7168,256]{1,0:T(8,128)S(1)} fusion(bf16[512,7296]{1,0:T(8,128)(2,1)} %all-gather.3.cloned.1.call-done, bf16[512,128]{0,1:T(8,128)(2,1)S(1)} %get-tuple-element.43, bf16[512,128]{0,1:T(8,128)(2,1)S(1)} %get-tuple-element.19), kind=kOutput, calls=%fused_computation.1 | convolution fusion | flops 1881407488 | bytes 14942208 | tf_op jit(solution)/shard_map/rd,rh->dh/dot_general | solution.py:105
  182.6 7.0 %all-to-all-start.7 = ((bf16[16,448,128]{2,1,0:T(8,128)(2,1)}), bf16[16,448,128]{2,1,0:T(8,128)(2,1)S(1)}, u32[]{:S(2)}, u32[]{:S(2)}) async-start(bf16[16,448,128]{2,1,0:T(8,128)(2,1)} %bitcast.63), calls=%async_computation.8 | async-start | bytes 3670016 | tf_op jit(solution)/shard_map/all_to_all | solution.py:142
  189.6 5.3 %convolution_reduce-precision_fusion.2 = f32[7168,256]{1,0:T(8,128)S(1)} fusion(bf16[512,7168]{1,0:T(8,128)(2,1)} %all-gather.5.cloned.1.call-done, bf16[512,128]{0,1:T(8,128)(2,1)S(1)} %get-tuple-element.44, bf16[512,128]{0,1:T(8,128)(2,1)S(1)} %get-tuple-element.37), kind=kOutput, calls=%fused_computation.3 | convolution fusion | flops 1881407488 | bytes 14942208 | tf_op jit(solution)/shard_map/rd,rh->dh/dot_general | solution.py:105
  196.5 22.3 %all-to-all-done.7 = bf16[16,448,128]{2,1,0:T(8,128)(2,1)S(1)} async-done(((bf16[16,448,128]{2,1,0:T(8,128)(2,1)}), bf16[16,448,128]{2,1,0:T(8,128)(2,1)S(1)}, u32[]{:S(2)}, u32[]{:S(2)}) %all-to-all-start.7) | async-done | bytes 1835040 | tf_op jit(solution)/shard_map/all_to_all | solution.py:142
  218.8 4.4 %all-to-all-start.5 = ((bf16[16,448,128]{2,1,0:T(8,128)(2,1)}), bf16[16,448,128]{2,1,0:T(8,128)(2,1)}, u32[]{:S(2)}, u32[]{:S(2)}) async-start(bf16[16,448,128]{2,1,0:T(8,128)(2,1)} %bitcast.61), calls=%async_computation.6 | async-start | bytes 3670016 | tf_op jit(solution)/shard_map/all_to_all | solution.py:137
  223.2 5.4 %convolution_reduce-precision_fusion.1 = f32[7168,256]{1,0:T(8,128)S(1)} fusion(bf16[512,7168]{1,0:T(8,128)(2,1)} %all-gather.5.cloned.1.call-done, bf16[512,128]{0,1:T(8,128)(2,1)S(1)} %get-tuple-element.45, bf16[512,128]{0,1:T(8,128)(2,1)S(1)} %get-tuple-element.39), kind=kOutput, calls=%fused_computation.2 | convolution fusion | flops 1881407488 | bytes 14942208 | tf_op jit(solution)/shard_map/rd,rh->dh/dot_general | solution.py:105
  230.2 20.3 %all-to-all-done.5 = bf16[16,448,128]{2,1,0:T(8,128)(2,1)} async-done(((bf16[16,448,128]{2,1,0:T(8,128)(2,1)}), bf16[16,448,128]{2,1,0:T(8,128)(2,1)}, u32[]{:S(2)}, u32[]{:S(2)}) %all-to-all-start.5) | async-done | bytes 1835040 | tf_op jit(solution)/shard_map/all_to_all | solution.py:137
  250.4 3.7 %all-to-all-start.6 = ((bf16[16,448,128]{2,1,0:T(8,128)(2,1)}), bf16[16,448,128]{2,1,0:T(8,128)(2,1)S(1)}, u32[]{:S(2)}, u32[]{:S(2)}) async-start(bf16[16,448,128]{2,1,0:T(8,128)(2,1)} %bitcast.62), calls=%async_computation.7 | async-start | bytes 3670016 | tf_op jit(solution)/shard_map/all_to_all | solution.py:137
  254.2 5.4 %reduce-scatter.2.cloned.1.call-done = f32[64,7296]{1,0:T(8,128)} async-done(((f32[512,7296]{1,0:T(8,128)}), f32[64,7296]{1,0:T(8,128)}) %reduce-scatter.2.cloned.1.call-update) | async-done | bytes 1867792 | tf_op jit(solution)/shard_map/reduce_scatter | solution.py:121
  259.6 2.9 reshape.178
  262.5 18.5 %all-to-all-done.6 = bf16[16,448,128]{2,1,0:T(8,128)(2,1)S(1)} async-done(((bf16[16,448,128]{2,1,0:T(8,128)(2,1)}), bf16[16,448,128]{2,1,0:T(8,128)(2,1)S(1)}, u32[]{:S(2)}, u32[]{:S(2)}) %all-to-all-start.6) | async-done | bytes 1835040 | tf_op jit(solution)/shard_map/all_to_all | solution.py:137
  282.2 4.0 %all-to-all-start.4 = ((f32[16,4,7296]{2,1,0:T(4,128)}), f32[16,4,7296]{2,1,0:T(4,128)S(1)}, u32[]{:S(2)}, u32[]{:S(2)}) async-start(f32[16,4,7296]{2,1,0:T(4,128)} %reshape.178), calls=%async_computation.5 | async-start | bytes 3735552 | tf_op jit(solution)/shard_map/all_to_all | solution.py:122
  291.0 2.3 pad_maximum_fusion.3
  293.3 19.9 %all-to-all-done.4 = f32[16,4,7296]{2,1,0:T(4,128)S(1)} async-done(((f32[16,4,7296]{2,1,0:T(4,128)}), f32[16,4,7296]{2,1,0:T(4,128)S(1)}, u32[]{:S(2)}, u32[]{:S(2)}) %all-to-all-start.4) | async-done | bytes 1867808 | tf_op jit(solution)/shard_map/all_to_all | solution.py:122
  314.1 4.5 %convolution_convert_fusion = bf16[256,7168]{1,0:T(8,128)(2,1)} fusion(f32[32,256]{1,0:T(8,128)S(1)} %get-tuple-element.18, f32[32,7296]{1,0:T(8,128)S(1)} %reshape.180), kind=kOutput, calls=%fused_computation.4 | convolution fusion | flops 354156544 | bytes 4620288 | tf_op jit(solution)/shard_map/qt,qd->td/dot_general | solution.py:125
  (62 shorter events, 29.9 us)
Async XLA Ops:
  7.2 122.6 %all-gather.5.cloned.1.call-start = ((), (), s32[]{:S(2)}) async-start(), calls=%async_computation.10 | async-start | bytes 8257536 | tf_op jit(solution)/shard_map/all_gather | solution.py:78
  12.8 3.1 copy-start.3
  60.2 91.0 %all-gather.3.cloned.1.call-start = ((), (), s32[]{:S(2)}) async-start(), calls=%async_computation.9 | async-start | bytes 8404992 | tf_op jit(solution)/shard_map/all_gather | solution.py:79
  64.2 30.3 %all-to-all-start.3 = ((bf16[16,448,128]{2,1,0:T(8,128)(2,1)}), bf16[16,448,128]{2,1,0:T(8,128)(2,1)S(1)}, u32[]{:S(2)}, u32[]{:S(2)}) async-start(bf16[16,448,128]{2,1,0:T(8,128)(2,1)} %bitcast.60), calls=%async_computation.3 | async-start | bytes 3670016 | tf_op jit(solution)/shard_map/all_to_all | solution.py:53
  94.6 30.5 %all-to-all-start.1 = ((bf16[16,448,128]{2,1,0:T(8,128)(2,1)}), bf16[16,448,128]{2,1,0:T(8,128)(2,1)}, u32[]{:S(2)}, u32[]{:S(2)}) async-start(bf16[16,448,128]{2,1,0:T(8,128)(2,1)} %bitcast.59), calls=%async_computation.1 | async-start | bytes 3670016 | tf_op jit(solution)/shard_map/all_to_all | solution.py:55
  125.1 33.3 %all-to-all-start.2 = ((bf16[16,448,128]{2,1,0:T(8,128)(2,1)}), bf16[16,448,128]{2,1,0:T(8,128)(2,1)}, u32[]{:S(2)}, u32[]{:S(2)}) async-start(bf16[16,448,128]{2,1,0:T(8,128)(2,1)} %bitcast.58), calls=%async_computation.2 | async-start | bytes 3670016 | tf_op jit(solution)/shard_map/all_to_all | solution.py:54
  129.5 130.1 %reduce-scatter.2.cloned.1.call-start = ((), (), s32[]{:S(2)}) async-start(), calls=%async_computation.11 | async-start | bytes 16809984 | tf_op jit(solution)/shard_map/reduce_scatter | solution.py:121
  182.6 36.2 %all-to-all-start.7 = ((bf16[16,448,128]{2,1,0:T(8,128)(2,1)}), bf16[16,448,128]{2,1,0:T(8,128)(2,1)S(1)}, u32[]{:S(2)}, u32[]{:S(2)}) async-start(bf16[16,448,128]{2,1,0:T(8,128)(2,1)} %bitcast.63), calls=%async_computation.8 | async-start | bytes 3670016 | tf_op jit(solution)/shard_map/all_to_all | solution.py:142
  218.8 9.8 %copy-start = (bf16[16,448,128]{2,1,0:T(8,128)(2,1)}, bf16[16,448,128]{2,1,0:T(8,128)(2,1)S(1)}, u32[]{:S(2)}) copy-start(bf16[16,448,128]{2,1,0:T(8,128)(2,1)S(1)} %all-to-all-done.7) | copy-start | bytes 5505028
  218.8 31.7 %all-to-all-start.5 = ((bf16[16,448,128]{2,1,0:T(8,128)(2,1)}), bf16[16,448,128]{2,1,0:T(8,128)(2,1)}, u32[]{:S(2)}, u32[]{:S(2)}) async-start(bf16[16,448,128]{2,1,0:T(8,128)(2,1)} %bitcast.61), calls=%async_computation.6 | async-start | bytes 3670016 | tf_op jit(solution)/shard_map/all_to_all | solution.py:137
  250.4 30.5 %all-to-all-start.6 = ((bf16[16,448,128]{2,1,0:T(8,128)(2,1)}), bf16[16,448,128]{2,1,0:T(8,128)(2,1)S(1)}, u32[]{:S(2)}, u32[]{:S(2)}) async-start(bf16[16,448,128]{2,1,0:T(8,128)(2,1)} %bitcast.62), calls=%async_computation.7 | async-start | bytes 3670016 | tf_op jit(solution)/shard_map/all_to_all | solution.py:137
  281.0 1.2 copy-start.1
  282.2 31.0 %all-to-all-start.4 = ((f32[16,4,7296]{2,1,0:T(4,128)}), f32[16,4,7296]{2,1,0:T(4,128)S(1)}, u32[]{:S(2)}, u32[]{:S(2)}) async-start(f32[16,4,7296]{2,1,0:T(4,128)} %reshape.178), calls=%async_computation.5 | async-start | bytes 3735552 | tf_op jit(solution)/shard_map/all_to_all | solution.py:122
  287.8 3.0 copy-start.2
  313.6 5.1 %copy-start.4 = (s32[256,8]{0,1:T(8,128)S(1)}, s32[256,8]{0,1:T(8,128)}, u32[]{:S(2)}) copy-start(s32[256,8]{0,1:T(8,128)} %param.13) | copy-start | bytes 24580
Sparse Core Ops, SparseCore 0:
  60.4 42.5 all-gather.4
  105.3 45.8 all-gather.2
  175.9 83.7 reduce-scatter.1

commit v8 on v6

--- a/solution.py
+++ b/solution.py
@@ -3,7 +3,7 @@
 from jax import lax
 from jax.sharding import PartitionSpec as P
 
-TOP = 8
+
 CAP = 2
 REPS = 2
 LANE = 128
@@ -36,7 +36,7 @@
 def local(tokens, grad_out, router_gates, expert_ids, slot_plan, w_gate, w_up, w_down):
     col_count = lax.axis_size("dev")
     node_count = lax.axis_size("node")
-    tok_rows, model_width = tokens.shape
+    _, model_width = tokens.shape
     round_total, chunk, node_hidden = w_gate.shape
     half = node_hidden // REPS
     per_rank = REPS * CAP
@@ -133,7 +133,8 @@
 
     def home(cols):
         sent = cols.reshape(col_count, chunk, half)
-        got = lax.all_to_all(sent, "dev", 0, 0, tiled=True).reshape(round_total, REPS, chunk, half)
+        got = lax.all_to_all(sent, "dev", 0, 0, tiled=True)
+        got = got.reshape(round_total, REPS, chunk, half)
         return jnp.concatenate([got[:, h] for h in range(REPS)], axis=-1)
 
     grad_w_gate = home(grad_gate_cols)

time: 322 us -> 322 us (level)
  no operation moved by 1% of the time
where the time goes in v8:
time: 322 us; the launch traced here: 321 us
  waiting for transfers between devices  149 us (46%)
  matrix products  53.4 us (17%)
  blocking collectives  33.8 us (10%)
  starting transfers between devices  32 us (10%)
  other arithmetic  20.1 us (6%)
  local copies, waits for them, and re-layouts  18.8 us (6%)
  between operations  14 us (4%)
    all_to_all x2, waiting for transfers between devices, home(): got = lax.all_to_all(sent, 'dev', 0, 0, tiled=True)  38.8 us
    all_to_all x1, blocking collectives, local(): lax.all_to_all(both.reshape(col_count, per_rank, both_width), 'dev', 0, 0...  33.8 us
    all_to_all x1, waiting for transfers between devices, local(): lax.all_to_all(send_wg, 'dev', 0, 0, tiled=True).reshape(model_width, half)  23.4 us
    all_to_all x1, waiting for transfers between devices, local(): lax.all_to_all(send_wd, 'dev', 0, 0, tiled=True).reshape(model_width, half)  23.1 us
    all_to_all x1, waiting for transfers between devices, local(): lax.all_to_all(grad_down_cols.reshape(col_count, chunk, half), 'dev', 0,...  22.3 us
    all_to_all x1, waiting for transfers between devices, local(): lax.all_to_all(summed.reshape(col_count, per_rank, wide), 'dev', 0, 0, ti...  19.9 us
    dot_general x3, matrix products, slot_pair_sum(): jnp.einsum('rd,rh->dh', rows, by_slot(d), preferred_element_type=jnp.floa...  15.9 us
    all_gather x1, waiting for transfers between devices, local(): dy_ext = lax.all_gather(both[:, model_width:], 'node', axis=0, tiled=True)  15.7 us
  transfers between devices with their start and end apart: 10, of which 8 were waited for; matrix products, arithmetic and copies ran while one was open for 17% of the time, Pallas kernels for 0%

profile of v8, /device:TPU:0, one launch (start us, length us, event | category | flops | bytes accessed | tf_op | source)
XLA Modules:
  0.0 320.9 jit_solution(8365309489777812165)
XLA Ops:
  12.8 2.9 convolution_convert_fusion.1
  17.5 33.8 %all_to_all.40 = bf16[16,4,14464]{2,1,0:T(4,128)(2,1)} all-to-all(bf16[16,4,14464]{2,1,0:T(4,128)(2,1)S(1)} %bitcast.57), channel_id=1, replica_groups=mesh['node'=8,'dev'=16] {'dev'}, dimensions={0} | all-to-all | bytes 3702784 | tf_op jit(solution)/shard_map/all_to_all | solution.py:75
  51.3 2.8 reshape.171
  59.2 3.7 %all-to-all-start.3 = ((bf16[16,448,128]{2,1,0:T(8,128)(2,1)}), bf16[16,448,128]{2,1,0:T(8,128)(2,1)S(1)}, u32[]{:S(2)}, u32[]{:S(2)}) async-start(bf16[16,448,128]{2,1,0:T(8,128)(2,1)} %bitcast.62), calls=%async_computation.3 | async-start | bytes 3670016 | tf_op jit(solution)/shard_map/all_to_all | solution.py:53
  62.9 1.8 fusion.41
  66.0 23.4 %all-to-all-done.3 = bf16[16,448,128]{2,1,0:T(8,128)(2,1)S(1)} async-done(((bf16[16,448,128]{2,1,0:T(8,128)(2,1)}), bf16[16,448,128]{2,1,0:T(8,128)(2,1)S(1)}, u32[]{:S(2)}, u32[]{:S(2)}) %all-to-all-start.3) | async-done | bytes 1835040 | tf_op jit(solution)/shard_map/all_to_all | solution.py:53
  89.5 4.4 %all-to-all-start.1 = ((bf16[16,448,128]{2,1,0:T(8,128)(2,1)}), bf16[16,448,128]{2,1,0:T(8,128)(2,1)}, u32[]{:S(2)}, u32[]{:S(2)}) async-start(bf16[16,448,128]{2,1,0:T(8,128)(2,1)} %bitcast.61), calls=%async_computation.1 | async-start | bytes 3670016 | tf_op jit(solution)/shard_map/all_to_all | solution.py:55
  93.9 1.6 fusion.42
  96.8 23.1 %all-to-all-done.1 = bf16[16,448,128]{2,1,0:T(8,128)(2,1)} async-done(((bf16[16,448,128]{2,1,0:T(8,128)(2,1)}), bf16[16,448,128]{2,1,0:T(8,128)(2,1)}, u32[]{:S(2)}, u32[]{:S(2)}) %all-to-all-start.1) | async-done | bytes 1835040 | tf_op jit(solution)/shard_map/all_to_all | solution.py:55
  120.0 4.4 %all-to-all-start.2 = ((bf16[16,448,128]{2,1,0:T(8,128)(2,1)}), bf16[16,448,128]{2,1,0:T(8,128)(2,1)}, u32[]{:S(2)}, u32[]{:S(2)}) async-start(bf16[16,448,128]{2,1,0:T(8,128)(2,1)} %bitcast.60), calls=%async_computation.2 | async-start | bytes 3670016 | tf_op jit(solution)/shard_map/all_to_all | solution.py:54
  124.7 5.8 %fusion.44 = f32[512,128]{0,1:T(8,128)S(1)} fusion(bf16[512,7168]{1,0:T(8,128)(2,1)} %all-gather.5.cloned.1.call-done, bf16[7168,128]{1,0:T(8,128)(2,1)S(1)} %bitcast.55), kind=kOutput, calls=%fused_computation.103 | convolution fusion | flops 939524096 | bytes 9437184 | tf_op jit(solution)/shard_map/dot_general | solution.py:82
  130.5 15.7 %all-gather.3.cloned.1.call-done = bf16[512,7296]{1,0:T(8,128)(2,1)} async-done(((bf16[64,7296]{1,0:T(8,128)(2,1)}), bf16[512,7296]{1,0:T(8,128)(2,1)}) %all-gather.3.cloned.1.call-update) | async-done | bytes 7471120 | tf_op jit(solution)/shard_map/all_gather | solution.py:78
  147.2 6.1 %fusion.1 = f32[512,128]{0,1:T(8,128)S(1)} fusion(bf16[7168,128]{1,0:T(8,128)(2,1)} %bitcast.6, bf16[512,7296]{1,0:T(8,128)(2,1)} %all-gather.3.cloned.1.call-done), kind=kOutput, calls=%fused_computation.8 | convolution fusion | flops 939524096 | bytes 9437184 | tf_op jit(solution)/shard_map/dot_general | solution.py:84
  153.3 6.2 %broadcast_select_fusion.1 = (bf16[512,128]{0,1:T(8,128)(2,1)S(1)}, bf16[512,128]{0,1:T(8,128)(2,1)S(1)}, bf16[512,128]{0,1:T(8,128)(2,1)S(1)}, bf16[512,128]{0,...) fusion(pred[512]{0:T(512)(128)(4,1)S(1)} %fusion.31, ...), kind=kOutput, calls=%fused_computation.61 | convolution fusion | flops 940834816 | bytes 10750464 | tf_op jit(solution)/shard_map/dot_general | solution.py:83
  159.6 2.1 fusion.7
  161.8 8.9 %select_add_fusion = f32[512,7296]{1,0:T(8,128)} fusion(f32[512,7296]{1,0:T(8,128)S(1)} %fusion.7, bf16[512,128]{0,1:T(8,128)(2,1)S(1)} %get-tuple-element.40, f32[512]{0:T(512)S(1)} %multiply_reduce_fusion, pred[7296]{0:T(1024)(128)(4,1)S(1)} %iota_compare_fusion.4, bf16[7168,128]{1,0:T(8,128)(2,1)} %bitcast.8), kind=kOutput, calls=%fused_computation | convolution fusion | flops 967507968 | bytes 31859840 | tf_op jit(solution)/shard_map/rh,dh->rd/dot_general | solution.py:114
  170.7 5.2 %convolution_reduce-precision_fusion = f32[7168,256]{1,0:T(8,128)S(1)} fusion(bf16[512,7296]{1,0:T(8,128)(2,1)} %all-gather.3.cloned.1.call-done, bf16[512,128]{0,1:T(8,128)(2,1)S(1)} %get-tuple-element.43, bf16[512,128]{0,1:T(8,128)(2,1)S(1)} %get-tuple-element.19), kind=kOutput, calls=%fused_computation.1 | convolution fusion | flops 1881407488 | bytes 14942208 | tf_op jit(solution)/shard_map/rd,rh->dh/dot_general | solution.py:104
  177.5 7.0 %all-to-all-start.7 = ((bf16[16,448,128]{2,1,0:T(8,128)(2,1)}), bf16[16,448,128]{2,1,0:T(8,128)(2,1)S(1)}, u32[]{:S(2)}, u32[]{:S(2)}) async-start(bf16[16,448,128]{2,1,0:T(8,128)(2,1)} %bitcast.65), calls=%async_computation.8 | async-start | bytes 3670016 | tf_op jit(solution)/shard_map/all_to_all | solution.py:142
  184.5 5.3 %convolution_reduce-precision_fusion.2 = f32[7168,256]{1,0:T(8,128)S(1)} fusion(bf16[512,7168]{1,0:T(8,128)(2,1)} %all-gather.5.cloned.1.call-done, bf16[512,128]{0,1:T(8,128)(2,1)S(1)} %get-tuple-element.44, bf16[512,128]{0,1:T(8,128)(2,1)S(1)} %get-tuple-element.37), kind=kOutput, calls=%fused_computation.3 | convolution fusion | flops 1881407488 | bytes 14942208 | tf_op jit(solution)/shard_map/rd,rh->dh/dot_general | solution.py:104
  191.4 22.3 %all-to-all-done.7 = bf16[16,448,128]{2,1,0:T(8,128)(2,1)S(1)} async-done(((bf16[16,448,128]{2,1,0:T(8,128)(2,1)}), bf16[16,448,128]{2,1,0:T(8,128)(2,1)S(1)}, u32[]{:S(2)}, u32[]{:S(2)}) %all-to-all-start.7) | async-done | bytes 1835040 | tf_op jit(solution)/shard_map/all_to_all | solution.py:142
  213.7 4.4 %all-to-all-start.5 = ((bf16[16,448,128]{2,1,0:T(8,128)(2,1)}), bf16[16,448,128]{2,1,0:T(8,128)(2,1)}, u32[]{:S(2)}, u32[]{:S(2)}) async-start(bf16[16,448,128]{2,1,0:T(8,128)(2,1)} %bitcast.63), calls=%async_computation.6 | async-start | bytes 3670016 | tf_op jit(solution)/shard_map/all_to_all | solution.py:136
  218.1 5.4 %convolution_reduce-precision_fusion.1 = f32[7168,256]{1,0:T(8,128)S(1)} fusion(bf16[512,7168]{1,0:T(8,128)(2,1)} %all-gather.5.cloned.1.call-done, bf16[512,128]{0,1:T(8,128)(2,1)S(1)} %get-tuple-element.45, bf16[512,128]{0,1:T(8,128)(2,1)S(1)} %get-tuple-element.39), kind=kOutput, calls=%fused_computation.2 | convolution fusion | flops 1881407488 | bytes 14942208 | tf_op jit(solution)/shard_map/rd,rh->dh/dot_general | solution.py:104
  225.1 20.3 %all-to-all-done.5 = bf16[16,448,128]{2,1,0:T(8,128)(2,1)} async-done(((bf16[16,448,128]{2,1,0:T(8,128)(2,1)}), bf16[16,448,128]{2,1,0:T(8,128)(2,1)}, u32[]{:S(2)}, u32[]{:S(2)}) %all-to-all-start.5) | async-done | bytes 1835040 | tf_op jit(solution)/shard_map/all_to_all | solution.py:136
  245.4 3.7 %all-to-all-start.6 = ((bf16[16,448,128]{2,1,0:T(8,128)(2,1)}), bf16[16,448,128]{2,1,0:T(8,128)(2,1)S(1)}, u32[]{:S(2)}, u32[]{:S(2)}) async-start(bf16[16,448,128]{2,1,0:T(8,128)(2,1)} %bitcast.64), calls=%async_computation.7 | async-start | bytes 3670016 | tf_op jit(solution)/shard_map/all_to_all | solution.py:136
  249.1 5.5 %reduce-scatter.2.cloned.1.call-done = f32[64,7296]{1,0:T(8,128)} async-done(((f32[512,7296]{1,0:T(8,128)}), f32[64,7296]{1,0:T(8,128)}) %reduce-scatter.2.cloned.1.call-update) | async-done | bytes 1867792 | tf_op jit(solution)/shard_map/reduce_scatter | solution.py:120
  254.6 2.9 reshape.178
  257.4 18.5 %all-to-all-done.6 = bf16[16,448,128]{2,1,0:T(8,128)(2,1)S(1)} async-done(((bf16[16,448,128]{2,1,0:T(8,128)(2,1)}), bf16[16,448,128]{2,1,0:T(8,128)(2,1)S(1)}, u32[]{:S(2)}, u32[]{:S(2)}) %all-to-all-start.6) | async-done | bytes 1835040 | tf_op jit(solution)/shard_map/all_to_all | solution.py:136
  277.2 4.0 %all-to-all-start.4 = ((f32[16,4,7296]{2,1,0:T(4,128)}), f32[16,4,7296]{2,1,0:T(4,128)S(1)}, u32[]{:S(2)}, u32[]{:S(2)}) async-start(f32[16,4,7296]{2,1,0:T(4,128)} %reshape.178), calls=%async_computation.5 | async-start | bytes 3735552 | tf_op jit(solution)/shard_map/all_to_all | solution.py:121
  281.1 1.6 slice_bitcast_fusion.1
  285.9 2.3 pad_maximum_fusion.3
  288.2 19.9 %all-to-all-done.4 = f32[16,4,7296]{2,1,0:T(4,128)S(1)} async-done(((f32[16,4,7296]{2,1,0:T(4,128)}), f32[16,4,7296]{2,1,0:T(4,128)S(1)}, u32[]{:S(2)}, u32[]{:S(2)}) %all-to-all-start.4) | async-done | bytes 1867808 | tf_op jit(solution)/shard_map/all_to_all | solution.py:121
  309.0 4.5 %convolution_convert_fusion = bf16[256,7168]{1,0:T(8,128)(2,1)} fusion(f32[32,256]{1,0:T(8,128)S(1)} %get-tuple-element.18, f32[32,7296]{1,0:T(8,128)S(1)} %reshape.180), kind=kOutput, calls=%fused_computation.4 | convolution fusion | flops 354156544 | bytes 4620288 | tf_op jit(solution)/shard_map/qt,qd->td/dot_general | solution.py:124
  (61 shorter events, 27.2 us)
Async XLA Ops:
  7.2 117.5 %all-gather.5.cloned.1.call-start = ((), (), s32[]{:S(2)}) async-start(), calls=%async_computation.10 | async-start | bytes 8257536 | tf_op jit(solution)/shard_map/all_gather | solution.py:77
  12.8 3.1 copy-start.3
  55.2 91.0 %all-gather.3.cloned.1.call-start = ((), (), s32[]{:S(2)}) async-start(), calls=%async_computation.9 | async-start | bytes 8404992 | tf_op jit(solution)/shard_map/all_gather | solution.py:78
  59.2 30.3 %all-to-all-start.3 = ((bf16[16,448,128]{2,1,0:T(8,128)(2,1)}), bf16[16,448,128]{2,1,0:T(8,128)(2,1)S(1)}, u32[]{:S(2)}, u32[]{:S(2)}) async-start(bf16[16,448,128]{2,1,0:T(8,128)(2,1)} %bitcast.62), calls=%async_computation.3 | async-start | bytes 3670016 | tf_op jit(solution)/shard_map/all_to_all | solution.py:53
  89.5 30.5 %all-to-all-start.1 = ((bf16[16,448,128]{2,1,0:T(8,128)(2,1)}), bf16[16,448,128]{2,1,0:T(8,128)(2,1)}, u32[]{:S(2)}, u32[]{:S(2)}) async-start(bf16[16,448,128]{2,1,0:T(8,128)(2,1)} %bitcast.61), calls=%async_computation.1 | async-start | bytes 3670016 | tf_op jit(solution)/shard_map/all_to_all | solution.py:55
  120.0 33.3 %all-to-all-start.2 = ((bf16[16,448,128]{2,1,0:T(8,128)(2,1)}), bf16[16,448,128]{2,1,0:T(8,128)(2,1)}, u32[]{:S(2)}, u32[]{:S(2)}) async-start(bf16[16,448,128]{2,1,0:T(8,128)(2,1)} %bitcast.60), calls=%async_computation.2 | async-start | bytes 3670016 | tf_op jit(solution)/shard_map/all_to_all | solution.py:54
  124.4 130.2 %reduce-scatter.2.cloned.1.call-start = ((), (), s32[]{:S(2)}) async-start(), calls=%async_computation.11 | async-start | bytes 16809984 | tf_op jit(solution)/shard_map/reduce_scatter | solution.py:120
  177.5 36.2 %all-to-all-start.7 = ((bf16[16,448,128]{2,1,0:T(8,128)(2,1)}), bf16[16,448,128]{2,1,0:T(8,128)(2,1)S(1)}, u32[]{:S(2)}, u32[]{:S(2)}) async-start(bf16[16,448,128]{2,1,0:T(8,128)(2,1)} %bitcast.65), calls=%async_computation.8 | async-start | bytes 3670016 | tf_op jit(solution)/shard_map/all_to_all | solution.py:142
  213.7 9.8 %copy-start = (bf16[16,448,128]{2,1,0:T(8,128)(2,1)}, bf16[16,448,128]{2,1,0:T(8,128)(2,1)S(1)}, u32[]{:S(2)}) copy-start(bf16[16,448,128]{2,1,0:T(8,128)(2,1)S(1)} %all-to-all-done.7) | copy-start | bytes 5505028
  213.7 31.7 %all-to-all-start.5 = ((bf16[16,448,128]{2,1,0:T(8,128)(2,1)}), bf16[16,448,128]{2,1,0:T(8,128)(2,1)}, u32[]{:S(2)}, u32[]{:S(2)}) async-start(bf16[16,448,128]{2,1,0:T(8,128)(2,1)} %bitcast.63), calls=%async_computation.6 | async-start | bytes 3670016 | tf_op jit(solution)/shard_map/all_to_all | solution.py:136
  245.4 30.5 %all-to-all-start.6 = ((bf16[16,448,128]{2,1,0:T(8,128)(2,1)}), bf16[16,448,128]{2,1,0:T(8,128)(2,1)S(1)}, u32[]{:S(2)}, u32[]{:S(2)}) async-start(bf16[16,448,128]{2,1,0:T(8,128)(2,1)} %bitcast.64), calls=%async_computation.7 | async-start | bytes 3670016 | tf_op jit(solution)/shard_map/all_to_all | solution.py:136
  275.9 1.2 copy-start.1
  277.2 31.0 %all-to-all-start.4 = ((f32[16,4,7296]{2,1,0:T(4,128)}), f32[16,4,7296]{2,1,0:T(4,128)S(1)}, u32[]{:S(2)}, u32[]{:S(2)}) async-start(f32[16,4,7296]{2,1,0:T(4,128)} %reshape.178), calls=%async_computation.5 | async-start | bytes 3735552 | tf_op jit(solution)/shard_map/all_to_all | solution.py:121
  282.7 3.0 copy-start.2
  308.6 5.1 %copy-start.4 = (s32[256,8]{0,1:T(8,128)S(1)}, s32[256,8]{0,1:T(8,128)}, u32[]{:S(2)}) copy-start(s32[256,8]{0,1:T(8,128)} %param.13) | copy-start | bytes 24580
Sparse Core Ops, SparseCore 0:
  55.3 42.6 all-gather.4
  100.2 45.8 all-gather.2
  170.8 83.7 reduce-scatter.1

commit v9 on v6

--- a/solution.py
+++ b/solution.py
@@ -65,7 +65,7 @@
 
     x_send = jnp.dot(pick_half, tokens, preferred_element_type=jnp.float32).astype(jnp.bfloat16)
     dy_send = jnp.dot(pick_half, grad_out, preferred_element_type=jnp.float32).astype(jnp.bfloat16)
-    gate_block = jnp.zeros((row_slots, LANE), jnp.bfloat16).at[:, 0].set(gate_send)
+    gate_block = jnp.where(jnp.arange(LANE)[None, :] == 0, gate_send[:, None], jnp.zeros((), jnp.bfloat16))
     dy_send = jnp.concatenate([dy_send, gate_block], axis=1)
 
     both_send = jnp.concatenate([x_send, dy_send], axis=1)
@@ -121,12 +121,12 @@
     back = lax.all_to_all(summed.reshape(col_count, per_rank, wide), "dev", 0, 0, tiled=True)
     back = jnp.sum(back.reshape(round_total, REPS, per_rank, wide), axis=1).reshape(row_slots, wide)
 
-    grad_tokens = jnp.einsum(
-        "qt,qd->td",
-        pick_rows,
-        back[:, :model_width],
-        precision=lax.Precision.HIGH,
-    ).astype(jnp.bfloat16)
+    back_tok = back[:, :model_width]
+    back_hi = back_tok.astype(jnp.bfloat16)
+    back_lo = (back_tok - back_hi.astype(jnp.float32)).astype(jnp.bfloat16)
+    grad_tokens = jnp.einsum("qt,qd->td", pick_half, back_hi, preferred_element_type=jnp.float32)
+    grad_tokens = grad_tokens + jnp.einsum("qt,qd->td", pick_half, back_lo, preferred_element_type=jnp.float32)
+    grad_tokens = grad_tokens.astype(jnp.bfloat16)
     back_q = back[:, model_width]
     rank_back = jnp.sum(jnp.where(chooser, back_q[:, None, None], 0.0), axis=0)
     grad_gates = jnp.sum(jnp.where(match, rank_back[:, None, :], 0.0), axis=-1)

time: 322 us -> 320 us (level)
  no operation moved by 1% of the time
where the time goes in v9:
time: 320 us; the launch traced here: 319 us
  waiting for transfers between devices  149 us (47%)
  matrix products  52.8 us (16%)
  blocking collectives  33.8 us (11%)
  starting transfers between devices  32 us (10%)
  other arithmetic  19.1 us (6%)
  local copies, waits for them, and re-layouts  18.5 us (6%)
  between operations  14.1 us (4%)
    all_to_all x2, waiting for transfers between devices, home(): lax.all_to_all(sent, 'dev', 0, 0, tiled=True)  38.8 us
    all_to_all x1, blocking collectives, local(): lax.all_to_all(both.reshape(col_count, per_rank, both_width), 'dev', 0, 0...  33.8 us
    all_to_all x1, waiting for transfers between devices, local(): lax.all_to_all(send_wg, 'dev', 0, 0, tiled=True).reshape(model_width, half)  23.4 us
    all_to_all x1, waiting for transfers between devices, local(): lax.all_to_all(send_wd, 'dev', 0, 0, tiled=True).reshape(model_width, half)  23.1 us
    all_to_all x1, waiting for transfers between devices, local(): lax.all_to_all(grad_down_cols.reshape(col_count, chunk, half), 'dev', 0,...  22.3 us
    all_to_all x1, waiting for transfers between devices, local(): lax.all_to_all(summed.reshape(col_count, per_rank, wide), 'dev', 0, 0, ti...  19.9 us
    dot_general x3, matrix products, slot_pair_sum(): jnp.einsum('rd,rh->dh', rows, by_slot(d), preferred_element_type=jnp.floa...  15.9 us
    all_gather x1, waiting for transfers between devices, local(): dy_ext = lax.all_gather(both[:, model_width:], 'node', axis=0, tiled=True)  15.7 us
  transfers between devices with their start and end apart: 10, of which 8 were waited for; matrix products, arithmetic and copies ran while one was open for 17% of the time, Pallas kernels for 0%

profile of v9, /device:TPU:0, one launch (start us, length us, event | category | flops | bytes accessed | tf_op | source)
XLA Modules:
  0.0 319.0 jit_solution(12823636620467152112)
XLA Ops:
  11.6 2.8 convolution_convert_fusion
  16.0 33.8 %all_to_all.40 = bf16[16,4,14464]{2,1,0:T(4,128)(2,1)} all-to-all(bf16[16,4,14464]{2,1,0:T(4,128)(2,1)S(1)} %bitcast.58), channel_id=1, replica_groups=mesh['node'=8,'dev'=16] {'dev'}, dimensions={0} | all-to-all | bytes 3702784 | tf_op jit(solution)/shard_map/all_to_all | solution.py:75
  49.8 2.8 reshape.139
  57.7 3.7 %all-to-all-start.3 = ((bf16[16,448,128]{2,1,0:T(8,128)(2,1)}), bf16[16,448,128]{2,1,0:T(8,128)(2,1)S(1)}, u32[]{:S(2)}, u32[]{:S(2)}) async-start(bf16[16,448,128]{2,1,0:T(8,128)(2,1)} %bitcast.63), calls=%async_computation.3 | async-start | bytes 3670016 | tf_op jit(solution)/shard_map/all_to_all | solution.py:53
  61.4 1.8 fusion.37
  64.5 23.4 %all-to-all-done.3 = bf16[16,448,128]{2,1,0:T(8,128)(2,1)S(1)} async-done(((bf16[16,448,128]{2,1,0:T(8,128)(2,1)}), bf16[16,448,128]{2,1,0:T(8,128)(2,1)S(1)}, u32[]{:S(2)}, u32[]{:S(2)}) %all-to-all-start.3) | async-done | bytes 1835040 | tf_op jit(solution)/shard_map/all_to_all | solution.py:53
  88.0 4.4 %all-to-all-start.1 = ((bf16[16,448,128]{2,1,0:T(8,128)(2,1)}), bf16[16,448,128]{2,1,0:T(8,128)(2,1)}, u32[]{:S(2)}, u32[]{:S(2)}) async-start(bf16[16,448,128]{2,1,0:T(8,128)(2,1)} %bitcast.62), calls=%async_computation.1 | async-start | bytes 3670016 | tf_op jit(solution)/shard_map/all_to_all | solution.py:55
  92.4 1.6 fusion.38
  95.4 23.1 %all-to-all-done.1 = bf16[16,448,128]{2,1,0:T(8,128)(2,1)} async-done(((bf16[16,448,128]{2,1,0:T(8,128)(2,1)}), bf16[16,448,128]{2,1,0:T(8,128)(2,1)}, u32[]{:S(2)}, u32[]{:S(2)}) %all-to-all-start.1) | async-done | bytes 1835040 | tf_op jit(solution)/shard_map/all_to_all | solution.py:55
  118.5 4.4 %all-to-all-start.2 = ((bf16[16,448,128]{2,1,0:T(8,128)(2,1)}), bf16[16,448,128]{2,1,0:T(8,128)(2,1)}, u32[]{:S(2)}, u32[]{:S(2)}) async-start(bf16[16,448,128]{2,1,0:T(8,128)(2,1)} %bitcast.61), calls=%async_computation.2 | async-start | bytes 3670016 | tf_op jit(solution)/shard_map/all_to_all | solution.py:54
  123.2 5.8 %fusion.40 = f32[512,128]{0,1:T(8,128)S(1)} fusion(bf16[512,7168]{1,0:T(8,128)(2,1)} %all-gather.5.cloned.1.call-done, bf16[7168,128]{1,0:T(8,128)(2,1)S(1)} %bitcast.56), kind=kOutput, calls=%fused_computation.101 | convolution fusion | flops 939524096 | bytes 9437184 | tf_op jit(solution)/shard_map/dot_general | solution.py:82
  129.0 15.7 %all-gather.3.cloned.1.call-done = bf16[512,7296]{1,0:T(8,128)(2,1)} async-done(((bf16[64,7296]{1,0:T(8,128)(2,1)}), bf16[512,7296]{1,0:T(8,128)(2,1)}) %all-gather.3.cloned.1.call-update) | async-done | bytes 7471120 | tf_op jit(solution)/shard_map/all_gather | solution.py:78
  145.7 6.1 %fusion.2 = f32[512,128]{0,1:T(8,128)S(1)} fusion(bf16[7168,128]{1,0:T(8,128)(2,1)} %bitcast.5, bf16[512,7296]{1,0:T(8,128)(2,1)} %all-gather.3.cloned.1.call-done), kind=kOutput, calls=%fused_computation.9 | convolution fusion | flops 939524096 | bytes 9437184 | tf_op jit(solution)/shard_map/dot_general | solution.py:84
  151.8 6.2 %broadcast_select_fusion.1 = (bf16[512,128]{0,1:T(8,128)(2,1)S(1)}, bf16[512,128]{0,1:T(8,128)(2,1)S(1)}, bf16[512,128]{0,1:T(8,128)(2,1)S(1)}, bf16[512,128]{0,...) fusion(pred[512]{0:T(512)(128)(4,1)S(1)} %fusion.28, ...), kind=kOutput, calls=%fused_computation.62 | convolution fusion | flops 940834816 | bytes 10750464 | tf_op jit(solution)/shard_map/dot_general | solution.py:83
  158.1 2.1 fusion.8
  160.3 8.9 %select_add_fusion = f32[512,7296]{1,0:T(8,128)} fusion(f32[512,7296]{1,0:T(8,128)S(1)} %fusion.8, bf16[512,128]{0,1:T(8,128)(2,1)S(1)} %get-tuple-element.28, f32[512]{0:T(512)S(1)} %multiply_reduce_fusion, pred[7296]{0:T(1024)(128)(4,1)S(1)} %iota_compare_fusion.3, bf16[7168,128]{1,0:T(8,128)(2,1)} %bitcast.7), kind=kOutput, calls=%fused_computation | convolution fusion | flops 967507968 | bytes 31859840 | tf_op jit(solution)/shard_map/rh,dh->rd/dot_general | solution.py:114
  169.2 5.2 %convolution_reduce-precision_fusion = f32[7168,256]{1,0:T(8,128)S(1)} fusion(bf16[512,7296]{1,0:T(8,128)(2,1)} %all-gather.3.cloned.1.call-done, bf16[512,128]{0,1:T(8,128)(2,1)S(1)} %get-tuple-element.31, bf16[512,128]{0,1:T(8,128)(2,1)S(1)} %get-tuple-element.7), kind=kOutput, calls=%fused_computation.2 | convolution fusion | flops 1881407488 | bytes 14942208 | tf_op jit(solution)/shard_map/rd,rh->dh/dot_general | solution.py:104
  176.0 7.0 %all-to-all-start.7 = ((bf16[16,448,128]{2,1,0:T(8,128)(2,1)}), bf16[16,448,128]{2,1,0:T(8,128)(2,1)S(1)}, u32[]{:S(2)}, u32[]{:S(2)}) async-start(bf16[16,448,128]{2,1,0:T(8,128)(2,1)} %bitcast.66), calls=%async_computation.8 | async-start | bytes 3670016 | tf_op jit(solution)/shard_map/all_to_all | solution.py:141
  183.0 5.3 %convolution_reduce-precision_fusion.2 = f32[7168,256]{1,0:T(8,128)S(1)} fusion(bf16[512,7168]{1,0:T(8,128)(2,1)} %all-gather.5.cloned.1.call-done, bf16[512,128]{0,1:T(8,128)(2,1)S(1)} %get-tuple-element.32, bf16[512,128]{0,1:T(8,128)(2,1)S(1)} %get-tuple-element.25), kind=kOutput, calls=%fused_computation.4 | convolution fusion | flops 1881407488 | bytes 14942208 | tf_op jit(solution)/shard_map/rd,rh->dh/dot_general | solution.py:104
  189.9 22.3 %all-to-all-done.7 = bf16[16,448,128]{2,1,0:T(8,128)(2,1)S(1)} async-done(((bf16[16,448,128]{2,1,0:T(8,128)(2,1)}), bf16[16,448,128]{2,1,0:T(8,128)(2,1)S(1)}, u32[]{:S(2)}, u32[]{:S(2)}) %all-to-all-start.7) | async-done | bytes 1835040 | tf_op jit(solution)/shard_map/all_to_all | solution.py:141
  212.2 4.4 %all-to-all-start.5 = ((bf16[16,448,128]{2,1,0:T(8,128)(2,1)}), bf16[16,448,128]{2,1,0:T(8,128)(2,1)}, u32[]{:S(2)}, u32[]{:S(2)}) async-start(bf16[16,448,128]{2,1,0:T(8,128)(2,1)} %bitcast.64), calls=%async_computation.6 | async-start | bytes 3670016 | tf_op jit(solution)/shard_map/all_to_all | solution.py:136
  216.6 5.4 %convolution_reduce-precision_fusion.1 = f32[7168,256]{1,0:T(8,128)S(1)} fusion(bf16[512,7168]{1,0:T(8,128)(2,1)} %all-gather.5.cloned.1.call-done, bf16[512,128]{0,1:T(8,128)(2,1)S(1)} %get-tuple-element.33, bf16[512,128]{0,1:T(8,128)(2,1)S(1)} %get-tuple-element.27), kind=kOutput, calls=%fused_computation.3 | convolution fusion | flops 1881407488 | bytes 14942208 | tf_op jit(solution)/shard_map/rd,rh->dh/dot_general | solution.py:104
  223.6 20.3 %all-to-all-done.5 = bf16[16,448,128]{2,1,0:T(8,128)(2,1)} async-done(((bf16[16,448,128]{2,1,0:T(8,128)(2,1)}), bf16[16,448,128]{2,1,0:T(8,128)(2,1)}, u32[]{:S(2)}, u32[]{:S(2)}) %all-to-all-start.5) | async-done | bytes 1835040 | tf_op jit(solution)/shard_map/all_to_all | solution.py:136
  243.9 3.7 %all-to-all-start.6 = ((bf16[16,448,128]{2,1,0:T(8,128)(2,1)}), bf16[16,448,128]{2,1,0:T(8,128)(2,1)S(1)}, u32[]{:S(2)}, u32[]{:S(2)}) async-start(bf16[16,448,128]{2,1,0:T(8,128)(2,1)} %bitcast.65), calls=%async_computation.7 | async-start | bytes 3670016 | tf_op jit(solution)/shard_map/all_to_all | solution.py:136
  247.6 5.5 %reduce-scatter.2.cloned.1.call-done = f32[64,7296]{1,0:T(8,128)} async-done(((f32[512,7296]{1,0:T(8,128)}), f32[64,7296]{1,0:T(8,128)}) %reduce-scatter.2.cloned.1.call-update) | async-done | bytes 1867792 | tf_op jit(solution)/shard_map/reduce_scatter | solution.py:120
  253.1 2.9 reshape.146
  255.9 18.5 %all-to-all-done.6 = bf16[16,448,128]{2,1,0:T(8,128)(2,1)S(1)} async-done(((bf16[16,448,128]{2,1,0:T(8,128)(2,1)}), bf16[16,448,128]{2,1,0:T(8,128)(2,1)S(1)}, u32[]{:S(2)}, u32[]{:S(2)}) %all-to-all-start.6) | async-done | bytes 1835040 | tf_op jit(solution)/shard_map/all_to_all | solution.py:136
  275.7 4.0 %all-to-all-start.4 = ((f32[16,4,7296]{2,1,0:T(4,128)}), f32[16,4,7296]{2,1,0:T(4,128)S(1)}, u32[]{:S(2)}, u32[]{:S(2)}) async-start(f32[16,4,7296]{2,1,0:T(4,128)} %reshape.146), calls=%async_computation.5 | async-start | bytes 3735552 | tf_op jit(solution)/shard_map/all_to_all | solution.py:121
  279.6 1.6 slice_bitcast_fusion.1
  284.4 2.3 pad_maximum_fusion.3
  286.8 19.9 %all-to-all-done.4 = f32[16,4,7296]{2,1,0:T(4,128)S(1)} async-done(((f32[16,4,7296]{2,1,0:T(4,128)}), f32[16,4,7296]{2,1,0:T(4,128)S(1)}, u32[]{:S(2)}, u32[]{:S(2)}) %all-to-all-start.4) | async-done | bytes 1867808 | tf_op jit(solution)/shard_map/all_to_all | solution.py:121
  309.5 3.0 fusion
  (61 shorter events, 27.0 us)
Async XLA Ops:
  7.2 116.0 %all-gather.5.cloned.1.call-start = ((), (), s32[]{:S(2)}) async-start(), calls=%async_computation.10 | async-start | bytes 8257536 | tf_op jit(solution)/shard_map/all_gather | solution.py:77
  8.4 6.0 %copy-start.3 = (bf16[256,7168]{1,0:T(8,128)(2,1)S(1)}, bf16[256,7168]{1,0:T(8,128)(2,1)}, u32[]{:S(2)}) copy-start(bf16[256,7168]{1,0:T(8,128)(2,1)} %param.8) | copy-start | bytes 11010052
  53.7 91.0 %all-gather.3.cloned.1.call-start = ((), (), s32[]{:S(2)}) async-start(), calls=%async_computation.9 | async-start | bytes 8404992 | tf_op jit(solution)/shard_map/all_gather | solution.py:78
  57.7 30.3 %all-to-all-start.3 = ((bf16[16,448,128]{2,1,0:T(8,128)(2,1)}), bf16[16,448,128]{2,1,0:T(8,128)(2,1)S(1)}, u32[]{:S(2)}, u32[]{:S(2)}) async-start(bf16[16,448,128]{2,1,0:T(8,128)(2,1)} %bitcast.63), calls=%async_computation.3 | async-start | bytes 3670016 | tf_op jit(solution)/shard_map/all_to_all | solution.py:53
  88.0 30.5 %all-to-all-start.1 = ((bf16[16,448,128]{2,1,0:T(8,128)(2,1)}), bf16[16,448,128]{2,1,0:T(8,128)(2,1)}, u32[]{:S(2)}, u32[]{:S(2)}) async-start(bf16[16,448,128]{2,1,0:T(8,128)(2,1)} %bitcast.62), calls=%async_computation.1 | async-start | bytes 3670016 | tf_op jit(solution)/shard_map/all_to_all | solution.py:55
  118.5 33.3 %all-to-all-start.2 = ((bf16[16,448,128]{2,1,0:T(8,128)(2,1)}), bf16[16,448,128]{2,1,0:T(8,128)(2,1)}, u32[]{:S(2)}, u32[]{:S(2)}) async-start(bf16[16,448,128]{2,1,0:T(8,128)(2,1)} %bitcast.61), calls=%async_computation.2 | async-start | bytes 3670016 | tf_op jit(solution)/shard_map/all_to_all | solution.py:54
  122.9 130.2 %reduce-scatter.2.cloned.1.call-start = ((), (), s32[]{:S(2)}) async-start(), calls=%async_computation.11 | async-start | bytes 16809984 | tf_op jit(solution)/shard_map/reduce_scatter | solution.py:120
  176.0 36.2 %all-to-all-start.7 = ((bf16[16,448,128]{2,1,0:T(8,128)(2,1)}), bf16[16,448,128]{2,1,0:T(8,128)(2,1)S(1)}, u32[]{:S(2)}, u32[]{:S(2)}) async-start(bf16[16,448,128]{2,1,0:T(8,128)(2,1)} %bitcast.66), calls=%async_computation.8 | async-start | bytes 3670016 | tf_op jit(solution)/shard_map/all_to_all | solution.py:141
  212.2 9.8 %copy-start = (bf16[16,448,128]{2,1,0:T(8,128)(2,1)}, bf16[16,448,128]{2,1,0:T(8,128)(2,1)S(1)}, u32[]{:S(2)}) copy-start(bf16[16,448,128]{2,1,0:T(8,128)(2,1)S(1)} %all-to-all-done.7) | copy-start | bytes 5505028
  212.2 31.7 %all-to-all-start.5 = ((bf16[16,448,128]{2,1,0:T(8,128)(2,1)}), bf16[16,448,128]{2,1,0:T(8,128)(2,1)}, u32[]{:S(2)}, u32[]{:S(2)}) async-start(bf16[16,448,128]{2,1,0:T(8,128)(2,1)} %bitcast.64), calls=%async_computation.6 | async-start | bytes 3670016 | tf_op jit(solution)/shard_map/all_to_all | solution.py:136
  243.9 30.5 %all-to-all-start.6 = ((bf16[16,448,128]{2,1,0:T(8,128)(2,1)}), bf16[16,448,128]{2,1,0:T(8,128)(2,1)S(1)}, u32[]{:S(2)}, u32[]{:S(2)}) async-start(bf16[16,448,128]{2,1,0:T(8,128)(2,1)} %bitcast.65), calls=%async_computation.7 | async-start | bytes 3670016 | tf_op jit(solution)/shard_map/all_to_all | solution.py:136
  274.4 1.2 copy-start.1
  275.7 31.0 %all-to-all-start.4 = ((f32[16,4,7296]{2,1,0:T(4,128)}), f32[16,4,7296]{2,1,0:T(4,128)S(1)}, u32[]{:S(2)}, u32[]{:S(2)}) async-start(f32[16,4,7296]{2,1,0:T(4,128)} %reshape.146), calls=%async_computation.5 | async-start | bytes 3735552 | tf_op jit(solution)/shard_map/all_to_all | solution.py:121
  281.2 3.0 copy-start.2
  307.5 1.3 copy-start.4
Sparse Core Ops, SparseCore 0:
  53.8 42.6 all-gather.4
  98.7 45.8 all-gather.2
  169.3 83.7 reduce-scatter.1

commit v10 on v9

--- a/solution.py
+++ b/solution.py
@@ -122,8 +122,9 @@
     back = jnp.sum(back.reshape(round_total, REPS, per_rank, wide), axis=1).reshape(row_slots, wide)
 
     back_tok = back[:, :model_width]
-    back_hi = back_tok.astype(jnp.bfloat16)
-    back_lo = (back_tok - back_hi.astype(jnp.float32)).astype(jnp.bfloat16)
+    back_top = lax.reduce_precision(back_tok, exponent_bits=8, mantissa_bits=7)
+    back_hi = back_top.astype(jnp.bfloat16)
+    back_lo = (back_tok - back_top).astype(jnp.bfloat16)
     grad_tokens = jnp.einsum("qt,qd->td", pick_half, back_hi, preferred_element_type=jnp.float32)
     grad_tokens = grad_tokens + jnp.einsum("qt,qd->td", pick_half, back_lo, preferred_element_type=jnp.float32)
     grad_tokens = grad_tokens.astype(jnp.bfloat16)

time: 320 us -> 320 us (level)
  no operation moved by 1% of the time
where the time goes in v10:
time: 320 us; the launch traced here: 319 us
  waiting for transfers between devices  149 us (47%)
  matrix products  52.8 us (16%)
  blocking collectives  33.8 us (11%)
  starting transfers between devices  32 us (10%)
  other arithmetic  19.1 us (6%)
  local copies, waits for them, and re-layouts  18.5 us (6%)
  between operations  14.1 us (4%)
    all_to_all x2, waiting for transfers between devices, home(): lax.all_to_all(sent, 'dev', 0, 0, tiled=True)  38.8 us
    all_to_all x1, blocking collectives, local(): lax.all_to_all(both.reshape(col_count, per_rank, both_width), 'dev', 0, 0...  33.8 us
    all_to_all x1, waiting for transfers between devices, local(): lax.all_to_all(send_wg, 'dev', 0, 0, tiled=True).reshape(model_width, half)  23.4 us
    all_to_all x1, waiting for transfers between devices, local(): lax.all_to_all(send_wd, 'dev', 0, 0, tiled=True).reshape(model_width, half)  23.1 us
    all_to_all x1, waiting for transfers between devices, local(): lax.all_to_all(grad_down_cols.reshape(col_count, chunk, half), 'dev', 0,...  22.3 us
    all_to_all x1, waiting for transfers between devices, local(): lax.all_to_all(summed.reshape(col_count, per_rank, wide), 'dev', 0, 0, ti...  19.9 us
    dot_general x3, matrix products, slot_pair_sum(): jnp.einsum('rd,rh->dh', rows, by_slot(d), preferred_element_type=jnp.floa...  15.9 us
    all_gather x1, waiting for transfers between devices, local(): dy_ext = lax.all_gather(both[:, model_width:], 'node', axis=0, tiled=True)  15.7 us
  transfers between devices with their start and end apart: 10, of which 8 were waited for; matrix products, arithmetic and copies ran while one was open for 17% of the time, Pallas kernels for 0%

profile of v10, /device:TPU:0, one launch (start us, length us, event | category | flops | bytes accessed | tf_op | source)
XLA Modules:
  0.0 319.0 jit_solution(10747468117801646981)
XLA Ops:
  11.6 2.8 convolution_convert_fusion
  16.0 33.8 %all_to_all.40 = bf16[16,4,14464]{2,1,0:T(4,128)(2,1)} all-to-all(bf16[16,4,14464]{2,1,0:T(4,128)(2,1)S(1)} %bitcast.58), channel_id=1, replica_groups=mesh['node'=8,'dev'=16] {'dev'}, dimensions={0} | all-to-all | bytes 3702784 | tf_op jit(solution)/shard_map/all_to_all | solution.py:75
  49.8 2.8 reshape.139
  57.7 3.7 %all-to-all-start.3 = ((bf16[16,448,128]{2,1,0:T(8,128)(2,1)}), bf16[16,448,128]{2,1,0:T(8,128)(2,1)S(1)}, u32[]{:S(2)}, u32[]{:S(2)}) async-start(bf16[16,448,128]{2,1,0:T(8,128)(2,1)} %bitcast.63), calls=%async_computation.3 | async-start | bytes 3670016 | tf_op jit(solution)/shard_map/all_to_all | solution.py:53
  61.4 1.8 fusion.39
  64.5 23.4 %all-to-all-done.3 = bf16[16,448,128]{2,1,0:T(8,128)(2,1)S(1)} async-done(((bf16[16,448,128]{2,1,0:T(8,128)(2,1)}), bf16[16,448,128]{2,1,0:T(8,128)(2,1)S(1)}, u32[]{:S(2)}, u32[]{:S(2)}) %all-to-all-start.3) | async-done | bytes 1835040 | tf_op jit(solution)/shard_map/all_to_all | solution.py:53
  88.0 4.4 %all-to-all-start.1 = ((bf16[16,448,128]{2,1,0:T(8,128)(2,1)}), bf16[16,448,128]{2,1,0:T(8,128)(2,1)}, u32[]{:S(2)}, u32[]{:S(2)}) async-start(bf16[16,448,128]{2,1,0:T(8,128)(2,1)} %bitcast.62), calls=%async_computation.1 | async-start | bytes 3670016 | tf_op jit(solution)/shard_map/all_to_all | solution.py:55
  92.4 1.6 fusion.40
  95.4 23.1 %all-to-all-done.1 = bf16[16,448,128]{2,1,0:T(8,128)(2,1)} async-done(((bf16[16,448,128]{2,1,0:T(8,128)(2,1)}), bf16[16,448,128]{2,1,0:T(8,128)(2,1)}, u32[]{:S(2)}, u32[]{:S(2)}) %all-to-all-start.1) | async-done | bytes 1835040 | tf_op jit(solution)/shard_map/all_to_all | solution.py:55
  118.5 4.4 %all-to-all-start.2 = ((bf16[16,448,128]{2,1,0:T(8,128)(2,1)}), bf16[16,448,128]{2,1,0:T(8,128)(2,1)}, u32[]{:S(2)}, u32[]{:S(2)}) async-start(bf16[16,448,128]{2,1,0:T(8,128)(2,1)} %bitcast.61), calls=%async_computation.2 | async-start | bytes 3670016 | tf_op jit(solution)/shard_map/all_to_all | solution.py:54
  123.2 5.8 %fusion.42 = f32[512,128]{0,1:T(8,128)S(1)} fusion(bf16[512,7168]{1,0:T(8,128)(2,1)} %all-gather.5.cloned.1.call-done, bf16[7168,128]{1,0:T(8,128)(2,1)S(1)} %bitcast.56), kind=kOutput, calls=%fused_computation.102 | convolution fusion | flops 939524096 | bytes 9437184 | tf_op jit(solution)/shard_map/dot_general | solution.py:82
  129.0 15.7 %all-gather.3.cloned.1.call-done = bf16[512,7296]{1,0:T(8,128)(2,1)} async-done(((bf16[64,7296]{1,0:T(8,128)(2,1)}), bf16[512,7296]{1,0:T(8,128)(2,1)}) %all-gather.3.cloned.1.call-update) | async-done | bytes 7471120 | tf_op jit(solution)/shard_map/all_gather | solution.py:78
  145.7 6.1 %fusion.2 = f32[512,128]{0,1:T(8,128)S(1)} fusion(bf16[7168,128]{1,0:T(8,128)(2,1)} %bitcast.5, bf16[512,7296]{1,0:T(8,128)(2,1)} %all-gather.3.cloned.1.call-done), kind=kOutput, calls=%fused_computation.9 | convolution fusion | flops 939524096 | bytes 9437184 | tf_op jit(solution)/shard_map/dot_general | solution.py:84
  151.8 6.2 %broadcast_select_fusion.1 = (bf16[512,128]{0,1:T(8,128)(2,1)S(1)}, bf16[512,128]{0,1:T(8,128)(2,1)S(1)}, bf16[512,128]{0,1:T(8,128)(2,1)S(1)}, bf16[512,128]{0,...) fusion(pred[512]{0:T(512)(128)(4,1)S(1)} %fusion.30, ...), kind=kOutput, calls=%fused_computation.63 | convolution fusion | flops 940834816 | bytes 10750464 | tf_op jit(solution)/shard_map/dot_general | solution.py:83
  158.1 2.1 fusion.8
  160.3 8.9 %select_add_fusion = f32[512,7296]{1,0:T(8,128)} fusion(f32[512,7296]{1,0:T(8,128)S(1)} %fusion.8, bf16[512,128]{0,1:T(8,128)(2,1)S(1)} %get-tuple-element.28, f32[512]{0:T(512)S(1)} %multiply_reduce_fusion, pred[7296]{0:T(1024)(128)(4,1)S(1)} %iota_compare_fusion.3, bf16[7168,128]{1,0:T(8,128)(2,1)} %bitcast.7), kind=kOutput, calls=%fused_computation | convolution fusion | flops 967507968 | bytes 31859840 | tf_op jit(solution)/shard_map/rh,dh->rd/dot_general | solution.py:114
  169.2 5.2 %convolution_reduce-precision_fusion = f32[7168,256]{1,0:T(8,128)S(1)} fusion(bf16[512,7296]{1,0:T(8,128)(2,1)} %all-gather.3.cloned.1.call-done, bf16[512,128]{0,1:T(8,128)(2,1)S(1)} %get-tuple-element.31, bf16[512,128]{0,1:T(8,128)(2,1)S(1)} %get-tuple-element.7), kind=kOutput, calls=%fused_computation.2 | convolution fusion | flops 1881407488 | bytes 14942208 | tf_op jit(solution)/shard_map/rd,rh->dh/dot_general | solution.py:104
  176.0 7.0 %all-to-all-start.7 = ((bf16[16,448,128]{2,1,0:T(8,128)(2,1)}), bf16[16,448,128]{2,1,0:T(8,128)(2,1)S(1)}, u32[]{:S(2)}, u32[]{:S(2)}) async-start(bf16[16,448,128]{2,1,0:T(8,128)(2,1)} %bitcast.66), calls=%async_computation.8 | async-start | bytes 3670016 | tf_op jit(solution)/shard_map/all_to_all | solution.py:142
  183.0 5.3 %convolution_reduce-precision_fusion.2 = f32[7168,256]{1,0:T(8,128)S(1)} fusion(bf16[512,7168]{1,0:T(8,128)(2,1)} %all-gather.5.cloned.1.call-done, bf16[512,128]{0,1:T(8,128)(2,1)S(1)} %get-tuple-element.32, bf16[512,128]{0,1:T(8,128)(2,1)S(1)} %get-tuple-element.25), kind=kOutput, calls=%fused_computation.4 | convolution fusion | flops 1881407488 | bytes 14942208 | tf_op jit(solution)/shard_map/rd,rh->dh/dot_general | solution.py:104
  189.9 22.3 %all-to-all-done.7 = bf16[16,448,128]{2,1,0:T(8,128)(2,1)S(1)} async-done(((bf16[16,448,128]{2,1,0:T(8,128)(2,1)}), bf16[16,448,128]{2,1,0:T(8,128)(2,1)S(1)}, u32[]{:S(2)}, u32[]{:S(2)}) %all-to-all-start.7) | async-done | bytes 1835040 | tf_op jit(solution)/shard_map/all_to_all | solution.py:142
  212.2 4.4 %all-to-all-start.5 = ((bf16[16,448,128]{2,1,0:T(8,128)(2,1)}), bf16[16,448,128]{2,1,0:T(8,128)(2,1)}, u32[]{:S(2)}, u32[]{:S(2)}) async-start(bf16[16,448,128]{2,1,0:T(8,128)(2,1)} %bitcast.64), calls=%async_computation.6 | async-start | bytes 3670016 | tf_op jit(solution)/shard_map/all_to_all | solution.py:137
  216.6 5.4 %convolution_reduce-precision_fusion.1 = f32[7168,256]{1,0:T(8,128)S(1)} fusion(bf16[512,7168]{1,0:T(8,128)(2,1)} %all-gather.5.cloned.1.call-done, bf16[512,128]{0,1:T(8,128)(2,1)S(1)} %get-tuple-element.33, bf16[512,128]{0,1:T(8,128)(2,1)S(1)} %get-tuple-element.27), kind=kOutput, calls=%fused_computation.3 | convolution fusion | flops 1881407488 | bytes 14942208 | tf_op jit(solution)/shard_map/rd,rh->dh/dot_general | solution.py:104
  223.6 20.3 %all-to-all-done.5 = bf16[16,448,128]{2,1,0:T(8,128)(2,1)} async-done(((bf16[16,448,128]{2,1,0:T(8,128)(2,1)}), bf16[16,448,128]{2,1,0:T(8,128)(2,1)}, u32[]{:S(2)}, u32[]{:S(2)}) %all-to-all-start.5) | async-done | bytes 1835040 | tf_op jit(solution)/shard_map/all_to_all | solution.py:137
  243.9 3.7 %all-to-all-start.6 = ((bf16[16,448,128]{2,1,0:T(8,128)(2,1)}), bf16[16,448,128]{2,1,0:T(8,128)(2,1)S(1)}, u32[]{:S(2)}, u32[]{:S(2)}) async-start(bf16[16,448,128]{2,1,0:T(8,128)(2,1)} %bitcast.65), calls=%async_computation.7 | async-start | bytes 3670016 | tf_op jit(solution)/shard_map/all_to_all | solution.py:137
  247.6 5.5 %reduce-scatter.2.cloned.1.call-done = f32[64,7296]{1,0:T(8,128)} async-done(((f32[512,7296]{1,0:T(8,128)}), f32[64,7296]{1,0:T(8,128)}) %reduce-scatter.2.cloned.1.call-update) | async-done | bytes 1867792 | tf_op jit(solution)/shard_map/reduce_scatter | solution.py:120
  253.1 2.9 reshape.146
  255.9 18.5 %all-to-all-done.6 = bf16[16,448,128]{2,1,0:T(8,128)(2,1)S(1)} async-done(((bf16[16,448,128]{2,1,0:T(8,128)(2,1)}), bf16[16,448,128]{2,1,0:T(8,128)(2,1)S(1)}, u32[]{:S(2)}, u32[]{:S(2)}) %all-to-all-start.6) | async-done | bytes 1835040 | tf_op jit(solution)/shard_map/all_to_all | solution.py:137
  275.7 4.0 %all-to-all-start.4 = ((f32[16,4,7296]{2,1,0:T(4,128)}), f32[16,4,7296]{2,1,0:T(4,128)S(1)}, u32[]{:S(2)}, u32[]{:S(2)}) async-start(f32[16,4,7296]{2,1,0:T(4,128)} %reshape.146), calls=%async_computation.5 | async-start | bytes 3735552 | tf_op jit(solution)/shard_map/all_to_all | solution.py:121
  279.6 1.6 slice_bitcast_fusion.1
  284.4 2.3 pad_maximum_fusion.3
  286.8 19.9 %all-to-all-done.4 = f32[16,4,7296]{2,1,0:T(4,128)S(1)} async-done(((f32[16,4,7296]{2,1,0:T(4,128)}), f32[16,4,7296]{2,1,0:T(4,128)S(1)}, u32[]{:S(2)}, u32[]{:S(2)}) %all-to-all-start.4) | async-done | bytes 1867808 | tf_op jit(solution)/shard_map/all_to_all | solution.py:121
  309.5 3.0 fusion
  (61 shorter events, 27.0 us)
Async XLA Ops:
  7.2 116.0 %all-gather.5.cloned.1.call-start = ((), (), s32[]{:S(2)}) async-start(), calls=%async_computation.10 | async-start | bytes 8257536 | tf_op jit(solution)/shard_map/all_gather | solution.py:77
  8.4 6.0 %copy-start.3 = (bf16[256,7168]{1,0:T(8,128)(2,1)S(1)}, bf16[256,7168]{1,0:T(8,128)(2,1)}, u32[]{:S(2)}) copy-start(bf16[256,7168]{1,0:T(8,128)(2,1)} %param.8) | copy-start | bytes 11010052
  53.7 91.0 %all-gather.3.cloned.1.call-start = ((), (), s32[]{:S(2)}) async-start(), calls=%async_computation.9 | async-start | bytes 8404992 | tf_op jit(solution)/shard_map/all_gather | solution.py:78
  57.7 30.3 %all-to-all-start.3 = ((bf16[16,448,128]{2,1,0:T(8,128)(2,1)}), bf16[16,448,128]{2,1,0:T(8,128)(2,1)S(1)}, u32[]{:S(2)}, u32[]{:S(2)}) async-start(bf16[16,448,128]{2,1,0:T(8,128)(2,1)} %bitcast.63), calls=%async_computation.3 | async-start | bytes 3670016 | tf_op jit(solution)/shard_map/all_to_all | solution.py:53
  88.0 30.5 %all-to-all-start.1 = ((bf16[16,448,128]{2,1,0:T(8,128)(2,1)}), bf16[16,448,128]{2,1,0:T(8,128)(2,1)}, u32[]{:S(2)}, u32[]{:S(2)}) async-start(bf16[16,448,128]{2,1,0:T(8,128)(2,1)} %bitcast.62), calls=%async_computation.1 | async-start | bytes 3670016 | tf_op jit(solution)/shard_map/all_to_all | solution.py:55
  118.5 33.3 %all-to-all-start.2 = ((bf16[16,448,128]{2,1,0:T(8,128)(2,1)}), bf16[16,448,128]{2,1,0:T(8,128)(2,1)}, u32[]{:S(2)}, u32[]{:S(2)}) async-start(bf16[16,448,128]{2,1,0:T(8,128)(2,1)} %bitcast.61), calls=%async_computation.2 | async-start | bytes 3670016 | tf_op jit(solution)/shard_map/all_to_all | solution.py:54
  122.9 130.2 %reduce-scatter.2.cloned.1.call-start = ((), (), s32[]{:S(2)}) async-start(), calls=%async_computation.11 | async-start | bytes 16809984 | tf_op jit(solution)/shard_map/reduce_scatter | solution.py:120
  176.0 36.2 %all-to-all-start.7 = ((bf16[16,448,128]{2,1,0:T(8,128)(2,1)}), bf16[16,448,128]{2,1,0:T(8,128)(2,1)S(1)}, u32[]{:S(2)}, u32[]{:S(2)}) async-start(bf16[16,448,128]{2,1,0:T(8,128)(2,1)} %bitcast.66), calls=%async_computation.8 | async-start | bytes 3670016 | tf_op jit(solution)/shard_map/all_to_all | solution.py:142
  212.2 9.8 %copy-start = (bf16[16,448,128]{2,1,0:T(8,128)(2,1)}, bf16[16,448,128]{2,1,0:T(8,128)(2,1)S(1)}, u32[]{:S(2)}) copy-start(bf16[16,448,128]{2,1,0:T(8,128)(2,1)S(1)} %all-to-all-done.7) | copy-start | bytes 5505028
  212.2 31.7 %all-to-all-start.5 = ((bf16[16,448,128]{2,1,0:T(8,128)(2,1)}), bf16[16,448,128]{2,1,0:T(8,128)(2,1)}, u32[]{:S(2)}, u32[]{:S(2)}) async-start(bf16[16,448,128]{2,1,0:T(8,128)(2,1)} %bitcast.64), calls=%async_computation.6 | async-start | bytes 3670016 | tf_op jit(solution)/shard_map/all_to_all | solution.py:137
  243.9 30.5 %all-to-all-start.6 = ((bf16[16,448,128]{2,1,0:T(8,128)(2,1)}), bf16[16,448,128]{2,1,0:T(8,128)(2,1)S(1)}, u32[]{:S(2)}, u32[]{:S(2)}) async-start(bf16[16,448,128]{2,1,0:T(8,128)(2,1)} %bitcast.65), calls=%async_computation.7 | async-start | bytes 3670016 | tf_op jit(solution)/shard_map/all_to_all | solution.py:137
  274.4 1.2 copy-start.1
  275.7 31.0 %all-to-all-start.4 = ((f32[16,4,7296]{2,1,0:T(4,128)}), f32[16,4,7296]{2,1,0:T(4,128)S(1)}, u32[]{:S(2)}, u32[]{:S(2)}) async-start(f32[16,4,7296]{2,1,0:T(4,128)} %reshape.146), calls=%async_computation.5 | async-start | bytes 3735552 | tf_op jit(solution)/shard_map/all_to_all | solution.py:121
  281.2 3.0 copy-start.2
  307.5 1.3 copy-start.4
Sparse Core Ops, SparseCore 0:
  53.8 42.6 all-gather.4
  98.7 45.8 all-gather.2
  169.3 83.7 reduce-scatter.1
